TPU v7x, 256 devices: a whole 4x4x8 slice. The times are simulated.
256 devices in a mesh: dp: 4 (over x), expert: 64 (over y, z, core).
Axes of the slice: x: 4, y: 4, z: 8, core: 2. Of those that a mesh axis runs over, the one named last changes fastest.
Arguments:
- tokens: bfloat16 [32768, 2048], P(('dp', 'expert')), may hold values from -6 to 6
- expert_ids: int32 [32768, 8], P(('dp', 'expert')), may hold values from 0 to 63, all different within a row; in each aligned block of 128 rows (0 to 127, 128 to 255, ...) at most 24 rows name the same one
- gate_probs: float32 [32768, 8], P(('dp', 'expert')), may hold values from 0.02 to 1
- placement: int32 [64], replicated, may hold values from 0 to 63, each once
- w_gate_up: bfloat16 [64, 2, 768, 2048], P('expert', None, 'dp'), may hold values from -0.125 to 0.125
- w_down: bfloat16 [64, 768, 2048], P('expert', 'dp'), may hold values from -0.21875 to 0.21875
Outputs:
- critic_mix: bfloat16 [32768, 2048], P(('dp', 'expert'))
- placed_gate_up: bfloat16 [64, 2, 768, 2048], P('expert', None, 'dp')
- placed_down: bfloat16 [64, 768, 2048], P('expert', 'dp')
Inputs may be any that keep to these rules, and one draw needn't show every extreme that they name: `expert_ids`: each token names 8 different experts; among the 128 tokens of one device at most 24 name the same expert, and some device reaches 24. `placement`: A permutation of the expert numbers.
All inputs are finite; a program needn't handle non-finite values.
Results may differ from a plain program's by a relative error of at most 0.0058.
Values may be sent and summed in bfloat16 or wider, within the bound.
No kernel may reach another device: no remote copies, remote signals or barrier semaphores. Data moves between devices by JAX's collectives and lax.ppermute only.
A program may use at most 128 MiB of HBM per device.

v0:
```python
import jax
import jax.numpy as jnp
from jax import lax
from jax.sharding import PartitionSpec as P


def per_device(tokens, expert_ids, gate_probs, placement, w_gate_up, w_down):
    tok_dev = tokens.shape[0]
    model_width = tokens.shape[1]
    top_count = expert_ids.shape[1]
    experts = placement.shape[0]
    capacity = min(tok_dev, 3 * tok_dev * top_count // (2 * experts))
    numbers = jnp.arange(experts, dtype=jnp.int32)
    inverse = jnp.sum(
        jnp.where(placement[:, None] == numbers[None, :], numbers[:, None], 0), axis=0
    )
    flat_ids = expert_ids.reshape(-1)
    onehot = (flat_ids[:, None] == numbers[None, :]).astype(jnp.int32)
    before = jnp.cumsum(onehot, axis=0) - onehot
    slot_of = jnp.sum(before * onehot, axis=1)
    down_four = w_down.reshape((1, 1) + w_down.shape[1:])
    pieces = (
        lax.all_to_all(w_gate_up, "expert", split_axis=3, concat_axis=0, tiled=True),
        lax.all_to_all(down_four, "expert", split_axis=3, concat_axis=0, tiled=True),
    )
    reordered = (jnp.take(pieces[0], inverse, axis=0), jnp.take(pieces[1], inverse, axis=0))
    placed = (
        lax.all_to_all(reordered[0], "expert", split_axis=0, concat_axis=3, tiled=True),
        lax.all_to_all(reordered[1], "expert", split_axis=0, concat_axis=3, tiled=True),
    )
    placed_gate_up = placed[0]
    placed_down = placed[1].reshape(w_down.shape)
    gathered = (
        lax.all_gather(placed[0], "dp", axis=2, tiled=True),
        lax.all_gather(placed[1], "dp", axis=2, tiled=True),
    )
    hidden_count = gathered[0].shape[2]
    gate_up_full = gathered[0].reshape(2 * hidden_count, model_width)
    down_full = gathered[1].reshape(hidden_count, model_width)
    flat_index = flat_ids * capacity + slot_of
    spread_rows = jnp.broadcast_to(tokens[:, None, :], (tok_dev, top_count, model_width)).reshape(
        -1, model_width
    )
    buffer = (
        jnp.zeros((experts * capacity, model_width), jnp.bfloat16).at[flat_index].set(spread_rows)
    )
    buffer = buffer.reshape(experts, capacity, model_width)
    received = lax.all_to_all(buffer, "expert", split_axis=0, concat_axis=0, tiled=True)
    row_block = received.reshape(-1, model_width)
    projected = lax.dot_general(
        row_block, gate_up_full, (((1,), (1,)), ((), ())), preferred_element_type=jnp.float32
    )
    gate_part = projected[:, :hidden_count]
    up_part = projected[:, hidden_count:]
    hidden = (jax.nn.silu(gate_part) * up_part).astype(jnp.bfloat16)
    result = jnp.dot(hidden, down_full, preferred_element_type=jnp.float32).astype(jnp.bfloat16)
    result = result.reshape(received.shape)
    returned = lax.all_to_all(result, "expert", split_axis=0, concat_axis=0, tiled=True)
    flat_out = returned.reshape(experts * capacity, model_width)
    picked = flat_out[flat_index].reshape(tok_dev, top_count, model_width)
    gates = gate_probs / jnp.sum(gate_probs, axis=1, keepdims=True)
    mixed_rows = jnp.einsum(
        "tk,tkd->td",
        gates,
        picked,
        preferred_element_type=jnp.float32,
        precision=lax.Precision.HIGHEST,
    )
    return (mixed_rows.astype(jnp.bfloat16), placed_gate_up, placed_down)


def solution(mesh):
    in_specs = (
        P(("dp", "expert"), None),
        P(("dp", "expert"), None),
        P(("dp", "expert"), None),
        P(),
        P("expert", None, "dp", None),
        P("expert", "dp", None),
    )
    out_specs = (P(("dp", "expert"), None), P("expert", None, "dp", None), P("expert", "dp", None))
    return jax.shard_map(
        per_device, mesh=mesh, in_specs=in_specs, out_specs=out_specs, check_vma=False
    )
```

profile of v0, /device:TPU:1, one launch (start us, length us, event | category | flops | bytes accessed | tf_op | source)
XLA Modules:
  0.0 561.2 jit_solution(7574284037175607885)
XLA Ops:
  7.2 0.0 copy-start
  7.2 4.6 copy.75
  11.8 0.5 broadcast.106
  12.3 12.6 %reduce = bf16[2048,192]{1,0:T(8,128)(2,1)} reduce(bf16[2048,1,1,192]{3,2,1,0:T(2,128)(2,1)S(1)} %bitcast.83, bf16[]{:T(256)} %broadcast.106), dimensions={1,2}, to_apply=%bitcast.70.reduce_sub_computation | reduce | bytes 1572866
  24.9 3.7 reshape.162
  28.6 13.2 %all-to-all-start.3 = ((bf16[64,2,3072]{2,1,0:T(2,128)(2,1)}), bf16[64,2,3072]{2,1,0:T(2,128)(2,1)S(1)}, u32[]{:S(2)}, u32[]{:S(2)}) async-start(bf16[64,2,3072]{2,1,0:T(2,128)(2,1)} %reshape.162), calls=%async_computation.3 | async-start | bytes 1572864 | tf_op jit(solution)/shard_map/all_to_all | solution.py:24
  41.7 0.0 copy-done.3
  41.7 0.0 copy-start.6
  41.8 3.8 copy.69
  45.5 19.2 %all-to-all-done.3 = bf16[64,2,3072]{2,1,0:T(2,128)(2,1)S(1)} async-done(((bf16[64,2,3072]{2,1,0:T(2,128)(2,1)}), bf16[64,2,3072]{2,1,0:T(2,128)(2,1)S(1)}, u32[]{:S(2)}, u32[]{:S(2)}) %all-to-all-start.3) | async-done | bytes 786464 | tf_op jit(solution)/shard_map/all_to_all | solution.py:24
  64.7 6.4 %all-to-all-start.1 = ((bf16[1,2,192,2048]{2,1,0,3:T(2,128)(2,1)}), bf16[1,2,192,2048]{2,1,0,3:T(2,128)(2,1)}, u32[]{:S(2)}, u32[]{:S(2)}) async-start(bf16[1,2,192,2048]{2,1,0,3:T(2,128)(2,1)} %copy.69), calls=%async_computation.1 | async-start | bytes 4194304 | tf_op jit(solution)/shard_map/all_to_all | solution.py:23
  71.1 0.0 copy-done.6
  71.1 0.1 select_reduce_fusion
  71.2 3.7 reshape.163
  75.0 1.8 copy.84
  76.7 0.6 gather_fusion.1
  77.4 1.1 fusion.10
  78.5 43.8 %all-to-all-done.1 = bf16[1,2,192,2048]{2,1,0,3:T(2,128)(2,1)} async-done(((bf16[1,2,192,2048]{2,1,0,3:T(2,128)(2,1)}), bf16[1,2,192,2048]{2,1,0,3:T(2,128)(2,1)}, u32[]{:S(2)}, u32[]{:S(2)}) %all-to-all-start.1) | async-done | bytes 1572896 | tf_op jit(solution)/shard_map/all_to_all | solution.py:23
  122.3 6.0 %all-to-all-start.4 = ((bf16[64,1,192,32]{2,3,1,0:T(8,128)(2,1)}), bf16[64,1,192,32]{2,3,1,0:T(8,128)(2,1)}, u32[]{:S(2)}, u32[]{:S(2)}) async-start(bf16[64,1,192,32]{2,3,1,0:T(8,128)(2,1)} %fusion.10), calls=%async_computation.4 | async-start | bytes 2097152 | tf_op jit(solution)/shard_map/all_to_all | solution.py:29
  128.3 3.4 copy.89
  131.7 2.3 gather_fusion
  133.9 0.0 copy-start.4
  133.9 1.6 broadcast_select_fusion
  135.6 21.2 %all-to-all-done.4 = bf16[64,1,192,32]{2,3,1,0:T(8,128)(2,1)} async-done(((bf16[64,1,192,32]{2,3,1,0:T(8,128)(2,1)}), bf16[64,1,192,32]{2,3,1,0:T(8,128)(2,1)}, u32[]{:S(2)}, u32[]{:S(2)}) %all-to-all-start.4) | async-done | bytes 786464 | tf_op jit(solution)/shard_map/all_to_all | solution.py:29
  156.8 6.2 %all-to-all-start.2 = ((bf16[64,2,192,32]{2,3,1,0:T(8,128)(2,1)}), bf16[64,2,192,32]{2,3,1,0:T(8,128)(2,1)S(1)}, u32[]{:S(2)}, u32[]{:S(2)}) async-start(bf16[64,2,192,32]{2,3,1,0:T(8,128)(2,1)} %broadcast_select_fusion), calls=%async_computation.2 | async-start | bytes 4194304 | tf_op jit(solution)/shard_map/all_to_all | solution.py:28
  163.0 0.0 copy-done.4
  163.0 0.1 copy.65
  163.1 0.1 eq.42
  163.2 0.1 eq.38
  163.3 18.0 %reduce-window.6 = s32[64,8,128]{2,1,0:T(8,128)S(1)} reduce-window(s32[64,8,128]{2,1,0:T(8,128)S(1)} %fusion.14, s32[]{:T(128)} %constant.32.clone.1), window={size=1x1x128 pad=0_0x0_0x127_0}, to_apply=%region_1.2 | reduce-window | flops 8323072 | bytes 524292 | tf_op jit(solution)/shard_map/reduce-window
  181.3 0.1 slice.22
  181.4 0.1 copy.67
  181.6 0.1 copy.68
  181.7 0.1 copy.64
  181.8 0.1 mul.28
  181.9 0.1 broadcast_add_fusion
  182.1 0.1 fusion.13
  182.2 0.0 copy-done
  182.2 10.2 %scatter_custom_fusion = bf16[1536,2048]{1,0:T(8,128)(2,1)} fusion(s32[1024]{0:T(1024)S(1)} %bitcast.92, bf16[]{:T(256)} %constant.24.clone.1, bf16[128,2048]{1,0:T(8,128)(2,1)S(1)} %copy-done), kind=kCustom, calls=%fused_computation.9 | custom fusion | bytes 6815746 | tf_op jit(solution)/shard_map/scatter | solution.py:45
  192.4 21.8 %all-to-all-done.2 = bf16[64,2,192,32]{2,3,1,0:T(8,128)(2,1)S(1)} async-done(((bf16[64,2,192,32]{2,3,1,0:T(8,128)(2,1)}), bf16[64,2,192,32]{2,3,1,0:T(8,128)(2,1)S(1)}, u32[]{:S(2)}, u32[]{:S(2)}) %all-to-all-start.2) | async-done | bytes 1572896 | tf_op jit(solution)/shard_map/all_to_all | solution.py:28
  214.2 6.0 %all-to-all-start = ((bf16[64,24,2048]{2,1,0:T(8,128)(2,1)}), bf16[64,24,2048]{2,1,0:T(8,128)(2,1)}, u32[]{:S(2)}, u32[]{:S(2)}) async-start(bf16[64,24,2048]{2,1,0:T(8,128)(2,1)} %bitcast.78), calls=%async_computation | async-start | bytes 12582912 | tf_op jit(solution)/shard_map/all_to_all | solution.py:48
  220.2 0.0 all-gather.3.cloned.1.call-start
  220.2 0.0 copy-done.2
  220.3 1.8 copy.72
  222.1 3.3 copy.73
  225.4 0.0 all-gather.3.cloned.1.call-update
  225.4 0.3 all-gather.5.cloned.1.call-start
  225.7 2.2 copy.77
  227.9 0.0 all-gather.5.cloned.1.call-update
  227.9 66.8 %all-gather.3.cloned.1.call-done = bf16[1,2,768,2048]{3,1,0,2:T(2,128)(2,1)} async-done(((bf16[1,2,192,2048]{3,1,0,2:T(2,128)(2,1)}), bf16[1,2,768,2048]{3,1,0,2:T(2,128)(2,1)}) %all-gather.3.cloned.1.call-update) | async-done | bytes 6291472 | tf_op jit(solution)/shard_map/all_gather | solution.py:34
  294.7 8.3 %copy.74 = bf16[1,2,768,2048]{3,2,1,0:T(8,128)(2,1)} copy(bf16[1,2,768,2048]{3,1,0,2:T(2,128)(2,1)} %all-gather.3.cloned.1.call-done) | data formatting | bytes 12582912 | tf_op jit(solution)/shard_map/all_gather | solution.py:34
  303.0 58.0 %all-to-all-done = bf16[64,24,2048]{2,1,0:T(8,128)(2,1)} async-done(((bf16[64,24,2048]{2,1,0:T(8,128)(2,1)}), bf16[64,24,2048]{2,1,0:T(8,128)(2,1)}, u32[]{:S(2)}, u32[]{:S(2)}) %all-to-all-start) | async-done | bytes 6291488 | tf_op jit(solution)/shard_map/all_to_all | solution.py:48
  361.0 15.7 %fusion.17 = f32[1536,1536]{1,0:T(8,128)} fusion(bf16[1536,2048]{1,0:T(8,128)(2,1)} %bitcast.7, bf16[1536,2048]{1,0:T(8,128)(2,1)} %bitcast.86), kind=kOutput, calls=%fused_computation.40 | convolution fusion | flops 9663676416 | bytes 22020096 | tf_op jit(solution)/shard_map/dot_general | solution.py:50
  376.8 11.4 %convolution_convert_fusion = bf16[1536,2048]{1,0:T(8,128)(2,1)} fusion(bf16[1,1,768,2048]{3,2,1,0:T(8,128)(2,1)} %all-gather.5.cloned.1.call-done, f32[1536,1536]{1,0:T(8,128)} %fusion.17), kind=kOutput, calls=%fused_computation.4 | convolution fusion | flops 4842061824 | bytes 18874368 | tf_op jit(solution)/shard_map/dot_general | solution.py:56
  388.1 6.1 %all-to-all-start.5 = ((bf16[64,24,2048]{2,1,0:T(8,128)(2,1)}), bf16[64,24,2048]{2,1,0:T(8,128)(2,1)}, u32[]{:S(2)}, u32[]{:S(2)}) async-start(bf16[64,24,2048]{2,1,0:T(8,128)(2,1)} %bitcast.85), calls=%async_computation.5 | async-start | bytes 12582912 | tf_op jit(solution)/shard_map/all_to_all | solution.py:58
  394.2 0.0 copy-done.5
  394.3 0.1 copy.80
  394.4 2.2 copy.79
  396.6 2.2 copy.78
  398.8 136.3 %all-to-all-done.5 = bf16[64,24,2048]{2,1,0:T(8,128)(2,1)} async-done(((bf16[64,24,2048]{2,1,0:T(8,128)(2,1)}), bf16[64,24,2048]{2,1,0:T(8,128)(2,1)}, u32[]{:S(2)}, u32[]{:S(2)}) %all-to-all-start.5) | async-done | bytes 6291488 | tf_op jit(solution)/shard_map/all_to_all | solution.py:58
  535.1 12.4 %gather_fusion.2 = bf16[1024,2048]{1,0:T(8,128)(2,1)} fusion(bf16[1536,2048]{1,0:T(8,128)(2,1)} %bitcast.27, s32[1024]{0:T(1024)S(1)} %broadcast_clamp_fusion), kind=kCustom, calls=%fused_computation.2 | custom fusion | bytes 8392704 | tf_op jit(solution)/shard_map/gather | solution.py:60
  547.5 5.7 %fusion.1 = bf16[128,1,2048]{2,1,0:T(2,128)(2,1)S(1)} fusion(f32[128,8,1]{1,2,0:T(1,128)S(1)} %copy.80, bf16[1024,2048]{1,0:T(8,128)(2,1)} %gather_fusion.2), kind=kOutput, calls=%fused_computation.7 | convolution fusion | flops 25165824 | bytes 4722688 | tf_op jit(solution)/shard_map/tk,tkd->td/dot_general | solution.py:62
  553.3 1.1 copy.90
  554.3 0.0 copy-done.1
  (16 shorter events, 0.1 us)
Async XLA Ops:
  7.2 175.0 %copy-start = (bf16[128,2048]{1,0:T(8,128)(2,1)S(1)}, bf16[128,2048]{1,0:T(8,128)(2,1)}, u32[]{:S(2)}) copy-start(bf16[128,2048]{1,0:T(8,128)(2,1)} %param.6) | copy-start | bytes 1572868
  24.9 16.8 %copy-start.3 = (bf16[1,2,192,2048]{3,2,1,0:T(8,128)(2,1)S(1)}, bf16[1,2,192,2048]{3,2,1,0:T(8,128)(2,1)}, u32[]{:S(2)}) copy-start(bf16[1,2,192,2048]{3,2,1,0:T(8,128)(2,1)} %param.10) | copy-start | bytes 4718596
  28.6 36.1 %all-to-all-start.3 = ((bf16[64,2,3072]{2,1,0:T(2,128)(2,1)}), bf16[64,2,3072]{2,1,0:T(2,128)(2,1)S(1)}, u32[]{:S(2)}, u32[]{:S(2)}) async-start(bf16[64,2,3072]{2,1,0:T(2,128)(2,1)} %reshape.162), calls=%async_computation.3 | async-start | bytes 1572864 | tf_op jit(solution)/shard_map/all_to_all | solution.py:24
  41.7 29.4 %copy-start.6 = (s32[64]{0:T(128)S(1)}, s32[64]{0:T(128)}, u32[]{:S(2)}) copy-start(s32[64]{0:T(128)} %param.9) | copy-start | bytes 772
  64.7 57.6 %all-to-all-start.1 = ((bf16[1,2,192,2048]{2,1,0,3:T(2,128)(2,1)}), bf16[1,2,192,2048]{2,1,0,3:T(2,128)(2,1)}, u32[]{:S(2)}, u32[]{:S(2)}) async-start(bf16[1,2,192,2048]{2,1,0,3:T(2,128)(2,1)} %copy.69), calls=%async_computation.1 | async-start | bytes 4194304 | tf_op jit(solution)/shard_map/all_to_all | solution.py:23
  122.3 34.5 %all-to-all-start.4 = ((bf16[64,1,192,32]{2,3,1,0:T(8,128)(2,1)}), bf16[64,1,192,32]{2,3,1,0:T(8,128)(2,1)}, u32[]{:S(2)}, u32[]{:S(2)}) async-start(bf16[64,1,192,32]{2,3,1,0:T(8,128)(2,1)} %fusion.10), calls=%async_computation.4 | async-start | bytes 2097152 | tf_op jit(solution)/shard_map/all_to_all | solution.py:29
  133.9 29.0 %copy-start.4 = (s32[128,8]{0,1:T(8,128)S(1)}, s32[128,8]{0,1:T(8,128)}, u32[]{:S(2)}) copy-start(s32[128,8]{0,1:T(8,128)} %param.7) | copy-start | bytes 12292
  156.8 57.4 %all-to-all-start.2 = ((bf16[64,2,192,32]{2,3,1,0:T(8,128)(2,1)}), bf16[64,2,192,32]{2,3,1,0:T(8,128)(2,1)S(1)}, u32[]{:S(2)}, u32[]{:S(2)}) async-start(bf16[64,2,192,32]{2,3,1,0:T(8,128)(2,1)} %broadcast_select_fusion), calls=%async_computation.2 | async-start | bytes 4194304 | tf_op jit(solution)/shard_map/all_to_all | solution.py:28
  214.2 6.0 %copy-start.2 = (bf16[64,2,192,32]{2,3,1,0:T(8,128)(2,1)}, bf16[64,2,192,32]{2,3,1,0:T(8,128)(2,1)S(1)}, u32[]{:S(2)}) copy-start(bf16[64,2,192,32]{2,3,1,0:T(8,128)(2,1)S(1)} %all-to-all-done.2) | copy-start | bytes 4718596
  214.2 146.8 %all-to-all-start = ((bf16[64,24,2048]{2,1,0:T(8,128)(2,1)}), bf16[64,24,2048]{2,1,0:T(8,128)(2,1)}, u32[]{:S(2)}, u32[]{:S(2)}) async-start(bf16[64,24,2048]{2,1,0:T(8,128)(2,1)} %bitcast.78), calls=%async_computation | async-start | bytes 12582912 | tf_op jit(solution)/shard_map/all_to_all | solution.py:48
  220.2 74.5 %all-gather.3.cloned.1.call-start = ((), (), s32[]{:S(2)}) async-start(), calls=%async_computation.6 | async-start | bytes 7864320 | tf_op jit(solution)/shard_map/all_gather | solution.py:34
  225.4 151.3 %all-gather.5.cloned.1.call-start = ((), (), s32[]{:S(2)}) async-start(), calls=%async_computation.7 | async-start | bytes 3932160 | tf_op jit(solution)/shard_map/all_gather | solution.py:35
  388.1 6.1 %copy-start.5 = (f32[128,8]{0,1:T(8,128)S(1)}, f32[128,8]{0,1:T(8,128)}, u32[]{:S(2)}) copy-start(f32[128,8]{0,1:T(8,128)} %param.8) | copy-start | bytes 12292
  388.1 146.9 %all-to-all-start.5 = ((bf16[64,24,2048]{2,1,0:T(8,128)(2,1)}), bf16[64,24,2048]{2,1,0:T(8,128)(2,1)}, u32[]{:S(2)}, u32[]{:S(2)}) async-start(bf16[64,24,2048]{2,1,0:T(8,128)(2,1)} %bitcast.85), calls=%async_computation.5 | async-start | bytes 12582912 | tf_op jit(solution)/shard_map/all_to_all | solution.py:58
  535.1 19.3 %copy-start.1 = (bf16[128,2048]{1,0:T(8,128)(2,1)S(1)}, bf16[128,2048]{1,0:T(8,128)(2,1)}, u32[]{:S(2)}) copy-start(bf16[128,2048]{1,0:T(8,128)(2,1)} %param.6) | copy-start | bytes 1572868
Sparse Core Ops, SparseCore 0:
  225.5 69.1 all-gather.2
  297.1 42.7 all-gather.4
where the time goes:
time: 562 us; the launch traced here: 561 us
  waiting for transfers between devices  367 us (65%)
  local copies, waits for them, and re-layouts  69.1 us (12%)
  starting transfers between devices  44.1 us (8%)
  other arithmetic  33.8 us (6%)
  matrix products  32.8 us (6%)
  between operations  14.3 us (3%)
    all_to_all x1, waiting for transfers between devices, per_device(): lax.all_to_all(result, 'expert', split_axis=0, concat_axis=0, tiled=True)  136 us
    all_gather x1, waiting for transfers between devices, per_device(): lax.all_gather(placed[0], 'dp', axis=2, tiled=True)  66.8 us
    all_to_all x1, waiting for transfers between devices, per_device(): lax.all_to_all(buffer, 'expert', split_axis=0, concat_axis=0, tiled=True)  58 us
    all_to_all x1, waiting for transfers between devices, per_device(): lax.all_to_all(w_gate_up, 'expert', split_axis=3, concat_axis=0, tiled=True)  43.8 us
    all_to_all x1, waiting for transfers between devices, per_device(): lax.all_to_all(reordered[0], 'expert', split_axis=0, concat_axis=3, tiled...  21.8 us
    all_to_all x1, waiting for transfers between devices, per_device(): lax.all_to_all(reordered[1], 'expert', split_axis=0, concat_axis=3, tiled...  21.2 us
    all_to_all x1, waiting for transfers between devices, per_device(): lax.all_to_all(down_four, 'expert', split_axis=3, concat_axis=0, tiled=True)  19.2 us
    another operation x3, other arithmetic  18.2 us
  transfers between devices with their start and end apart: 8, of which 7 were waited for; matrix products, arithmetic and copies ran while one was open for 15% of the time, Pallas kernels for 0%

commit v1 on v0

--- a/solution.py
+++ b/solution.py
@@ -14,7 +14,7 @@
     inverse = jnp.sum(
         jnp.where(placement[:, None] == numbers[None, :], numbers[:, None], 0), axis=0
     )
-    flat_ids = expert_ids.reshape(-1)
+    flat_ids = jnp.take(inverse, expert_ids.reshape(-1), axis=0)
     onehot = (flat_ids[:, None] == numbers[None, :]).astype(jnp.int32)
     before = jnp.cumsum(onehot, axis=0) - onehot
     slot_of = jnp.sum(before * onehot, axis=1)
@@ -31,8 +31,8 @@
     placed_gate_up = placed[0]
     placed_down = placed[1].reshape(w_down.shape)
     gathered = (
-        lax.all_gather(placed[0], "dp", axis=2, tiled=True),
-        lax.all_gather(placed[1], "dp", axis=2, tiled=True),
+        lax.all_gather(w_gate_up, "dp", axis=2, tiled=True),
+        lax.all_gather(w_down, "dp", axis=1, tiled=True),
     )
     hidden_count = gathered[0].shape[2]
     gate_up_full = gathered[0].reshape(2 * hidden_count, model_width)

time: 562 us -> 580 us (1.032)
  other arithmetic: 33.8 us -> 74.7 us
  waiting for transfers between devices: 367 us -> 349 us
  local copies, waits for them, and re-layouts: 69.1 us -> 60.5 us
    all_to_all x1, waiting for transfers between devices: 58 us -> 132 us  [per_device(): lax.all_to_all(buffer, 'expert', split_axis=0, concat_axis=0, tiled=True)]
    all_gather x2, waiting for transfers between devices: 66.8 us -> 0.02 us  [the longest x1 0.02 us: per_device(): lax.all_gather(w_gate_up, 'dp', axis=2, tiled=True)]
    select_n x0 -> x2, other arithmetic: none -> 35.6 us  [per_device(): flat_ids = jnp.take(inverse, expert_ids.reshape(-1), axis=0)]
    all_to_all x1, waiting for transfers between devices: 21.2 us -> 0.01 us  [per_device(): lax.all_to_all(reordered[1], 'expert', split_axis=0, concat_axis=3, tiled...]
    all_gather x1 -> x0, local copies, waits for them, and re-layouts: 8.29 us -> none  [per_device(): lax.all_gather(placed[0], 'dp', axis=2, tiled=True)]
    all_to_all x1, waiting for transfers between devices: 43.8 us -> 37.6 us  [per_device(): lax.all_to_all(w_gate_up, 'expert', split_axis=3, concat_axis=0, tiled=True)]
    unnamed x22 -> x24, local copies, waits for them, and re-layouts: 18 us -> 20.4 us
  transfers between devices with their start and end apart: 8 -> 8, of which waited for: 7 -> 5; matrix products, arithmetic and copies ran while one was open for 15% -> 22% of each run, Pallas kernels for 0% -> 0%
where the time goes in v1:
time: 580 us; the launch traced here: 579 us
  waiting for transfers between devices  349 us (60%)
  other arithmetic  74.7 us (13%)
  local copies, waits for them, and re-layouts  60.5 us (10%)
  starting transfers between devices  47.7 us (8%)
  matrix products  32.8 us (6%)
  between operations  14.3 us (2%)
    all_to_all x1, waiting for transfers between devices, per_device(): lax.all_to_all(result, 'expert', split_axis=0, concat_axis=0, tiled=True)  134 us
    all_to_all x1, waiting for transfers between devices, per_device(): lax.all_to_all(buffer, 'expert', split_axis=0, concat_axis=0, tiled=True)  132 us
    all_to_all x1, waiting for transfers between devices, per_device(): lax.all_to_all(w_gate_up, 'expert', split_axis=3, concat_axis=0, tiled=True)  37.6 us
    select_n x2, other arithmetic, per_device(): flat_ids = jnp.take(inverse, expert_ids.reshape(-1), axis=0)  35.6 us
    all_to_all x1, waiting for transfers between devices, per_device(): lax.all_to_all(reordered[0], 'expert', split_axis=0, concat_axis=3, tiled...  24.1 us
    unnamed x24, local copies, waits for them, and re-layouts  20.4 us
    all_to_all x1, waiting for transfers between devices, per_device(): lax.all_to_all(down_four, 'expert', split_axis=3, concat_axis=0, tiled=True)  19.1 us
    another operation x3, other arithmetic  18.2 us
  transfers between devices with their start and end apart: 8, of which 5 were waited for; matrix products, arithmetic and copies ran while one was open for 22% of the time, Pallas kernels for 0%

profile of v1, /device:TPU:1, one launch (start us, length us, event | category | flops | bytes accessed | tf_op | source)
XLA Modules:
  0.0 578.7 jit_solution(4741536056463283527)
XLA Ops:
  7.2 0.0 copy-start
  7.2 4.6 copy.55
  11.8 0.5 broadcast.687
  12.3 12.6 %reduce.114 = bf16[2048,192]{1,0:T(8,128)(2,1)} reduce(bf16[2048,1,1,192]{3,2,1,0:T(2,128)(2,1)S(1)} %bitcast.148, bf16[]{:T(256)} %broadcast.687), dimensions={1,2}, to_apply=%bitcast.136.reduce_sub_computation | reduce | bytes 1572866
  24.9 3.7 reshape.503
  28.6 13.2 %all-to-all-start.4 = ((bf16[64,2,3072]{2,1,0:T(2,128)(2,1)}), bf16[64,2,3072]{2,1,0:T(2,128)(2,1)S(1)}, u32[]{:S(2)}, u32[]{:S(2)}) async-start(bf16[64,2,3072]{2,1,0:T(2,128)(2,1)} %reshape.503), calls=%async_computation.4 | async-start | bytes 1572864 | tf_op jit(solution)/shard_map/all_to_all | solution.py:24
  41.7 0.0 copy-done.3
  41.7 0.0 copy-start.6
  41.8 0.0 copy-start.7
  41.8 3.8 copy.51
  45.6 19.1 %all-to-all-done.4 = bf16[64,2,3072]{2,1,0:T(2,128)(2,1)S(1)} async-done(((bf16[64,2,3072]{2,1,0:T(2,128)(2,1)}), bf16[64,2,3072]{2,1,0:T(2,128)(2,1)S(1)}, u32[]{:S(2)}, u32[]{:S(2)}) %all-to-all-start.4) | async-done | bytes 786464 | tf_op jit(solution)/shard_map/all_to_all | solution.py:24
  64.7 6.4 %all-to-all-start.2 = ((bf16[1,2,192,2048]{2,1,0,3:T(2,128)(2,1)}), bf16[1,2,192,2048]{2,1,0,3:T(2,128)(2,1)}, u32[]{:S(2)}, u32[]{:S(2)}) async-start(bf16[1,2,192,2048]{2,1,0,3:T(2,128)(2,1)} %copy.51), calls=%async_computation.2 | async-start | bytes 4194304 | tf_op jit(solution)/shard_map/all_to_all | solution.py:23
  71.1 0.1 copy.46
  71.2 0.1 reshape.181
  71.3 0.0 copy-done.7
  71.3 0.1 select_reduce_fusion
  71.4 0.7 fusion.20
  72.1 0.7 fusion.19
  72.8 4.5 compare_select_fusion.2
  77.4 3.8 reshape.504
  81.2 1.8 copy.63
  82.9 0.6 gather_fusion.2
  83.6 1.1 fusion.10
  84.7 37.6 %all-to-all-done.2 = bf16[1,2,192,2048]{2,1,0,3:T(2,128)(2,1)} async-done(((bf16[1,2,192,2048]{2,1,0,3:T(2,128)(2,1)}), bf16[1,2,192,2048]{2,1,0,3:T(2,128)(2,1)}, u32[]{:S(2)}, u32[]{:S(2)}) %all-to-all-start.2) | async-done | bytes 1572896 | tf_op jit(solution)/shard_map/all_to_all | solution.py:23
  122.3 5.8 %all-to-all-start.5 = ((bf16[64,1,192,32]{2,3,1,0:T(8,128)(2,1)}), bf16[64,1,192,32]{2,3,1,0:T(8,128)(2,1)S(1)}, u32[]{:S(2)}, u32[]{:S(2)}) async-start(bf16[64,1,192,32]{2,3,1,0:T(8,128)(2,1)} %fusion.10), calls=%async_computation.5 | async-start | bytes 2097152 | tf_op jit(solution)/shard_map/all_to_all | solution.py:29
  128.1 0.7 fusion.17
  128.8 0.1 reshape.182
  128.9 0.1 reshape.183
  129.0 0.7 fusion.18
  129.8 0.7 compare_reduce_fusion.56
  130.5 35.6 %and_select_fusion.1 = (s32[1024]{0:T(1024)S(1)}, s32[1024]{0:T(1024)S(1)}) fusion(s32[1024]{0:T(1024)S(1)} %reshape.182, pred[1024]{0:T(1024)(128)(4,1)S(1)} %get-tuple-element.70, pred[1024]{0:T(1024)(128)(4,1)S(1)} %get-tuple-element.69, pred[1024]{0:T(1024)(128)(4,1)S(1)} %get-tuple-element.71, pred[1024]{0:T(1024)(128)(4,1)S(1)} %get-tuple-element.68, ...), kind=kLoop, calls=%fused_computation.102 | loop fusion | flops 65536 | bytes 74980 | tf_op jit(solution)/shard_map/jit(_take)/select_n | solution.py:17
  166.2 18.0 %reduce-window.6 = s32[64,8,128]{2,1,0:T(8,128)S(1)} reduce-window(s32[64,8,128]{2,1,0:T(8,128)S(1)} %fusion.14, s32[]{:T(128)} %constant.37.clone.1), window={size=1x1x128 pad=0_0x0_0x127_0}, to_apply=%region_2.3 | reduce-window | flops 8323072 | bytes 524292 | tf_op jit(solution)/shard_map/reduce-window
  184.2 0.1 slice.87
  184.3 0.1 copy.49
  184.5 0.1 copy.50
  184.6 0.1 broadcast_add_fusion
  184.7 0.1 fusion.13
  184.8 10.2 %scatter_custom_fusion = bf16[1536,2048]{1,0:T(8,128)(2,1)} fusion(s32[1024]{0:T(1024)S(1)} %bitcast.159, bf16[]{:T(256)} %constant.36.clone.1, bf16[128,2048]{1,0:T(8,128)(2,1)S(1)} %copy-done), kind=kCustom, calls=%fused_computation.9 | custom fusion | bytes 6815746 | tf_op jit(solution)/shard_map/scatter | solution.py:45
  195.0 0.0 all-to-all-done.5
  195.0 1.0 copy-done.4
  196.0 10.5 %all-to-all-start = ((bf16[64,24,2048]{2,1,0:T(8,128)(2,1)}), bf16[64,24,2048]{2,1,0:T(8,128)(2,1)}, u32[]{:S(2)}, u32[]{:S(2)}) async-start(bf16[64,24,2048]{2,1,0:T(8,128)(2,1)} %bitcast.144), calls=%async_computation | async-start | bytes 12582912 | tf_op jit(solution)/shard_map/all_to_all | solution.py:48
  206.5 0.0 all-gather.3.cloned.1.call-start
  206.6 0.7 all-gather.3.cloned.1.call-update
  207.2 0.0 all-gather.5.cloned.1.call-start
  207.3 0.7 all-gather.5.cloned.1.call-update
  208.0 3.5 copy.68
  211.5 2.3 gather_fusion.1
  213.7 1.6 broadcast_select_fusion
  215.4 132.0 %all-to-all-done = bf16[64,24,2048]{2,1,0:T(8,128)(2,1)} async-done(((bf16[64,24,2048]{2,1,0:T(8,128)(2,1)}), bf16[64,24,2048]{2,1,0:T(8,128)(2,1)}, u32[]{:S(2)}, u32[]{:S(2)}) %all-to-all-start) | async-done | bytes 6291488 | tf_op jit(solution)/shard_map/all_to_all | solution.py:48
  347.4 5.8 %all-to-all-start.3 = ((bf16[64,2,192,32]{2,3,1,0:T(8,128)(2,1)}), bf16[64,2,192,32]{2,3,1,0:T(8,128)(2,1)S(1)}, u32[]{:S(2)}, u32[]{:S(2)}) async-start(bf16[64,2,192,32]{2,3,1,0:T(8,128)(2,1)} %broadcast_select_fusion), calls=%async_computation.3 | async-start | bytes 4194304 | tf_op jit(solution)/shard_map/all_to_all | solution.py:28
  353.2 0.0 all-gather.3.cloned.1.call-done
  353.2 15.7 %fusion.21 = f32[1536,1536]{1,0:T(8,128)} fusion(bf16[1536,2048]{1,0:T(8,128)(2,1)} %bitcast.74, bf16[1536,2048]{1,0:T(8,128)(2,1)} %bitcast.161), kind=kOutput, calls=%fused_computation.113 | convolution fusion | flops 9663676416 | bytes 22020096 | tf_op jit(solution)/shard_map/dot_general | solution.py:50
  368.9 11.4 %convolution_convert_fusion = bf16[1536,2048]{1,0:T(8,128)(2,1)} fusion(bf16[1,768,2048]{2,1,0:T(8,128)(2,1)} %all-gather.5.cloned.1.call-done, f32[1536,1536]{1,0:T(8,128)} %fusion.21), kind=kOutput, calls=%fused_computation.4 | convolution fusion | flops 4842061824 | bytes 18874368 | tf_op jit(solution)/shard_map/dot_general | solution.py:56
  380.3 24.1 %all-to-all-done.3 = bf16[64,2,192,32]{2,3,1,0:T(8,128)(2,1)S(1)} async-done(((bf16[64,2,192,32]{2,3,1,0:T(8,128)(2,1)}), bf16[64,2,192,32]{2,3,1,0:T(8,128)(2,1)S(1)}, u32[]{:S(2)}, u32[]{:S(2)}) %all-to-all-start.3) | async-done | bytes 1572896 | tf_op jit(solution)/shard_map/all_to_all | solution.py:28
  404.4 1.3 copy-done.2
  405.7 6.0 %all-to-all-start.1 = ((bf16[64,24,2048]{2,1,0:T(8,128)(2,1)}), bf16[64,24,2048]{2,1,0:T(8,128)(2,1)}, u32[]{:S(2)}, u32[]{:S(2)}) async-start(bf16[64,24,2048]{2,1,0:T(8,128)(2,1)} %bitcast.150), calls=%async_computation.1 | async-start | bytes 12582912 | tf_op jit(solution)/shard_map/all_to_all | solution.py:58
  411.8 0.1 copy.59
  411.9 2.2 copy.58
  414.1 1.8 copy.54
  415.9 2.2 copy.57
  418.1 134.5 %all-to-all-done.1 = bf16[64,24,2048]{2,1,0:T(8,128)(2,1)} async-done(((bf16[64,24,2048]{2,1,0:T(8,128)(2,1)}), bf16[64,24,2048]{2,1,0:T(8,128)(2,1)}, u32[]{:S(2)}, u32[]{:S(2)}) %all-to-all-start.1) | async-done | bytes 6291488 | tf_op jit(solution)/shard_map/all_to_all | solution.py:58
  552.6 12.5 %gather_fusion = bf16[1024,2048]{1,0:T(8,128)(2,1)} fusion(bf16[1536,2048]{1,0:T(8,128)(2,1)} %bitcast.78, s32[1024]{0:T(1024)S(1)} %broadcast_clamp_fusion), kind=kCustom, calls=%fused_computation | custom fusion | bytes 8392704 | tf_op jit(solution)/shard_map/gather | solution.py:60
  565.0 5.7 fusion.1
  570.8 1.1 copy.69
  (21 shorter events, 0.1 us)
Async XLA Ops:
  7.2 177.7 %copy-start = (bf16[128,2048]{1,0:T(8,128)(2,1)S(1)}, bf16[128,2048]{1,0:T(8,128)(2,1)}, u32[]{:S(2)}) copy-start(bf16[128,2048]{1,0:T(8,128)(2,1)} %param.6) | copy-start | bytes 1572868
  24.9 16.8 %copy-start.3 = (bf16[1,2,192,2048]{3,2,1,0:T(8,128)(2,1)S(1)}, bf16[1,2,192,2048]{3,2,1,0:T(8,128)(2,1)}, u32[]{:S(2)}) copy-start(bf16[1,2,192,2048]{3,2,1,0:T(8,128)(2,1)} %param.10) | copy-start | bytes 4718596
  28.6 36.1 %all-to-all-start.4 = ((bf16[64,2,3072]{2,1,0:T(2,128)(2,1)}), bf16[64,2,3072]{2,1,0:T(2,128)(2,1)S(1)}, u32[]{:S(2)}, u32[]{:S(2)}) async-start(bf16[64,2,3072]{2,1,0:T(2,128)(2,1)} %reshape.503), calls=%async_computation.4 | async-start | bytes 1572864 | tf_op jit(solution)/shard_map/all_to_all | solution.py:24
  41.7 29.4 %copy-start.6 = (s32[128,8]{0,1:T(8,128)S(1)}, s32[128,8]{0,1:T(8,128)}, u32[]{:S(2)}) copy-start(s32[128,8]{0,1:T(8,128)} %param.7) | copy-start | bytes 12292
  41.8 29.6 %copy-start.7 = (s32[64]{0:T(128)S(1)}, s32[64]{0:T(128)}, u32[]{:S(2)}) copy-start(s32[64]{0:T(128)} %param.9) | copy-start | bytes 772
  64.7 57.6 %all-to-all-start.2 = ((bf16[1,2,192,2048]{2,1,0,3:T(2,128)(2,1)}), bf16[1,2,192,2048]{2,1,0,3:T(2,128)(2,1)}, u32[]{:S(2)}, u32[]{:S(2)}) async-start(bf16[1,2,192,2048]{2,1,0,3:T(2,128)(2,1)} %copy.51), calls=%async_computation.2 | async-start | bytes 4194304 | tf_op jit(solution)/shard_map/all_to_all | solution.py:23
  122.3 72.8 %all-to-all-start.5 = ((bf16[64,1,192,32]{2,3,1,0:T(8,128)(2,1)}), bf16[64,1,192,32]{2,3,1,0:T(8,128)(2,1)S(1)}, u32[]{:S(2)}, u32[]{:S(2)}) async-start(bf16[64,1,192,32]{2,3,1,0:T(8,128)(2,1)} %fusion.10), calls=%async_computation.5 | async-start | bytes 2097152 | tf_op jit(solution)/shard_map/all_to_all | solution.py:29
  195.0 1.0 copy-start.4
  196.0 151.3 %all-to-all-start = ((bf16[64,24,2048]{2,1,0:T(8,128)(2,1)}), bf16[64,24,2048]{2,1,0:T(8,128)(2,1)}, u32[]{:S(2)}, u32[]{:S(2)}) async-start(bf16[64,24,2048]{2,1,0:T(8,128)(2,1)} %bitcast.144), calls=%async_computation | async-start | bytes 12582912 | tf_op jit(solution)/shard_map/all_to_all | solution.py:48
  206.5 146.7 %all-gather.3.cloned.1.call-start = ((), (), s32[]{:S(2)}) async-start(), calls=%async_computation.6 | async-start | bytes 7864320 | tf_op jit(solution)/shard_map/all_gather | solution.py:34
  207.2 161.7 %all-gather.5.cloned.1.call-start = ((), (), s32[]{:S(2)}) async-start(), calls=%async_computation.7 | async-start | bytes 3932160 | tf_op jit(solution)/shard_map/all_gather | solution.py:35
  347.4 57.0 %all-to-all-start.3 = ((bf16[64,2,192,32]{2,3,1,0:T(8,128)(2,1)}), bf16[64,2,192,32]{2,3,1,0:T(8,128)(2,1)S(1)}, u32[]{:S(2)}, u32[]{:S(2)}) async-start(bf16[64,2,192,32]{2,3,1,0:T(8,128)(2,1)} %broadcast_select_fusion), calls=%async_computation.3 | async-start | bytes 4194304 | tf_op jit(solution)/shard_map/all_to_all | solution.py:28
  404.4 1.3 copy-start.2
  404.4 7.3 %copy-start.5 = (f32[128,8]{0,1:T(8,128)S(1)}, f32[128,8]{0,1:T(8,128)}, u32[]{:S(2)}) copy-start(f32[128,8]{0,1:T(8,128)} %param.8) | copy-start | bytes 12292
  405.7 146.8 %all-to-all-start.1 = ((bf16[64,24,2048]{2,1,0:T(8,128)(2,1)}), bf16[64,24,2048]{2,1,0:T(8,128)(2,1)}, u32[]{:S(2)}, u32[]{:S(2)}) async-start(bf16[64,24,2048]{2,1,0:T(8,128)(2,1)} %bitcast.150), calls=%async_computation.1 | async-start | bytes 12582912 | tf_op jit(solution)/shard_map/all_to_all | solution.py:58
  552.6 19.3 %copy-start.1 = (bf16[128,2048]{1,0:T(8,128)(2,1)S(1)}, bf16[128,2048]{1,0:T(8,128)(2,1)}, u32[]{:S(2)}) copy-start(bf16[128,2048]{1,0:T(8,128)(2,1)} %param.6) | copy-start | bytes 1572868
Sparse Core Ops, SparseCore 0:
  209.2 69.1 all-gather.2
  280.1 42.7 all-gather.4

commit v2 on v1

v2 whole, which is shorter than its diff:
```python
import jax
import jax.numpy as jnp
from jax import lax
from jax.sharding import PartitionSpec as P


def per_device(tokens, expert_ids, gate_probs, placement, w_gate_up, w_down):
    tok_dev = tokens.shape[0]
    model_width = tokens.shape[1]
    top_count = expert_ids.shape[1]
    experts = placement.shape[0]
    capacity = min(tok_dev, 3 * tok_dev * top_count // (2 * experts))
    slots = experts * capacity
    numbers = jnp.arange(experts, dtype=jnp.int32)

    gate_rows = w_gate_up.reshape(-1, model_width)
    down_rows = w_down.reshape(-1, model_width)
    shard = jnp.concatenate([gate_rows, down_rows], axis=0).reshape(experts, -1)
    spread = lax.all_to_all(shard, "expert", 0, 0, tiled=True)

    owner = (placement[None, None, :] == expert_ids[:, :, None]).astype(jnp.int32)
    old_ids = jnp.sum(owner * numbers[None, None, :], axis=2)
    choice = (old_ids[:, :, None] == numbers[None, None, :]).astype(jnp.float32)
    token_hot = jnp.sum(choice, axis=1)
    earlier = (
        jnp.arange(tok_dev, dtype=jnp.int32)[None, :] < jnp.arange(tok_dev, dtype=jnp.int32)[:, None]
    ).astype(jnp.float32)
    before = jnp.dot(earlier, token_hot, preferred_element_type=jnp.float32)
    slot_of = jnp.sum(before[:, None, :] * choice, axis=2).astype(jnp.int32)
    flat_index = old_ids * capacity + slot_of
    slot_numbers = jnp.arange(slots, dtype=jnp.int32)
    hits = flat_index[None, :, :] == slot_numbers[:, None, None]
    pick = jnp.any(hits, axis=2).astype(jnp.bfloat16)
    buffer = jnp.dot(pick, tokens, preferred_element_type=jnp.float32).astype(jnp.bfloat16)
    buffer = buffer.reshape(experts, capacity, model_width)
    spread, buffer = lax.optimization_barrier((spread, buffer))

    gathered = (
        lax.all_gather(w_gate_up, "dp", axis=2, tiled=True),
        lax.all_gather(w_down, "dp", axis=1, tiled=True),
    )
    hidden_count = gathered[0].shape[2]
    gate_up_full = gathered[0].reshape(2 * hidden_count, model_width)
    down_full = gathered[1].reshape(hidden_count, model_width)

    received = lax.all_to_all(buffer, "expert", split_axis=0, concat_axis=0, tiled=True)
    reordered = jnp.take(spread, jnp.sum(
        jnp.where(placement[:, None] == numbers[None, :], numbers[:, None], 0), axis=0
    ), axis=0)
    reordered, received = lax.optimization_barrier((reordered, received))
    placed_rows = lax.all_to_all(reordered, "expert", 0, 0, tiled=True)

    row_block = received.reshape(-1, model_width)
    projected = lax.dot_general(
        row_block, gate_up_full, (((1,), (1,)), ((), ())), preferred_element_type=jnp.float32
    )
    gate_part = projected[:, :hidden_count]
    up_part = projected[:, hidden_count:]
    hidden = (jax.nn.silu(gate_part) * up_part).astype(jnp.bfloat16)
    result = jnp.dot(hidden, down_full, preferred_element_type=jnp.float32).astype(jnp.bfloat16)
    result = result.reshape(received.shape)
    placed_rows, result = lax.optimization_barrier((placed_rows, result))
    returned = lax.all_to_all(result, "expert", split_axis=0, concat_axis=0, tiled=True)
    flat_out = returned.reshape(slots, model_width)

    placed_rows = placed_rows.reshape(-1, model_width)
    gate_count = gate_rows.shape[0]
    placed_gate_up = placed_rows[:gate_count].reshape(w_gate_up.shape)
    placed_down = placed_rows[gate_count:].reshape(w_down.shape)

    gates = gate_probs / jnp.sum(gate_probs, axis=1, keepdims=True)
    weights = jnp.sum(jnp.where(hits, gates[None, :, :], 0.0), axis=2).T
    weights_hi = weights.astype(jnp.bfloat16)
    weights_lo = (weights - weights_hi.astype(jnp.float32)).astype(jnp.bfloat16)
    mixed_rows = jnp.dot(weights_hi, flat_out, preferred_element_type=jnp.float32) + jnp.dot(
        weights_lo, flat_out, preferred_element_type=jnp.float32
    )
    return (mixed_rows.astype(jnp.bfloat16), placed_gate_up, placed_down)


def solution(mesh):
    in_specs = (
        P(("dp", "expert"), None),
        P(("dp", "expert"), None),
        P(("dp", "expert"), None),
        P(),
        P("expert", None, "dp", None),
        P("expert", "dp", None),
    )
    out_specs = (P(("dp", "expert"), None), P("expert", None, "dp", None), P("expert", "dp", None))
    return jax.shard_map(
        per_device, mesh=mesh, in_specs=in_specs, out_specs=out_specs, check_vma=False
    )
```

time: 580 us -> 504 us (0.87)
  other arithmetic: 74.7 us -> 36.7 us
  starting transfers between devices: 47.7 us -> 31.5 us
  waiting for transfers between devices: 349 us -> 333 us
  local copies, waits for them, and re-layouts: 60.5 us -> 47.4 us
  matrix products: 32.8 us -> 40.1 us
    select_n x6 -> x2, other arithmetic: 38.5 us -> 1.96 us  [per_device(): jnp.take(spread, jnp.sum(jnp.where(placement[:, None] == numbers[None, :]...]
    another operation x3 -> x0, other arithmetic: 18.2 us -> none
    all_to_all x0 -> x2, other arithmetic: none -> 17.9 us  [the longest x1 14.8 us: per_device(): spread = lax.all_to_all(shard, 'expert', 0, 0, tiled=True)]
    gather x7 -> x1, local copies, waits for them, and re-layouts: 18.2 us -> 3.46 us  [per_device(): jnp.take(spread, jnp.sum(jnp.where(placement[:, None] == numbers[None, :]...]
    unnamed x1 -> x0, other arithmetic: 12.6 us -> none
    all_to_all x4 -> x2, starting transfers between devices: 31.2 us -> 18.9 us  [the longest x1 13.2 us: per_device(): spread = lax.all_to_all(shard, 'expert', 0, 0, tiled=True)]
    all_to_all x1, waiting for transfers between devices: 134 us -> 122 us  [per_device(): lax.all_to_all(result, 'expert', split_axis=0, concat_axis=0, tiled=True)]
    scatter x1 -> x0, local copies, waits for them, and re-layouts: 10.2 us -> none  [per_device(): jnp.zeros((experts * capacity, model_width), jnp.bfloat16).at[flat_index]]
  transfers between devices with their start and end apart: 8 -> 6, of which waited for: 5 -> 4; matrix products, arithmetic and copies ran while one was open for 22% -> 16% of each run, Pallas kernels for 0% -> 0%
where the time goes in v2:
time: 504 us; the launch traced here: 503 us
  waiting for transfers between devices  333 us (66%)
  local copies, waits for them, and re-layouts  47.4 us (9%)
  matrix products  40.1 us (8%)
  other arithmetic  36.7 us (7%)
  starting transfers between devices  31.5 us (6%)
  between operations  14.2 us (3%)
    all_to_all x1, waiting for transfers between devices, per_device(): lax.all_to_all(buffer, 'expert', split_axis=0, concat_axis=0, tiled=True)  135 us
    all_to_all x1, waiting for transfers between devices, per_device(): lax.all_to_all(result, 'expert', split_axis=0, concat_axis=0, tiled=True)  122 us
    all_to_all x1, waiting for transfers between devices, per_device(): spread = lax.all_to_all(shard, 'expert', 0, 0, tiled=True)  45.5 us
    all_to_all x1, waiting for transfers between devices, per_device(): placed_rows = lax.all_to_all(reordered, 'expert', 0, 0, tiled=True)  29.5 us
    unnamed x18, local copies, waits for them, and re-layouts  28.6 us
    dot_general x1, matrix products, per_device(): lax.dot_general(row_block, gate_up_full, (((1,), (1,)), ((), ())), prefer...  15.7 us
    all_to_all x1, other arithmetic, per_device(): spread = lax.all_to_all(shard, 'expert', 0, 0, tiled=True)  14.8 us
    all_to_all x1, starting transfers between devices, per_device(): spread = lax.all_to_all(shard, 'expert', 0, 0, tiled=True)  13.2 us
  transfers between devices with their start and end apart: 6, of which 4 were waited for; matrix products, arithmetic and copies ran while one was open for 16% of the time, Pallas kernels for 0%

profile of v2, /device:TPU:1, one launch (start us, length us, event | category | flops | bytes accessed | tf_op | source)
XLA Modules:
  0.0 503.2 jit_solution(15749133329509743146)
XLA Ops:
  7.2 0.0 copy-start
  7.2 1.9 pad_maximum_fusion
  9.0 5.6 %all_to_all.30 = bf16[64,1,18432]{2,1,0:T(2,128)(2,1)} reshape(bf16[576,2048]{1,0:T(8,128)(2,1)S(1)} %pad_maximum_fusion) | data formatting | bytes 4718592 | tf_op jit(solution)/shard_map/all_to_all | solution.py:19
  14.6 0.5 broadcast.51
  15.1 14.8 %reduce = bf16[64,18432]{1,0:T(8,128)(2,1)S(1)} reduce(bf16[64,1,18432]{2,1,0:T(2,128)(2,1)} %all_to_all.30, bf16[]{:T(256)} %broadcast.51), dimensions={1}, to_apply=%all_to_all.30.reduce_sub_computation | reduce | bytes 4718594 | tf_op jit(solution)/shard_map/all_to_all | solution.py:19
  29.9 0.0 copy-start.4
  29.9 0.0 copy-start.5
  29.9 3.0 reshape.96
  33.0 13.2 %all-to-all-start = ((bf16[64,2,9216]{2,1,0:T(2,128)(2,1)}), bf16[64,2,9216]{2,1,0:T(2,128)(2,1)S(1)}, u32[]{:S(2)}, u32[]{:S(2)}) async-start(bf16[64,2,9216]{2,1,0:T(2,128)(2,1)} %reshape.96), calls=%async_computation | async-start | bytes 4718592 | tf_op jit(solution)/shard_map/all_to_all | solution.py:19
  46.1 0.0 all-gather.3.cloned.1.call-start
  46.2 0.7 all-gather.3.cloned.1.call-update
  46.9 0.0 copy-done.4
  46.9 0.0 copy-done.5
  46.9 0.1 select_reduce_fusion.2
  47.0 0.1 fusion.9
  47.2 0.1 select_reduce_fusion.1
  47.2 5.6 %fusion = pred[1536,128]{1,0:T(8,128)(4,1)S(1)} fusion(s32[128,8]{0,1:T(8,128)S(1)} %convert_add_fusion), kind=kLoop, calls=%fused_computation.5 | loop fusion | flops 2949120 | bytes 200704 | tf_op jit(solution)/shard_map/reduce_or | solution.py:33
  52.8 0.0 copy-done
  52.8 4.4 convolution_convert_fusion.1
  57.3 45.5 %all-to-all-done = bf16[64,2,9216]{2,1,0:T(2,128)(2,1)S(1)} async-done(((bf16[64,2,9216]{2,1,0:T(2,128)(2,1)}), bf16[64,2,9216]{2,1,0:T(2,128)(2,1)S(1)}, u32[]{:S(2)}, u32[]{:S(2)}) %all-to-all-start) | async-done | bytes 2359328 | tf_op jit(solution)/shard_map/all_to_all | solution.py:19
  102.8 6.7 %reshape.97 = bf16[64,1,18432]{2,1,0:T(2,128)(2,1)} reshape(bf16[64,2,9216]{2,1,0:T(2,128)(2,1)S(1)} %all-to-all-done) | data formatting | bytes 4718592
  109.5 3.7 copy.28
  113.2 6.2 %all-to-all-start.1 = ((bf16[64,24,2048]{2,1,0:T(8,128)(2,1)}), bf16[64,24,2048]{2,1,0:T(8,128)(2,1)}, u32[]{:S(2)}, u32[]{:S(2)}) async-start(bf16[64,24,2048]{2,1,0:T(8,128)(2,1)} %bitcast.51), calls=%async_computation.1 | async-start | bytes 12582912 | tf_op jit(solution)/shard_map/all_to_all | solution.py:46
  119.3 0.2 all-gather.5.cloned.1.call-start
  119.6 0.5 all-gather.5.cloned.1.call-update
  120.1 0.1 select_reduce_fusion.3
  120.2 3.5 gather_fusion
  123.7 2.0 broadcast_select_fusion
  125.6 134.5 %all-to-all-done.1 = bf16[64,24,2048]{2,1,0:T(8,128)(2,1)} async-done(((bf16[64,24,2048]{2,1,0:T(8,128)(2,1)}), bf16[64,24,2048]{2,1,0:T(8,128)(2,1)}, u32[]{:S(2)}, u32[]{:S(2)}) %all-to-all-start.1) | async-done | bytes 6291488 | tf_op jit(solution)/shard_map/all_to_all | solution.py:46
  260.2 3.1 reduce.1
  263.3 4.7 reshape.98
  268.0 5.8 %all-to-all-start.2 = ((bf16[64,2,9216]{2,1,0:T(2,128)(2,1)}), bf16[64,2,9216]{2,1,0:T(2,128)(2,1)S(1)}, u32[]{:S(2)}, u32[]{:S(2)}) async-start(bf16[64,2,9216]{2,1,0:T(2,128)(2,1)} %reshape.98), calls=%async_computation.2 | async-start | bytes 4718592 | tf_op jit(solution)/shard_map/all_to_all | solution.py:51
  273.8 0.0 all-gather.3.cloned.1.call-done
  273.9 15.7 %fusion.16 = f32[1536,1536]{1,0:T(8,128)} fusion(bf16[1536,2048]{1,0:T(8,128)(2,1)} %bitcast.7, bf16[1536,2048]{1,0:T(8,128)(2,1)} %bitcast.58), kind=kOutput, calls=%fused_computation.39 | convolution fusion | flops 9663676416 | bytes 22020096 | tf_op jit(solution)/shard_map/dot_general | solution.py:54
  289.6 0.0 all-gather.5.cloned.1.call-done
  289.6 11.4 %convolution_convert_fusion = bf16[1536,2048]{1,0:T(8,128)(2,1)} fusion(bf16[1,768,2048]{2,1,0:T(8,128)(2,1)} %all-gather.5.cloned.1.call-done, f32[1536,1536]{1,0:T(8,128)} %fusion.16), kind=kOutput, calls=%fused_computation.1 | convolution fusion | flops 4842061824 | bytes 18874368 | tf_op jit(solution)/shard_map/dot_general | solution.py:60
  301.0 29.5 %all-to-all-done.2 = bf16[64,2,9216]{2,1,0:T(2,128)(2,1)S(1)} async-done(((bf16[64,2,9216]{2,1,0:T(2,128)(2,1)}), bf16[64,2,9216]{2,1,0:T(2,128)(2,1)S(1)}, u32[]{:S(2)}, u32[]{:S(2)}) %all-to-all-start.2) | async-done | bytes 2359328 | tf_op jit(solution)/shard_map/all_to_all | solution.py:51
  330.5 6.7 %reshape.99 = bf16[64,1,18432]{2,1,0:T(2,128)(2,1)} reshape(bf16[64,2,9216]{2,1,0:T(2,128)(2,1)S(1)} %all-to-all-done.2) | data formatting | bytes 4718592
  337.2 3.7 copy.27
  340.9 0.0 copy-start.3
  340.9 6.2 %all-to-all-start.3 = ((bf16[64,24,2048]{2,1,0:T(8,128)(2,1)}), bf16[64,24,2048]{2,1,0:T(8,128)(2,1)}, u32[]{:S(2)}, u32[]{:S(2)}) async-start(bf16[64,24,2048]{2,1,0:T(8,128)(2,1)} %bitcast.54), calls=%async_computation.3 | async-start | bytes 12582912 | tf_op jit(solution)/shard_map/all_to_all | solution.py:63
  347.1 0.0 copy-done.3
  347.1 9.1 %select_reduce_fusion = f32[1536,128]{1,0:T(8,128)} fusion(f32[128,8]{0,1:T(8,128)S(1)} %broadcast_divide_fusion, s32[128,8]{0,1:T(8,128)S(1)} %convert_add_fusion), kind=kLoop, calls=%fused_computation.3 | loop fusion | flops 4521984 | bytes 794624 | tf_op jit(solution)/shard_map/reduce_sum | solution.py:72
  356.2 4.4 reshape.85
  360.6 0.0 copy-start.2
  360.6 2.8 slice.20
  363.4 2.1 slice_bitcast_fusion
  365.5 122.4 %all-to-all-done.3 = bf16[64,24,2048]{2,1,0:T(8,128)(2,1)} async-done(((bf16[64,24,2048]{2,1,0:T(8,128)(2,1)}), bf16[64,24,2048]{2,1,0:T(8,128)(2,1)}, u32[]{:S(2)}, u32[]{:S(2)}) %all-to-all-start.3) | async-done | bytes 6291488 | tf_op jit(solution)/shard_map/all_to_all | solution.py:63
  487.9 0.0 copy-done.2
  487.9 0.0 copy-start.1
  487.9 3.9 fusion.13
  491.8 4.6 fusion.3
  496.4 0.0 copy-done.1
  (7 shorter events, 0.1 us)
Async XLA Ops:
  7.2 45.6 %copy-start = (bf16[128,2048]{1,0:T(8,128)(2,1)S(1)}, bf16[128,2048]{1,0:T(8,128)(2,1)}, u32[]{:S(2)}) copy-start(bf16[128,2048]{1,0:T(8,128)(2,1)} %param.6) | copy-start | bytes 1572868
  29.9 16.9 %copy-start.4 = (s32[128,8]{0,1:T(8,128)S(1)}, s32[128,8]{0,1:T(8,128)}, u32[]{:S(2)}) copy-start(s32[128,8]{0,1:T(8,128)} %param.7) | copy-start | bytes 12292
  29.9 16.9 %copy-start.5 = (s32[64]{0:T(128)S(1)}, s32[64]{0:T(128)}, u32[]{:S(2)}) copy-start(s32[64]{0:T(128)} %param.9) | copy-start | bytes 772
  33.0 69.8 %all-to-all-start = ((bf16[64,2,9216]{2,1,0:T(2,128)(2,1)}), bf16[64,2,9216]{2,1,0:T(2,128)(2,1)S(1)}, u32[]{:S(2)}, u32[]{:S(2)}) async-start(bf16[64,2,9216]{2,1,0:T(2,128)(2,1)} %reshape.96), calls=%async_computation | async-start | bytes 4718592 | tf_op jit(solution)/shard_map/all_to_all | solution.py:19
  46.1 227.7 %all-gather.3.cloned.1.call-start = ((), (), s32[]{:S(2)}) async-start(), calls=%async_computation.4 | async-start | bytes 7864320 | tf_op jit(solution)/shard_map/all_gather | solution.py:39
  113.2 147.0 %all-to-all-start.1 = ((bf16[64,24,2048]{2,1,0:T(8,128)(2,1)}), bf16[64,24,2048]{2,1,0:T(8,128)(2,1)}, u32[]{:S(2)}, u32[]{:S(2)}) async-start(bf16[64,24,2048]{2,1,0:T(8,128)(2,1)} %bitcast.51), calls=%async_computation.1 | async-start | bytes 12582912 | tf_op jit(solution)/shard_map/all_to_all | solution.py:46
  119.3 170.3 %all-gather.5.cloned.1.call-start = ((), (), s32[]{:S(2)}) async-start(), calls=%async_computation.5 | async-start | bytes 3932160 | tf_op jit(solution)/shard_map/all_gather | solution.py:40
  268.0 62.4 %all-to-all-start.2 = ((bf16[64,2,9216]{2,1,0:T(2,128)(2,1)}), bf16[64,2,9216]{2,1,0:T(2,128)(2,1)S(1)}, u32[]{:S(2)}, u32[]{:S(2)}) async-start(bf16[64,2,9216]{2,1,0:T(2,128)(2,1)} %reshape.98), calls=%async_computation.2 | async-start | bytes 4718592 | tf_op jit(solution)/shard_map/all_to_all | solution.py:51
  340.9 6.2 %copy-start.3 = (f32[128,8]{0,1:T(8,128)S(1)}, f32[128,8]{0,1:T(8,128)}, u32[]{:S(2)}) copy-start(f32[128,8]{0,1:T(8,128)} %param.8) | copy-start | bytes 12292
  340.9 147.0 %all-to-all-start.3 = ((bf16[64,24,2048]{2,1,0:T(8,128)(2,1)}), bf16[64,24,2048]{2,1,0:T(8,128)(2,1)}, u32[]{:S(2)}, u32[]{:S(2)}) async-start(bf16[64,24,2048]{2,1,0:T(8,128)(2,1)} %bitcast.54), calls=%async_computation.3 | async-start | bytes 12582912 | tf_op jit(solution)/shard_map/all_to_all | solution.py:63
  360.6 127.3 %copy-start.2 = (f32[1536,128]{1,0:T(8,128)S(1)}, f32[1536,128]{1,0:T(8,128)}, u32[]{:S(2)}) copy-start(f32[1536,128]{1,0:T(8,128)} %select_reduce_fusion) | copy-start | bytes 2359300
  487.9 8.5 %copy-start.1 = (bf16[128,2048]{1,0:T(8,128)(2,1)S(1)}, bf16[128,2048]{1,0:T(8,128)(2,1)}, u32[]{:S(2)}) copy-start(bf16[128,2048]{1,0:T(8,128)(2,1)} %param.6) | copy-start | bytes 1572868
Sparse Core Ops, SparseCore 0:
  48.8 69.1 all-gather.2
  122.0 43.0 all-gather.4

commit v3 on v2

--- a/solution.py
+++ b/solution.py
@@ -12,11 +12,6 @@
     capacity = min(tok_dev, 3 * tok_dev * top_count // (2 * experts))
     slots = experts * capacity
     numbers = jnp.arange(experts, dtype=jnp.int32)
-
-    gate_rows = w_gate_up.reshape(-1, model_width)
-    down_rows = w_down.reshape(-1, model_width)
-    shard = jnp.concatenate([gate_rows, down_rows], axis=0).reshape(experts, -1)
-    spread = lax.all_to_all(shard, "expert", 0, 0, tiled=True)
 
     owner = (placement[None, None, :] == expert_ids[:, :, None]).astype(jnp.int32)
     old_ids = jnp.sum(owner * numbers[None, None, :], axis=2)
@@ -33,7 +28,12 @@
     pick = jnp.any(hits, axis=2).astype(jnp.bfloat16)
     buffer = jnp.dot(pick, tokens, preferred_element_type=jnp.float32).astype(jnp.bfloat16)
     buffer = buffer.reshape(experts, capacity, model_width)
-    spread, buffer = lax.optimization_barrier((spread, buffer))
+
+    gate_rows = w_gate_up.reshape(-1, model_width)
+    down_rows = w_down.reshape(-1, model_width)
+    shard = jnp.concatenate([gate_rows, down_rows], axis=0)
+    chunks = shard.reshape(experts, capacity, -1)
+    outgoing = jnp.concatenate([buffer, chunks], axis=2)
 
     gathered = (
         lax.all_gather(w_gate_up, "dp", axis=2, tiled=True),
@@ -43,14 +43,11 @@
     gate_up_full = gathered[0].reshape(2 * hidden_count, model_width)
     down_full = gathered[1].reshape(hidden_count, model_width)
 
-    received = lax.all_to_all(buffer, "expert", split_axis=0, concat_axis=0, tiled=True)
-    reordered = jnp.take(spread, jnp.sum(
-        jnp.where(placement[:, None] == numbers[None, :], numbers[:, None], 0), axis=0
-    ), axis=0)
-    reordered, received = lax.optimization_barrier((reordered, received))
-    placed_rows = lax.all_to_all(reordered, "expert", 0, 0, tiled=True)
+    arrived = lax.all_to_all(outgoing, "expert", split_axis=0, concat_axis=0, tiled=True)
+    inverse = jnp.sum(jnp.where(placement[:, None] == numbers[None, :], numbers[:, None], 0), axis=0)
+    reordered = jnp.take(arrived[:, :, model_width:], inverse, axis=0)
 
-    row_block = received.reshape(-1, model_width)
+    row_block = arrived[:, :, :model_width].reshape(-1, model_width)
     projected = lax.dot_general(
         row_block, gate_up_full, (((1,), (1,)), ((), ())), preferred_element_type=jnp.float32
     )
@@ -58,12 +55,13 @@
     up_part = projected[:, hidden_count:]
     hidden = (jax.nn.silu(gate_part) * up_part).astype(jnp.bfloat16)
     result = jnp.dot(hidden, down_full, preferred_element_type=jnp.float32).astype(jnp.bfloat16)
-    result = result.reshape(received.shape)
-    placed_rows, result = lax.optimization_barrier((placed_rows, result))
-    returned = lax.all_to_all(result, "expert", split_axis=0, concat_axis=0, tiled=True)
-    flat_out = returned.reshape(slots, model_width)
+    result = result.reshape(experts, capacity, model_width)
+    back = lax.all_to_all(
+        jnp.concatenate([result, reordered], axis=2), "expert", split_axis=0, concat_axis=0, tiled=True
+    )
+    flat_out = back[:, :, :model_width].reshape(slots, model_width)
 
-    placed_rows = placed_rows.reshape(-1, model_width)
+    placed_rows = back[:, :, model_width:].reshape(-1, model_width)
     gate_count = gate_rows.shape[0]
     placed_gate_up = placed_rows[:gate_count].reshape(w_gate_up.shape)
     placed_down = placed_rows[gate_count:].reshape(w_down.shape)
@@ -72,9 +70,10 @@
     weights = jnp.sum(jnp.where(hits, gates[None, :, :], 0.0), axis=2).T
     weights_hi = weights.astype(jnp.bfloat16)
     weights_lo = (weights - weights_hi.astype(jnp.float32)).astype(jnp.bfloat16)
-    mixed_rows = jnp.dot(weights_hi, flat_out, preferred_element_type=jnp.float32) + jnp.dot(
-        weights_lo, flat_out, preferred_element_type=jnp.float32
+    both = jnp.dot(
+        jnp.concatenate([weights_hi, weights_lo], axis=0), flat_out, preferred_element_type=jnp.float32
     )
+    mixed_rows = both[:tok_dev] + both[tok_dev:]
     return (mixed_rows.astype(jnp.bfloat16), placed_gate_up, placed_down)
 
 

time: 504 us -> 494 us (0.980)
  waiting for transfers between devices: 333 us -> 373 us
  local copies, waits for them, and re-layouts: 47.4 us -> 29 us
  starting transfers between devices: 31.5 us -> 20 us
  matrix products: 40.1 us -> 29.3 us
  other arithmetic: 36.7 us -> 27.5 us
    all_to_all x4 -> x2, waiting for transfers between devices: 332 us -> 372 us  [the longest x1 190 us: per_device(): lax.all_to_all(outgoing, 'expert', split_axis=0, concat_axis=0, tiled=True)]
    unnamed x18 -> x14, local copies, waits for them, and re-layouts: 28.6 us -> 0.04 us
    all_to_all x2 -> x0, other arithmetic: 17.9 us -> none  [the longest x1 14.8 us: per_device(): spread = lax.all_to_all(shard, 'expert', 0, 0, tiled=True)]
    slice x0 -> x4, local copies, waits for them, and re-layouts: none -> 16.6 us  [the longest x1 6.6 us: per_device(): row_block = arrived[:, :, :model_width].reshape(-1, model_width)]
    all_to_all x4 -> x2, starting transfers between devices: 31.3 us -> 19.7 us  [the longest x1 13.4 us: per_device(): lax.all_to_all(outgoing, 'expert', split_axis=0, concat_axis=0, tiled=True)]
    concatenate x1 -> x3, other arithmetic: 1.86 us -> 9.28 us  [the longest x1 3.74 us: per_device(): outgoing = jnp.concatenate([buffer, chunks], axis=2)]
    dot_general x2 -> x1, matrix products: 8.46 us -> 1.82 us  [per_device(): jnp.dot(jnp.concatenate([weights_hi, weights_lo], axis=0), flat_out, pref...]
    all_to_all x2 -> x0, local copies, waits for them, and re-layouts: 6.07 us -> none  [per_device(): spread = lax.all_to_all(shard, 'expert', 0, 0, tiled=True)]
  transfers between devices with their start and end apart: 6 -> 4, of which waited for: 4 -> 2; matrix products, arithmetic and copies ran while one was open for 16% -> 8% of each run, Pallas kernels for 0% -> 0%
where the time goes in v3:
time: 494 us; the launch traced here: 493 us
  waiting for transfers between devices  373 us (76%)
  matrix products  29.3 us (6%)
  local copies, waits for them, and re-layouts  29 us (6%)
  other arithmetic  27.5 us (6%)
  starting transfers between devices  20 us (4%)
  between operations  14.2 us (3%)
    all_to_all x1, waiting for transfers between devices, per_device(): lax.all_to_all(outgoing, 'expert', split_axis=0, concat_axis=0, tiled=True)  190 us
    all_to_all x1, waiting for transfers between devices, per_device(): lax.all_to_all(jnp.concatenate([result, reordered], axis=2), 'expert', sp...  182 us
    dot_general x1, matrix products, per_device(): lax.dot_general(row_block, gate_up_full, (((1,), (1,)), ((), ())), prefer...  15.7 us
    all_to_all x1, starting transfers between devices, per_device(): lax.all_to_all(outgoing, 'expert', split_axis=0, concat_axis=0, tiled=True)  13.4 us
  transfers between devices with their start and end apart: 4, of which 2 were waited for; matrix products, arithmetic and copies ran while one was open for 8% of the time, Pallas kernels for 0%

profile of v3, /device:TPU:1, one launch (start us, length us, event | category | flops | bytes accessed | tf_op | source)
XLA Modules:
  0.0 493.3 jit_solution(1332162074656986565)
XLA Ops:
  7.2 0.0 copy-start
  7.2 0.8 select_reduce_fusion.2
  8.1 0.1 fusion.11
  8.2 0.1 select_reduce_fusion.1
  8.3 5.6 %fusion = pred[1536,128]{1,0:T(8,128)(4,1)S(1)} fusion(s32[128,8]{0,1:T(8,128)S(1)} %convert_add_fusion), kind=kLoop, calls=%fused_computation.7 | loop fusion | flops 2949120 | bytes 200704 | tf_op jit(solution)/shard_map/reduce_or | solution.py:28
  13.9 1.8 pad_maximum_fusion.2
  15.7 3.6 reshape.77
  19.3 0.0 copy-done
  19.3 0.0 copy-start.3
  19.3 1.8 convolution_convert_fusion.1
  21.1 0.0 copy-done.3
  21.1 3.7 pad_maximum_fusion
  24.8 0.0 copy-start.6
  24.9 13.4 %all-to-all-start = ((bf16[64,24,2816]{2,1,0:T(8,128)(2,1)}), bf16[64,24,2816]{2,1,0:T(8,128)(2,1)}, u32[]{:S(2)}, u32[]{:S(2)}) async-start(bf16[64,24,2816]{2,1,0:T(8,128)(2,1)} %pad_maximum_fusion), calls=%async_computation | async-start | bytes 17301504 | tf_op jit(solution)/shard_map/all_to_all | solution.py:46
  38.3 0.0 all-gather.3.cloned.1.call-start
  38.4 0.7 all-gather.3.cloned.1.call-update
  39.0 0.2 all-gather.5.cloned.1.call-start
  39.3 0.5 all-gather.5.cloned.1.call-update
  39.8 0.0 copy-done.6
  39.8 0.1 select_reduce_fusion.3
  39.9 189.8 %all-to-all-done = bf16[64,24,2816]{2,1,0:T(8,128)(2,1)} async-done(((bf16[64,24,2816]{2,1,0:T(8,128)(2,1)}), bf16[64,24,2816]{2,1,0:T(8,128)(2,1)}, u32[]{:S(2)}, u32[]{:S(2)}) %all-to-all-start) | async-done | bytes 8650784 | tf_op jit(solution)/shard_map/all_to_all | solution.py:46
  229.7 3.3 slice.45
  233.0 2.4 gather_fusion
  235.4 6.6 %slice.42 = bf16[64,24,2048]{2,1,0:T(8,128)(2,1)} slice(bf16[64,24,2816]{2,1,0:T(8,128)(2,1)} %all-to-all-done), slice={[0:64], [0:24], [0:2048]} | slice | bytes 12582912 | tf_op jit(solution)/shard_map/slice | solution.py:50
  242.0 1.7 broadcast_select_fusion
  243.6 0.0 all-gather.3.cloned.1.call-done
  243.6 15.7 %fusion.15 = f32[1536,1536]{1,0:T(8,128)} fusion(bf16[1536,2048]{1,0:T(8,128)(2,1)} %bitcast.31, bf16[1536,2048]{1,0:T(8,128)(2,1)} %bitcast.36), kind=kOutput, calls=%fused_computation.41 | convolution fusion | flops 9663676416 | bytes 22020096 | tf_op jit(solution)/shard_map/dot_general | solution.py:51
  259.4 0.0 copy-start.2
  259.4 0.0 all-gather.5.cloned.1.call-done
  259.4 9.8 %convolution_convert_fusion = bf16[1536,2048]{1,0:T(8,128)(2,1)S(1)} fusion(bf16[1,768,2048]{2,1,0:T(8,128)(2,1)} %all-gather.5.cloned.1.call-done, f32[1536,1536]{1,0:T(8,128)} %fusion.15), kind=kOutput, calls=%fused_computation.3 | convolution fusion | flops 4842061824 | bytes 18874368 | tf_op jit(solution)/shard_map/dot_general | solution.py:57
  269.2 0.0 copy-done.2
  269.2 3.7 pad_maximum_fusion.1
  273.0 0.0 copy-start.5
  273.0 6.3 %all-to-all-start.1 = ((bf16[64,24,2816]{2,1,0:T(8,128)(2,1)}), bf16[64,24,2816]{2,1,0:T(8,128)(2,1)}, u32[]{:S(2)}, u32[]{:S(2)}) async-start(bf16[64,24,2816]{2,1,0:T(8,128)(2,1)} %pad_maximum_fusion.1), calls=%async_computation.1 | async-start | bytes 17301504 | tf_op jit(solution)/shard_map/all_to_all | solution.py:59
  279.2 0.0 copy-done.5
  279.3 8.1 %select_reduce_fusion = f32[1536,128]{1,0:T(8,128)S(1)} fusion(f32[128,8]{0,1:T(8,128)S(1)} %broadcast_divide_fusion, s32[128,8]{0,1:T(8,128)S(1)} %convert_add_fusion), kind=kLoop, calls=%fused_computation.5 | loop fusion | flops 4521984 | bytes 794624 | tf_op jit(solution)/shard_map/reduce_sum | solution.py:70
  287.4 0.8 fusion.10
  288.2 182.4 %all-to-all-done.1 = bf16[64,24,2816]{2,1,0:T(8,128)(2,1)} async-done(((bf16[64,24,2816]{2,1,0:T(8,128)(2,1)}), bf16[64,24,2816]{2,1,0:T(8,128)(2,1)}, u32[]{:S(2)}, u32[]{:S(2)}) %all-to-all-start.1) | async-done | bytes 8650784 | tf_op jit(solution)/shard_map/all_to_all | solution.py:59
  470.6 3.3 slice.49
  473.9 4.2 reshape.83
  478.1 1.2 slice.50
  479.4 0.9 slice_bitcast_fusion
  480.3 0.0 copy-start.4
  480.3 3.4 slice.46
  483.7 0.0 copy-done.4
  483.7 0.0 copy-start.1
  483.8 1.8 fusion.6
  485.6 0.9 fusion.5
  486.5 0.0 copy-done.1
  (7 shorter events, 0.1 us)
Async XLA Ops:
  7.2 12.1 %copy-start = (bf16[128,2048]{1,0:T(8,128)(2,1)S(1)}, bf16[128,2048]{1,0:T(8,128)(2,1)}, u32[]{:S(2)}) copy-start(bf16[128,2048]{1,0:T(8,128)(2,1)} %param.6) | copy-start | bytes 1572868
  19.3 1.8 copy-start.3
  24.8 14.9 %copy-start.6 = (s32[64]{0:T(128)S(1)}, s32[64]{0:T(128)}, u32[]{:S(2)}) copy-start(s32[64]{0:T(128)} %param.9) | copy-start | bytes 772
  24.9 204.9 %all-to-all-start = ((bf16[64,24,2816]{2,1,0:T(8,128)(2,1)}), bf16[64,24,2816]{2,1,0:T(8,128)(2,1)}, u32[]{:S(2)}, u32[]{:S(2)}) async-start(bf16[64,24,2816]{2,1,0:T(8,128)(2,1)} %pad_maximum_fusion), calls=%async_computation | async-start | bytes 17301504 | tf_op jit(solution)/shard_map/all_to_all | solution.py:46
  38.3 205.3 %all-gather.3.cloned.1.call-start = ((), (), s32[]{:S(2)}) async-start(), calls=%async_computation.2 | async-start | bytes 7864320 | tf_op jit(solution)/shard_map/all_gather | solution.py:39
  39.0 220.3 %all-gather.5.cloned.1.call-start = ((), (), s32[]{:S(2)}) async-start(), calls=%async_computation.3 | async-start | bytes 3932160 | tf_op jit(solution)/shard_map/all_gather | solution.py:40
  259.4 9.9 %copy-start.2 = (bf16[64,24,768]{2,1,0:T(8,128)(2,1)S(1)}, bf16[64,24,768]{2,1,0:T(8,128)(2,1)}, u32[]{:S(2)}) copy-start(bf16[64,24,768]{2,1,0:T(8,128)(2,1)} %broadcast_select_fusion) | copy-start | bytes 7077892
  273.0 6.3 %copy-start.5 = (f32[128,8]{0,1:T(8,128)S(1)}, f32[128,8]{0,1:T(8,128)}, u32[]{:S(2)}) copy-start(f32[128,8]{0,1:T(8,128)} %param.8) | copy-start | bytes 12292
  273.0 197.7 %all-to-all-start.1 = ((bf16[64,24,2816]{2,1,0:T(8,128)(2,1)}), bf16[64,24,2816]{2,1,0:T(8,128)(2,1)}, u32[]{:S(2)}, u32[]{:S(2)}) async-start(bf16[64,24,2816]{2,1,0:T(8,128)(2,1)} %pad_maximum_fusion.1), calls=%async_computation.1 | async-start | bytes 17301504 | tf_op jit(solution)/shard_map/all_to_all | solution.py:59
  480.3 3.4 copy-start.4
  483.7 2.7 copy-start.1
Sparse Core Ops, SparseCore 0:
  41.0 69.1 all-gather.2
  111.9 42.7 all-gather.4

commit v4 on v3

v4 whole, which is shorter than its diff:
```python
import jax
import jax.numpy as jnp
from jax import lax
from jax.sharding import PartitionSpec as P


def per_device(tokens, expert_ids, gate_probs, placement, w_gate_up, w_down):
    tok_dev = tokens.shape[0]
    model_width = tokens.shape[1]
    top_count = expert_ids.shape[1]
    experts = placement.shape[0]
    capacity = min(tok_dev, 3 * tok_dev * top_count // (2 * experts))
    slots = experts * capacity
    numbers = jnp.arange(experts, dtype=jnp.int32)

    owner = (placement[None, None, :] == expert_ids[:, :, None]).astype(jnp.int32)
    old_ids = jnp.sum(owner * numbers[None, None, :], axis=2)
    choice = (old_ids[:, :, None] == numbers[None, None, :]).astype(jnp.float32)
    token_hot = jnp.sum(choice, axis=1)
    earlier = (
        jnp.arange(tok_dev, dtype=jnp.int32)[None, :] < jnp.arange(tok_dev, dtype=jnp.int32)[:, None]
    ).astype(jnp.float32)
    before = jnp.dot(earlier, token_hot, preferred_element_type=jnp.float32)
    slot_of = jnp.sum(before[:, None, :] * choice, axis=2).astype(jnp.int32)
    flat_index = old_ids * capacity + slot_of
    slot_numbers = jnp.arange(slots, dtype=jnp.int32)
    hits = flat_index.T[None, :, :] == slot_numbers[:, None, None]
    pick = jnp.any(hits, axis=1).astype(jnp.bfloat16).reshape(experts, capacity, tok_dev)
    head = 8 if capacity > 8 else capacity
    first_pick = pick[:, :head].reshape(-1, tok_dev)
    second_pick = pick[:, head:].reshape(-1, tok_dev)

    def select_rows(chosen):
        rows = jnp.dot(chosen, tokens, preferred_element_type=jnp.float32).astype(jnp.bfloat16)
        return rows.reshape(experts, -1, model_width)

    gate_rows = w_gate_up.reshape(experts, head, -1)
    down_rows = w_down.reshape(experts, head, -1)
    gate_width = gate_rows.shape[2]
    chunk_width = gate_width + down_rows.shape[2]

    gathered = (
        lax.all_gather(w_gate_up, "dp", axis=2, tiled=True),
        lax.all_gather(w_down, "dp", axis=1, tiled=True),
    )
    hidden_count = gathered[0].shape[2]
    gate_up_full = gathered[0].reshape(2 * hidden_count, model_width)
    down_full = gathered[1].reshape(hidden_count, model_width)

    def expert_block(rows):
        row_block = rows.reshape(-1, model_width)
        projected = lax.dot_general(
            row_block, gate_up_full, (((1,), (1,)), ((), ())), preferred_element_type=jnp.float32
        )
        gate_part = projected[:, :hidden_count]
        up_part = projected[:, hidden_count:]
        hidden = (jax.nn.silu(gate_part) * up_part).astype(jnp.bfloat16)
        out = jnp.dot(hidden, down_full, preferred_element_type=jnp.float32).astype(jnp.bfloat16)
        return out.reshape(experts, -1, model_width)

    def exchange(block):
        return lax.all_to_all(block, "expert", split_axis=0, concat_axis=0, tiled=True)

    first_out = jnp.concatenate([select_rows(first_pick), gate_rows, down_rows], axis=2)
    second_out = select_rows(second_pick)
    first_in = exchange(first_out)
    first_in, second_out = lax.optimization_barrier((first_in, second_out))
    second_in = exchange(second_out)

    inverse = jnp.sum(jnp.where(placement[:, None] == numbers[None, :], numbers[:, None], 0), axis=0)
    reordered = jnp.take(first_in[:, :, model_width:], inverse, axis=0)
    first_back = jnp.concatenate([expert_block(first_in[:, :, :model_width]), reordered], axis=2)
    second_in, first_back = lax.optimization_barrier((second_in, first_back))
    first_ret = exchange(first_back)
    second_back = expert_block(second_in)
    first_ret, second_back = lax.optimization_barrier((first_ret, second_back))
    second_ret = exchange(second_back)

    placed_chunks = first_ret[:, :, model_width:]
    placed_gate_up = placed_chunks[:, :, :gate_width].reshape(w_gate_up.shape)
    placed_down = placed_chunks[:, :, gate_width:chunk_width].reshape(w_down.shape)

    gates = gate_probs / jnp.sum(gate_probs, axis=1, keepdims=True)
    weights = jnp.sum(jnp.where(hits, gates.T[None, :, :], 0.0), axis=1)
    weights = weights.reshape(experts, capacity, tok_dev)

    def mix(part, returned):
        part = part.reshape(-1, tok_dev).T
        part_hi = part.astype(jnp.bfloat16)
        part_lo = (part - part_hi.astype(jnp.float32)).astype(jnp.bfloat16)
        flat = returned.reshape(-1, model_width)
        both = jnp.dot(
            jnp.concatenate([part_hi, part_lo], axis=0), flat, preferred_element_type=jnp.float32
        )
        return both[:tok_dev] + both[tok_dev:]

    mixed_rows = mix(weights[:, :head], first_ret[:, :, :model_width]) + mix(
        weights[:, head:], second_ret
    )
    return (mixed_rows.astype(jnp.bfloat16), placed_gate_up, placed_down)


def solution(mesh):
    in_specs = (
        P(("dp", "expert"), None),
        P(("dp", "expert"), None),
        P(("dp", "expert"), None),
        P(),
        P("expert", None, "dp", None),
        P("expert", "dp", None),
    )
    out_specs = (P(("dp", "expert"), None), P("expert", None, "dp", None), P("expert", "dp", None))
    return jax.shard_map(
        per_device, mesh=mesh, in_specs=in_specs, out_specs=out_specs, check_vma=False
    )
```

time: 494 us -> 460 us (0.931)
  waiting for transfers between devices: 373 us -> 335 us
  starting transfers between devices: 20 us -> 31.8 us
  local copies, waits for them, and re-layouts: 29 us -> 17.3 us
  matrix products: 29.3 us -> 38.5 us
  other arithmetic: 27.5 us -> 22.3 us
    all_to_all x2 -> x4, waiting for transfers between devices: 372 us -> 305 us  [exchange(): lax.all_to_all(block, 'expert', split_axis=0, concat_axis=0, tiled=True)]
    all_gather x1, waiting for transfers between devices: 0.01 us -> 28.9 us  [per_device(): lax.all_gather(w_down, 'dp', axis=1, tiled=True)]
    slice x5, local copies, waits for them, and re-layouts: 17.8 us -> 5.98 us  [the longest x1 3.22 us: per_device(): reordered = jnp.take(first_in[:, :, model_width:], inverse, axis=0)]
    all_to_all x2 -> x4, starting transfers between devices: 19.7 us -> 31.5 us  [exchange(): lax.all_to_all(block, 'expert', split_axis=0, concat_axis=0, tiled=True)]
    dot_general x4 -> x8, matrix products: 29.1 us -> 38.3 us  [the longest x2 18.8 us: expert_block(): lax.dot_general(row_block, gate_up_full, (((1,), (1,)), ((), ())), prefer...]
  transfers between devices with their start and end apart: 4 -> 6, of which waited for: 2 -> 5; matrix products, arithmetic and copies ran while one was open for 8% -> 13% of each run, Pallas kernels for 0% -> 0%
where the time goes in v4:
time: 460 us; the launch traced here: 459 us
  waiting for transfers between devices  335 us (73%)
  matrix products  38.5 us (8%)
  starting transfers between devices  31.8 us (7%)
  other arithmetic  22.3 us (5%)
  local copies, waits for them, and re-layouts  17.3 us (4%)
  between operations  14.3 us (3%)
    all_to_all x4, waiting for transfers between devices, exchange(): lax.all_to_all(block, 'expert', split_axis=0, concat_axis=0, tiled=True)  305 us
    all_to_all x4, starting transfers between devices, exchange(): lax.all_to_all(block, 'expert', split_axis=0, concat_axis=0, tiled=True)  31.5 us
    all_gather x1, waiting for transfers between devices, per_device(): lax.all_gather(w_down, 'dp', axis=1, tiled=True)  28.9 us
    dot_general x2, matrix products, expert_block(): lax.dot_general(row_block, gate_up_full, (((1,), (1,)), ((), ())), prefer...  18.8 us
    dot_general x2, matrix products, expert_block(): jnp.dot(hidden, down_full, preferred_element_type=jnp.float32)  9.74 us
  transfers between devices with their start and end apart: 6, of which 5 were waited for; matrix products, arithmetic and copies ran while one was open for 13% of the time, Pallas kernels for 0%

profile of v4, /device:TPU:1, one launch (start us, length us, event | category | flops | bytes accessed | tf_op | source)
XLA Modules:
  0.0 459.0 jit_solution(4246679109943259744)
XLA Ops:
  7.2 0.0 copy-start
  7.2 0.0 copy-start.5
  7.2 0.0 copy-start.6
  7.2 2.1 reshape.98
  9.3 2.9 reshape.97
  12.2 0.0 copy-done.5
  12.2 0.0 copy-done.6
  12.2 0.1 select_reduce_fusion.2
  12.3 0.1 fusion.34
  12.5 0.1 select_reduce_fusion.1
  12.6 5.6 %fusion = pred[1536,128]{1,0:T(8,128)(4,1)S(1)} fusion(s32[8,128]{1,0:T(8,128)S(1)} %add_bitcast_fusion), kind=kLoop, calls=%fused_computation.3 | loop fusion | flops 2949120 | bytes 200704 | tf_op jit(solution)/shard_map/reduce_or | solution.py:28
  18.1 0.0 copy-done
  18.1 0.7 fusion.8
  18.9 2.3 pad_maximum_fusion
  21.2 13.3 %all-to-all-start = ((bf16[64,8,4352]{2,1,0:T(8,128)(2,1)}), bf16[64,8,4352]{2,1,0:T(8,128)(2,1)}, u32[]{:S(2)}, u32[]{:S(2)}) async-start(bf16[64,8,4352]{2,1,0:T(8,128)(2,1)} %pad_maximum_fusion), calls=%async_computation | async-start | bytes 8912896 | tf_op jit(solution)/shard_map/all_to_all | solution.py:62
  34.5 0.0 all-gather.3.cloned.1.call-start
  34.5 0.7 all-gather.3.cloned.1.call-update
  35.3 3.2 convolution_convert_fusion.1
  38.4 97.6 %all-to-all-done = bf16[64,8,4352]{2,1,0:T(8,128)(2,1)} async-done(((bf16[64,8,4352]{2,1,0:T(8,128)(2,1)}), bf16[64,8,4352]{2,1,0:T(8,128)(2,1)}, u32[]{:S(2)}, u32[]{:S(2)}) %all-to-all-start) | async-done | bytes 4456480 | tf_op jit(solution)/shard_map/all_to_all | solution.py:62
  136.0 6.1 %all-to-all-start.1 = ((bf16[64,16,2048]{2,1,0:T(8,128)(2,1)}), bf16[64,16,2048]{2,1,0:T(8,128)(2,1)}, u32[]{:S(2)}, u32[]{:S(2)}) async-start(bf16[64,16,2048]{2,1,0:T(8,128)(2,1)} %bitcast.65), calls=%async_computation.1 | async-start | bytes 8388608 | tf_op jit(solution)/shard_map/all_to_all | solution.py:62
  142.1 0.2 all-gather.5.cloned.1.call-start
  142.3 0.5 all-gather.5.cloned.1.call-update
  142.8 0.1 select_reduce_fusion.3
  143.0 3.2 slice.60
  146.2 2.4 gather_fusion
  148.6 1.7 broadcast_select_fusion
  150.3 0.0 all-gather.3.cloned.1.call-done
  150.3 8.6 %fusion.14 = f32[512,1536]{1,0:T(8,128)} fusion(bf16[1536,2048]{1,0:T(8,128)(2,1)} %bitcast.72, bf16[64,8,4352]{2,1,0:T(8,128)(2,1)} %all-to-all-done), kind=kOutput, calls=%fused_computation.20 | convolution fusion | flops 3221225472 | bytes 11534336 | tf_op jit(solution)/shard_map/dot_general | solution.py:52
  158.9 0.0 copy-start.2
  158.9 28.9 %all-gather.5.cloned.1.call-done = bf16[1,768,2048]{2,1,0:T(8,128)(2,1)} async-done(((bf16[1,192,2048]{2,1,0:T(8,128)(2,1)}), bf16[1,768,2048]{2,1,0:T(8,128)(2,1)}) %all-gather.5.cloned.1.call-update) | async-done | bytes 3145744 | tf_op jit(solution)/shard_map/all_gather | solution.py:44
  187.8 4.7 %fusion.9 = bf16[64,8,2048]{2,1,0:T(8,128)(2,1)S(1)} fusion(bf16[1,768,2048]{2,1,0:T(8,128)(2,1)} %all-gather.5.cloned.1.call-done, f32[512,1536]{1,0:T(8,128)} %fusion.14), kind=kOutput, calls=%fused_computation.16 | convolution fusion | flops 1614020608 | bytes 8388608 | tf_op jit(solution)/shard_map/dot_general | solution.py:58
  192.5 0.0 copy-done.2
  192.5 2.4 pad_maximum_fusion.1
  194.9 43.1 %all-to-all-done.1 = bf16[64,16,2048]{2,1,0:T(8,128)(2,1)} async-done(((bf16[64,16,2048]{2,1,0:T(8,128)(2,1)}), bf16[64,16,2048]{2,1,0:T(8,128)(2,1)}, u32[]{:S(2)}, u32[]{:S(2)}) %all-to-all-start.1) | async-done | bytes 4194336 | tf_op jit(solution)/shard_map/all_to_all | solution.py:62
  238.0 5.9 %all-to-all-start.2 = ((bf16[64,8,4352]{2,1,0:T(8,128)(2,1)}), bf16[64,8,4352]{2,1,0:T(8,128)(2,1)}, u32[]{:S(2)}, u32[]{:S(2)}) async-start(bf16[64,8,4352]{2,1,0:T(8,128)(2,1)} %pad_maximum_fusion.1), calls=%async_computation.2 | async-start | bytes 8912896 | tf_op jit(solution)/shard_map/all_to_all | solution.py:62
  243.9 0.0 copy-start.7
  243.9 10.2 %fusion.41 = f32[1024,1536]{1,0:T(8,128)S(1)} fusion(bf16[1024,2048]{1,0:T(8,128)(2,1)} %bitcast.17, bf16[1536,2048]{1,0:T(8,128)(2,1)} %bitcast.73), kind=kOutput, calls=%fused_computation.65 | convolution fusion | flops 6442450944 | bytes 16777216 | tf_op jit(solution)/shard_map/dot_general | solution.py:52
  254.1 0.0 copy-done.7
  254.1 5.1 %convolution_convert_fusion = bf16[1024,2048]{1,0:T(8,128)(2,1)} fusion(bf16[1,768,2048]{2,1,0:T(8,128)(2,1)S(1)} %copy-done.7, f32[1024,1536]{1,0:T(8,128)S(1)} %fusion.41), kind=kOutput, calls=%fused_computation.6 | convolution fusion | flops 3228041216 | bytes 13631488 | tf_op jit(solution)/shard_map/dot_general | solution.py:58
  259.2 86.2 %all-to-all-done.2 = bf16[64,8,4352]{2,1,0:T(8,128)(2,1)} async-done(((bf16[64,8,4352]{2,1,0:T(8,128)(2,1)}), bf16[64,8,4352]{2,1,0:T(8,128)(2,1)}, u32[]{:S(2)}, u32[]{:S(2)}) %all-to-all-start.2) | async-done | bytes 4456480 | tf_op jit(solution)/shard_map/all_to_all | solution.py:62
  345.4 0.0 copy-start.4
  345.4 6.2 %all-to-all-start.3 = ((bf16[64,16,2048]{2,1,0:T(8,128)(2,1)}), bf16[64,16,2048]{2,1,0:T(8,128)(2,1)}, u32[]{:S(2)}, u32[]{:S(2)}) async-start(bf16[64,16,2048]{2,1,0:T(8,128)(2,1)} %bitcast.66), calls=%async_computation.3 | async-start | bytes 8388608 | tf_op jit(solution)/shard_map/all_to_all | solution.py:62
  351.7 0.0 copy-done.4
  351.7 8.1 %select_reduce_fusion = f32[1536,128]{1,0:T(8,128)S(1)} fusion(f32[8,128]{1,0:T(8,128)S(1)} %divide_bitcast_fusion, s32[8,128]{1,0:T(8,128)S(1)} %add_bitcast_fusion), kind=kLoop, calls=%fused_computation.1 | loop fusion | flops 4521984 | bytes 794624 | tf_op jit(solution)/shard_map/reduce_sum | solution.py:84
  359.9 0.8 fusion.29
  360.7 1.5 slice.69
  362.2 1.2 slice.70
  363.4 2.2 reshape.110
  365.6 1.8 reshape.111
  367.3 0.0 copy-start.3
  367.3 2.4 fusion.12
  369.7 77.9 %all-to-all-done.3 = bf16[64,16,2048]{2,1,0:T(8,128)(2,1)} async-done(((bf16[64,16,2048]{2,1,0:T(8,128)(2,1)}), bf16[64,16,2048]{2,1,0:T(8,128)(2,1)}, u32[]{:S(2)}, u32[]{:S(2)}) %all-to-all-start.3) | async-done | bytes 4194336 | tf_op jit(solution)/shard_map/all_to_all | solution.py:62
  447.5 0.0 copy-done.3
  447.5 0.0 copy-start.1
  447.5 3.5 fusion.25
  451.0 1.1 fusion.22
  452.1 0.0 copy-done.1
  (10 shorter events, 0.2 us)
Async XLA Ops:
  7.2 11.0 %copy-start = (bf16[128,2048]{1,0:T(8,128)(2,1)S(1)}, bf16[128,2048]{1,0:T(8,128)(2,1)}, u32[]{:S(2)}) copy-start(bf16[128,2048]{1,0:T(8,128)(2,1)} %param.6) | copy-start | bytes 1572868
  7.2 5.0 %copy-start.5 = (s32[128,8]{0,1:T(8,128)S(1)}, s32[128,8]{0,1:T(8,128)}, u32[]{:S(2)}) copy-start(s32[128,8]{0,1:T(8,128)} %param.7) | copy-start | bytes 12292
  7.2 5.0 %copy-start.6 = (s32[64]{0:T(128)S(1)}, s32[64]{0:T(128)}, u32[]{:S(2)}) copy-start(s32[64]{0:T(128)} %param.9) | copy-start | bytes 772
  21.2 114.9 %all-to-all-start = ((bf16[64,8,4352]{2,1,0:T(8,128)(2,1)}), bf16[64,8,4352]{2,1,0:T(8,128)(2,1)}, u32[]{:S(2)}, u32[]{:S(2)}) async-start(bf16[64,8,4352]{2,1,0:T(8,128)(2,1)} %pad_maximum_fusion), calls=%async_computation | async-start | bytes 8912896 | tf_op jit(solution)/shard_map/all_to_all | solution.py:62
  34.5 115.8 %all-gather.3.cloned.1.call-start = ((), (), s32[]{:S(2)}) async-start(), calls=%async_computation.4 | async-start | bytes 7864320 | tf_op jit(solution)/shard_map/all_gather | solution.py:43
  136.0 102.0 %all-to-all-start.1 = ((bf16[64,16,2048]{2,1,0:T(8,128)(2,1)}), bf16[64,16,2048]{2,1,0:T(8,128)(2,1)}, u32[]{:S(2)}, u32[]{:S(2)}) async-start(bf16[64,16,2048]{2,1,0:T(8,128)(2,1)} %bitcast.65), calls=%async_computation.1 | async-start | bytes 8388608 | tf_op jit(solution)/shard_map/all_to_all | solution.py:62
  142.1 45.7 %all-gather.5.cloned.1.call-start = ((), (), s32[]{:S(2)}) async-start(), calls=%async_computation.5 | async-start | bytes 3932160 | tf_op jit(solution)/shard_map/all_gather | solution.py:44
  158.9 33.6 %copy-start.2 = (bf16[64,8,2304]{2,1,0:T(8,128)(2,1)S(1)}, bf16[64,8,2304]{2,1,0:T(8,128)(2,1)}, u32[]{:S(2)}) copy-start(bf16[64,8,2304]{2,1,0:T(8,128)(2,1)} %broadcast_select_fusion) | copy-start | bytes 7077892
  238.0 107.4 %all-to-all-start.2 = ((bf16[64,8,4352]{2,1,0:T(8,128)(2,1)}), bf16[64,8,4352]{2,1,0:T(8,128)(2,1)}, u32[]{:S(2)}, u32[]{:S(2)}) async-start(bf16[64,8,4352]{2,1,0:T(8,128)(2,1)} %pad_maximum_fusion.1), calls=%async_computation.2 | async-start | bytes 8912896 | tf_op jit(solution)/shard_map/all_to_all | solution.py:62
  243.9 10.2 %copy-start.7 = (bf16[1,768,2048]{2,1,0:T(8,128)(2,1)S(1)}, bf16[1,768,2048]{2,1,0:T(8,128)(2,1)}, u32[]{:S(2)}) copy-start(bf16[1,768,2048]{2,1,0:T(8,128)(2,1)} %all-gather.5.cloned.1.call-done) | copy-start | bytes 9437188
  345.4 6.2 %copy-start.4 = (f32[128,8]{0,1:T(8,128)S(1)}, f32[128,8]{0,1:T(8,128)}, u32[]{:S(2)}) copy-start(f32[128,8]{0,1:T(8,128)} %param.8) | copy-start | bytes 12292
  345.4 102.1 %all-to-all-start.3 = ((bf16[64,16,2048]{2,1,0:T(8,128)(2,1)}), bf16[64,16,2048]{2,1,0:T(8,128)(2,1)}, u32[]{:S(2)}, u32[]{:S(2)}) async-start(bf16[64,16,2048]{2,1,0:T(8,128)(2,1)} %bitcast.66), calls=%async_computation.3 | async-start | bytes 8388608 | tf_op jit(solution)/shard_map/all_to_all | solution.py:62
  367.3 80.2 %copy-start.3 = (bf16[128,1024]{0,1:T(8,128)(2,1)S(1)}, bf16[128,1024]{0,1:T(8,128)(2,1)}, u32[]{:S(2)}) copy-start(bf16[128,1024]{0,1:T(8,128)(2,1)} %get-tuple-element.18) | copy-start | bytes 786436
  447.5 4.6 %copy-start.1 = (bf16[128,2048]{1,0:T(8,128)(2,1)S(1)}, bf16[128,2048]{1,0:T(8,128)(2,1)}, u32[]{:S(2)}) copy-start(bf16[128,2048]{1,0:T(8,128)(2,1)} %param.6) | copy-start | bytes 1572868
Sparse Core Ops, SparseCore 0:
  37.1 69.1 all-gather.2
  144.7 43.0 all-gather.4

commit v5 on v4

--- a/solution.py
+++ b/solution.py
@@ -23,12 +23,16 @@
     before = jnp.dot(earlier, token_hot, preferred_element_type=jnp.float32)
     slot_of = jnp.sum(before[:, None, :] * choice, axis=2).astype(jnp.int32)
     flat_index = old_ids * capacity + slot_of
-    slot_numbers = jnp.arange(slots, dtype=jnp.int32)
-    hits = flat_index.T[None, :, :] == slot_numbers[:, None, None]
-    pick = jnp.any(hits, axis=1).astype(jnp.bfloat16).reshape(experts, capacity, tok_dev)
     head = 8 if capacity > 8 else capacity
-    first_pick = pick[:, :head].reshape(-1, tok_dev)
-    second_pick = pick[:, head:].reshape(-1, tok_dev)
+    slot_numbers = (
+        numbers[:, None] * capacity + jnp.arange(capacity, dtype=jnp.int32)[None, :]
+    )
+    first_numbers = slot_numbers[:, :head].reshape(-1)
+    second_numbers = slot_numbers[:, head:].reshape(-1)
+    first_hits = flat_index.T[None, :, :] == first_numbers[:, None, None]
+    second_hits = flat_index.T[None, :, :] == second_numbers[:, None, None]
+    first_pick = jnp.any(first_hits, axis=1).astype(jnp.bfloat16)
+    second_pick = jnp.any(second_hits, axis=1).astype(jnp.bfloat16)
 
     def select_rows(chosen):
         rows = jnp.dot(chosen, tokens, preferred_element_type=jnp.float32).astype(jnp.bfloat16)
@@ -81,22 +85,19 @@
     placed_down = placed_chunks[:, :, gate_width:chunk_width].reshape(w_down.shape)
 
     gates = gate_probs / jnp.sum(gate_probs, axis=1, keepdims=True)
-    weights = jnp.sum(jnp.where(hits, gates.T[None, :, :], 0.0), axis=1)
-    weights = weights.reshape(experts, capacity, tok_dev)
 
-    def mix(part, returned):
-        part = part.reshape(-1, tok_dev).T
-        part_hi = part.astype(jnp.bfloat16)
-        part_lo = (part - part_hi.astype(jnp.float32)).astype(jnp.bfloat16)
+    def mix(hits, returned):
+        part = jnp.sum(jnp.where(hits, gates.T[None, :, :], 0.0), axis=1).T
+        rounded = lax.reduce_precision(part, exponent_bits=8, mantissa_bits=7)
+        part_hi = rounded.astype(jnp.bfloat16)
+        part_lo = (part - rounded).astype(jnp.bfloat16)
         flat = returned.reshape(-1, model_width)
         both = jnp.dot(
             jnp.concatenate([part_hi, part_lo], axis=0), flat, preferred_element_type=jnp.float32
         )
         return both[:tok_dev] + both[tok_dev:]
 
-    mixed_rows = mix(weights[:, :head], first_ret[:, :, :model_width]) + mix(
-        weights[:, head:], second_ret
-    )
+    mixed_rows = mix(first_hits, first_ret[:, :, :model_width]) + mix(second_hits, second_ret)
     return (mixed_rows.astype(jnp.bfloat16), placed_gate_up, placed_down)
 
 

time: 460 us -> 457 us (level)
  waiting for transfers between devices: 335 us -> 328 us
    all_to_all x4, waiting for transfers between devices: 305 us -> 298 us  [exchange(): lax.all_to_all(block, 'expert', split_axis=0, concat_axis=0, tiled=True)]
  transfers between devices with their start and end apart: 6 -> 6, of which waited for: 5 -> 5; matrix products, arithmetic and copies ran while one was open for 13% -> 14% of each run, Pallas kernels for 0% -> 0%
where the time goes in v5:
time: 457 us; the launch traced here: 456 us
  waiting for transfers between devices  328 us (72%)
  matrix products  38.4 us (8%)
  starting transfers between devices  31.8 us (7%)
  other arithmetic  26.2 us (6%)
  local copies, waits for them, and re-layouts  17.5 us (4%)
  between operations  14.3 us (3%)
    all_to_all x4, waiting for transfers between devices, exchange(): lax.all_to_all(block, 'expert', split_axis=0, concat_axis=0, tiled=True)  298 us
    all_to_all x4, starting transfers between devices, exchange(): lax.all_to_all(block, 'expert', split_axis=0, concat_axis=0, tiled=True)  31.5 us
    all_gather x1, waiting for transfers between devices, per_device(): lax.all_gather(w_down, 'dp', axis=1, tiled=True)  28.9 us
    dot_general x2, matrix products, expert_block(): lax.dot_general(row_block, gate_up_full, (((1,), (1,)), ((), ())), prefer...  18.8 us
    dot_general x2, matrix products, expert_block(): jnp.dot(hidden, down_full, preferred_element_type=jnp.float32)  9.73 us
  transfers between devices with their start and end apart: 6, of which 5 were waited for; matrix products, arithmetic and copies ran while one was open for 14% of the time, Pallas kernels for 0%

profile of v5, /device:TPU:1, one launch (start us, length us, event | category | flops | bytes accessed | tf_op | source)
XLA Modules:
  0.0 456.5 jit_solution(1663335056767992885)
XLA Ops:
  7.2 0.0 copy-start
  7.2 0.0 copy-start.5
  7.2 0.0 copy-start.6
  7.2 2.1 reshape.83
  9.3 2.9 reshape.82
  12.2 0.0 copy-done.5
  12.2 0.0 copy-done.6
  12.2 0.1 select_reduce_fusion.1
  12.4 0.1 fusion.35
  12.5 0.1 select_reduce_fusion
  12.6 0.1 iota_add_fusion
  12.6 0.1 eq.73
  12.7 2.9 compare_reduce_fusion.1
  15.7 0.0 copy-done
  15.7 0.7 fusion.8
  16.4 2.3 pad_maximum_fusion
  18.7 13.3 %all-to-all-start = ((bf16[64,8,4352]{2,1,0:T(8,128)(2,1)}), bf16[64,8,4352]{2,1,0:T(8,128)(2,1)}, u32[]{:S(2)}, u32[]{:S(2)}) async-start(bf16[64,8,4352]{2,1,0:T(8,128)(2,1)} %pad_maximum_fusion), calls=%async_computation | async-start | bytes 8912896 | tf_op jit(solution)/shard_map/all_to_all | solution.py:66
  32.0 0.0 all-gather.3.cloned.1.call-start
  32.0 0.7 all-gather.3.cloned.1.call-update
  32.7 0.1 slice.66
  32.8 0.1 eq.77
  32.9 5.8 %compare_reduce_fusion = pred[1024,128]{1,0:T(8,128)(4,1)S(1)} fusion(s32[8,128]{1,0:T(8,128)S(1)} %add_bitcast_fusion, s32[1024]{0:T(1024)S(1)} %eq.77), kind=kLoop, calls=%fused_computation.2 | loop fusion | flops 1966080 | bytes 139264 | tf_op jit(solution)/shard_map/reduce_or | solution.py:35
  38.7 3.2 convolution_convert_fusion.1
  41.9 91.6 %all-to-all-done = bf16[64,8,4352]{2,1,0:T(8,128)(2,1)} async-done(((bf16[64,8,4352]{2,1,0:T(8,128)(2,1)}), bf16[64,8,4352]{2,1,0:T(8,128)(2,1)}, u32[]{:S(2)}, u32[]{:S(2)}) %all-to-all-start) | async-done | bytes 4456480 | tf_op jit(solution)/shard_map/all_to_all | solution.py:66
  133.5 6.1 %all-to-all-start.1 = ((bf16[64,16,2048]{2,1,0:T(8,128)(2,1)}), bf16[64,16,2048]{2,1,0:T(8,128)(2,1)}, u32[]{:S(2)}, u32[]{:S(2)}) async-start(bf16[64,16,2048]{2,1,0:T(8,128)(2,1)} %bitcast.50), calls=%async_computation.1 | async-start | bytes 8388608 | tf_op jit(solution)/shard_map/all_to_all | solution.py:66
  139.6 0.2 all-gather.5.cloned.1.call-start
  139.8 0.5 all-gather.5.cloned.1.call-update
  140.4 0.1 select_reduce_fusion.2
  140.5 3.2 slice.53
  143.7 2.4 gather_fusion
  146.1 1.7 broadcast_select_fusion
  147.8 0.0 all-gather.3.cloned.1.call-done
  147.8 8.6 %fusion.15 = f32[512,1536]{1,0:T(8,128)} fusion(bf16[1536,2048]{1,0:T(8,128)(2,1)} %bitcast.53, bf16[64,8,4352]{2,1,0:T(8,128)(2,1)} %all-to-all-done), kind=kOutput, calls=%fused_computation.23 | convolution fusion | flops 3221225472 | bytes 11534336 | tf_op jit(solution)/shard_map/dot_general | solution.py:56
  156.4 0.0 copy-start.2
  156.4 28.9 %all-gather.5.cloned.1.call-done = bf16[1,768,2048]{2,1,0:T(8,128)(2,1)} async-done(((bf16[1,192,2048]{2,1,0:T(8,128)(2,1)}), bf16[1,768,2048]{2,1,0:T(8,128)(2,1)}) %all-gather.5.cloned.1.call-update) | async-done | bytes 3145744 | tf_op jit(solution)/shard_map/all_gather | solution.py:48
  185.3 4.7 %fusion.9 = bf16[64,8,2048]{2,1,0:T(8,128)(2,1)S(1)} fusion(bf16[1,768,2048]{2,1,0:T(8,128)(2,1)} %all-gather.5.cloned.1.call-done, f32[512,1536]{1,0:T(8,128)} %fusion.15), kind=kOutput, calls=%fused_computation.16 | convolution fusion | flops 1614020608 | bytes 8388608 | tf_op jit(solution)/shard_map/dot_general | solution.py:62
  190.0 0.0 copy-done.2
  190.0 2.4 pad_maximum_fusion.1
  192.4 43.1 %all-to-all-done.1 = bf16[64,16,2048]{2,1,0:T(8,128)(2,1)} async-done(((bf16[64,16,2048]{2,1,0:T(8,128)(2,1)}), bf16[64,16,2048]{2,1,0:T(8,128)(2,1)}, u32[]{:S(2)}, u32[]{:S(2)}) %all-to-all-start.1) | async-done | bytes 4194336 | tf_op jit(solution)/shard_map/all_to_all | solution.py:66
  235.5 5.9 %all-to-all-start.2 = ((bf16[64,8,4352]{2,1,0:T(8,128)(2,1)}), bf16[64,8,4352]{2,1,0:T(8,128)(2,1)}, u32[]{:S(2)}, u32[]{:S(2)}) async-start(bf16[64,8,4352]{2,1,0:T(8,128)(2,1)} %pad_maximum_fusion.1), calls=%async_computation.2 | async-start | bytes 8912896 | tf_op jit(solution)/shard_map/all_to_all | solution.py:66
  241.4 0.0 copy-start.7
  241.4 10.2 %fusion.41 = f32[1024,1536]{1,0:T(8,128)S(1)} fusion(bf16[1024,2048]{1,0:T(8,128)(2,1)} %bitcast.11, bf16[1536,2048]{1,0:T(8,128)(2,1)} %bitcast.54), kind=kOutput, calls=%fused_computation.69 | convolution fusion | flops 6442450944 | bytes 16777216 | tf_op jit(solution)/shard_map/dot_general | solution.py:56
  251.6 0.0 copy-done.7
  251.6 5.1 %convolution_convert_fusion = bf16[1024,2048]{1,0:T(8,128)(2,1)} fusion(bf16[1,768,2048]{2,1,0:T(8,128)(2,1)S(1)} %copy-done.7, f32[1024,1536]{1,0:T(8,128)S(1)} %fusion.41), kind=kOutput, calls=%fused_computation.6 | convolution fusion | flops 3228041216 | bytes 13631488 | tf_op jit(solution)/shard_map/dot_general | solution.py:62
  256.7 86.2 %all-to-all-done.2 = bf16[64,8,4352]{2,1,0:T(8,128)(2,1)} async-done(((bf16[64,8,4352]{2,1,0:T(8,128)(2,1)}), bf16[64,8,4352]{2,1,0:T(8,128)(2,1)}, u32[]{:S(2)}, u32[]{:S(2)}) %all-to-all-start.2) | async-done | bytes 4456480 | tf_op jit(solution)/shard_map/all_to_all | solution.py:66
  342.9 0.0 copy-start.4
  342.9 6.2 %all-to-all-start.3 = ((bf16[64,16,2048]{2,1,0:T(8,128)(2,1)}), bf16[64,16,2048]{2,1,0:T(8,128)(2,1)}, u32[]{:S(2)}, u32[]{:S(2)}) async-start(bf16[64,16,2048]{2,1,0:T(8,128)(2,1)} %bitcast.51), calls=%async_computation.3 | async-start | bytes 8388608 | tf_op jit(solution)/shard_map/all_to_all | solution.py:66
  349.2 0.0 copy-done.4
  349.2 2.9 fusion.12
  352.1 5.8 %fusion = f32[1024,128]{1,0:T(8,128)S(1)} fusion(f32[8,128]{1,0:T(8,128)S(1)} %divide_bitcast_fusion, s32[8,128]{1,0:T(8,128)S(1)} %add_bitcast_fusion, s32[1024]{0:T(1024)S(1)} %eq.77), kind=kLoop, calls=%fused_computation.5 | loop fusion | flops 3014656 | bytes 536576 | tf_op jit(solution)/shard_map/reduce_sum | solution.py:90
  357.9 0.8 reduce-precision_convert_fusion
  358.7 1.5 slice.61
  360.2 1.2 slice.62
  361.4 2.2 reshape.93
  363.6 1.8 reshape.94
  365.4 0.0 copy-start.3
  365.4 2.4 fusion.13
  367.7 77.3 %all-to-all-done.3 = bf16[64,16,2048]{2,1,0:T(8,128)(2,1)} async-done(((bf16[64,16,2048]{2,1,0:T(8,128)(2,1)}), bf16[64,16,2048]{2,1,0:T(8,128)(2,1)}, u32[]{:S(2)}, u32[]{:S(2)}) %all-to-all-start.3) | async-done | bytes 4194336 | tf_op jit(solution)/shard_map/all_to_all | solution.py:66
  445.0 0.0 copy-done.3
  445.0 0.0 copy-start.1
  445.0 3.5 fusion.27
  448.6 1.1 fusion.23
  449.6 0.0 copy-done.1
  (9 shorter events, 0.1 us)
Async XLA Ops:
  7.2 8.5 %copy-start = (bf16[128,2048]{1,0:T(8,128)(2,1)S(1)}, bf16[128,2048]{1,0:T(8,128)(2,1)}, u32[]{:S(2)}) copy-start(bf16[128,2048]{1,0:T(8,128)(2,1)} %param.6) | copy-start | bytes 1572868
  7.2 5.0 %copy-start.5 = (s32[128,8]{0,1:T(8,128)S(1)}, s32[128,8]{0,1:T(8,128)}, u32[]{:S(2)}) copy-start(s32[128,8]{0,1:T(8,128)} %param.7) | copy-start | bytes 12292
  7.2 5.0 %copy-start.6 = (s32[64]{0:T(128)S(1)}, s32[64]{0:T(128)}, u32[]{:S(2)}) copy-start(s32[64]{0:T(128)} %param.9) | copy-start | bytes 772
  18.7 114.9 %all-to-all-start = ((bf16[64,8,4352]{2,1,0:T(8,128)(2,1)}), bf16[64,8,4352]{2,1,0:T(8,128)(2,1)}, u32[]{:S(2)}, u32[]{:S(2)}) async-start(bf16[64,8,4352]{2,1,0:T(8,128)(2,1)} %pad_maximum_fusion), calls=%async_computation | async-start | bytes 8912896 | tf_op jit(solution)/shard_map/all_to_all | solution.py:66
  32.0 115.8 %all-gather.3.cloned.1.call-start = ((), (), s32[]{:S(2)}) async-start(), calls=%async_computation.4 | async-start | bytes 7864320 | tf_op jit(solution)/shard_map/all_gather | solution.py:47
  133.5 102.0 %all-to-all-start.1 = ((bf16[64,16,2048]{2,1,0:T(8,128)(2,1)}), bf16[64,16,2048]{2,1,0:T(8,128)(2,1)}, u32[]{:S(2)}, u32[]{:S(2)}) async-start(bf16[64,16,2048]{2,1,0:T(8,128)(2,1)} %bitcast.50), calls=%async_computation.1 | async-start | bytes 8388608 | tf_op jit(solution)/shard_map/all_to_all | solution.py:66
  139.6 45.7 %all-gather.5.cloned.1.call-start = ((), (), s32[]{:S(2)}) async-start(), calls=%async_computation.5 | async-start | bytes 3932160 | tf_op jit(solution)/shard_map/all_gather | solution.py:48
  156.4 33.6 %copy-start.2 = (bf16[64,8,2304]{2,1,0:T(8,128)(2,1)S(1)}, bf16[64,8,2304]{2,1,0:T(8,128)(2,1)}, u32[]{:S(2)}) copy-start(bf16[64,8,2304]{2,1,0:T(8,128)(2,1)} %broadcast_select_fusion) | copy-start | bytes 7077892
  235.5 107.4 %all-to-all-start.2 = ((bf16[64,8,4352]{2,1,0:T(8,128)(2,1)}), bf16[64,8,4352]{2,1,0:T(8,128)(2,1)}, u32[]{:S(2)}, u32[]{:S(2)}) async-start(bf16[64,8,4352]{2,1,0:T(8,128)(2,1)} %pad_maximum_fusion.1), calls=%async_computation.2 | async-start | bytes 8912896 | tf_op jit(solution)/shard_map/all_to_all | solution.py:66
  241.4 10.2 %copy-start.7 = (bf16[1,768,2048]{2,1,0:T(8,128)(2,1)S(1)}, bf16[1,768,2048]{2,1,0:T(8,128)(2,1)}, u32[]{:S(2)}) copy-start(bf16[1,768,2048]{2,1,0:T(8,128)(2,1)} %all-gather.5.cloned.1.call-done) | copy-start | bytes 9437188
  342.9 6.2 %copy-start.4 = (f32[128,8]{0,1:T(8,128)S(1)}, f32[128,8]{0,1:T(8,128)}, u32[]{:S(2)}) copy-start(f32[128,8]{0,1:T(8,128)} %param.8) | copy-start | bytes 12292
  342.9 102.1 %all-to-all-start.3 = ((bf16[64,16,2048]{2,1,0:T(8,128)(2,1)}), bf16[64,16,2048]{2,1,0:T(8,128)(2,1)}, u32[]{:S(2)}, u32[]{:S(2)}) async-start(bf16[64,16,2048]{2,1,0:T(8,128)(2,1)} %bitcast.51), calls=%async_computation.3 | async-start | bytes 8388608 | tf_op jit(solution)/shard_map/all_to_all | solution.py:66
  365.4 79.7 %copy-start.3 = (bf16[128,1024]{0,1:T(8,128)(2,1)S(1)}, bf16[128,1024]{0,1:T(8,128)(2,1)}, u32[]{:S(2)}) copy-start(bf16[128,1024]{0,1:T(8,128)(2,1)} %get-tuple-element.16) | copy-start | bytes 786436
  445.0 4.6 %copy-start.1 = (bf16[128,2048]{1,0:T(8,128)(2,1)S(1)}, bf16[128,2048]{1,0:T(8,128)(2,1)}, u32[]{:S(2)}) copy-start(bf16[128,2048]{1,0:T(8,128)(2,1)} %param.6) | copy-start | bytes 1572868
Sparse Core Ops, SparseCore 0:
  34.6 69.1 all-gather.2
  142.2 43.0 all-gather.4

commit v6 on v5

--- a/solution.py
+++ b/solution.py
@@ -43,13 +43,21 @@
     gate_width = gate_rows.shape[2]
     chunk_width = gate_width + down_rows.shape[2]
 
-    gathered = (
-        lax.all_gather(w_gate_up, "dp", axis=2, tiled=True),
-        lax.all_gather(w_down, "dp", axis=1, tiled=True),
+    ring = lax.psum(1, "dp")
+    own = jnp.concatenate(
+        [w_gate_up.reshape(-1, model_width), w_down.reshape(-1, model_width)], axis=0
     )
-    hidden_count = gathered[0].shape[2]
-    gate_up_full = gathered[0].reshape(2 * hidden_count, model_width)
-    down_full = gathered[1].reshape(hidden_count, model_width)
+    parts = [own] + [
+        lax.ppermute(own, "dp", [(j, (j + shift) % ring) for j in range(ring)])
+        for shift in range(1, ring)
+    ]
+    local_count = w_down.shape[1]
+    hidden_count = local_count * ring
+    gate_up_full = jnp.concatenate(
+        [part[:local_count] for part in parts] + [part[local_count:2 * local_count] for part in parts],
+        axis=0,
+    )
+    down_full = jnp.concatenate([part[2 * local_count:] for part in parts], axis=0)
 
     def expert_block(rows):
         row_block = rows.reshape(-1, model_width)

time: 457 us -> 445 us (0.974)
  waiting for transfers between devices: 328 us -> 313 us
  local copies, waits for them, and re-layouts: 17.5 us -> 31.4 us
  between operations: 14.3 us -> 0.99 us
  starting transfers between devices: 31.8 us -> 38.2 us
  matrix products: 38.4 us -> 33.5 us
    ppermute x0 -> x3, waiting for transfers between devices: none -> 45.1 us  [per_device(): lax.ppermute(own, 'dp', [(j, (j + shift) % ring) for j in range(ring)])]
    all_to_all x4, waiting for transfers between devices: 298 us -> 268 us  [exchange(): lax.all_to_all(block, 'expert', split_axis=0, concat_axis=0, tiled=True)]
    all_gather x2 -> x0, waiting for transfers between devices: 28.9 us -> none  [the longest x1 28.9 us: per_device(): lax.all_gather(w_down, 'dp', axis=1, tiled=True)]
    unnamed x16 -> x33, local copies, waits for them, and re-layouts: 0.04 us -> 7.19 us
    slice x0 -> x3, local copies, waits for them, and re-layouts: none -> 6.75 us  [per_device(): part[2 * local_count:]]
    ppermute x0 -> x3, starting transfers between devices: none -> 6.4 us  [per_device(): lax.ppermute(own, 'dp', [(j, (j + shift) % ring) for j in range(ring)])]
  transfers between devices with their start and end apart: 6 -> 7, of which waited for: 5 -> 5; matrix products, arithmetic and copies ran while one was open for 14% -> 17% of each run, Pallas kernels for 0% -> 0%
where the time goes in v6:
time: 445 us; the launch traced here: 444 us
  waiting for transfers between devices  313 us (70%)
  starting transfers between devices  38.2 us (9%)
  matrix products  33.5 us (8%)
  local copies, waits for them, and re-layouts  31.4 us (7%)
  other arithmetic  27.1 us (6%)
    all_to_all x4, waiting for transfers between devices, exchange(): lax.all_to_all(block, 'expert', split_axis=0, concat_axis=0, tiled=True)  268 us
    ppermute x3, waiting for transfers between devices, per_device(): lax.ppermute(own, 'dp', [(j, (j + shift) % ring) for j in range(ring)])  45.1 us
    all_to_all x4, starting transfers between devices, exchange(): lax.all_to_all(block, 'expert', split_axis=0, concat_axis=0, tiled=True)  31.8 us
    dot_general x2, matrix products, expert_block(): lax.dot_general(row_block, gate_up_full, (((1,), (1,)), ((), ())), prefer...  16.6 us
  transfers between devices with their start and end apart: 7, of which 5 were waited for; matrix products, arithmetic and copies ran while one was open for 17% of the time, Pallas kernels for 0%

profile of v6, /device:TPU:1, one launch (start us, length us, event | category | flops | bytes accessed | tf_op | source)
XLA Modules:
  0.0 444.1 jit_solution(13224778345309828987)
XLA Ops:
  0.6 0.0 copy-start
  0.7 0.8 select_reduce_fusion.1
  1.5 0.1 fusion.27
  1.7 0.1 select_reduce_fusion
  1.8 0.1 iota_add_fusion
  1.8 0.1 eq.73
  1.9 2.9 reshape.84
  4.8 2.0 reshape.85
  6.9 2.9 compare_reduce_fusion.1
  9.8 0.0 copy-done
  9.8 0.7 fusion.2
  10.5 2.3 pad_maximum_fusion
  12.8 13.5 %all-to-all-start = ((bf16[64,8,4352]{2,1,0:T(8,128)(2,1)}), bf16[64,8,4352]{2,1,0:T(8,128)(2,1)}, u32[]{:S(2)}, u32[]{:S(2)}) async-start(bf16[64,8,4352]{2,1,0:T(8,128)(2,1)} %pad_maximum_fusion), calls=%async_computation | async-start | bytes 8912896 | tf_op jit(solution)/shard_map/all_to_all | solution.py:74
  26.3 1.6 pad_maximum_fusion.3
  27.9 1.2 collective-permute-start
  29.1 2.5 collective-permute-start.1
  31.5 0.1 slice.118
  31.6 0.1 eq.77
  31.7 5.8 %compare_reduce_fusion = pred[1024,128]{1,0:T(8,128)(4,1)S(1)} fusion(s32[8,128]{1,0:T(8,128)S(1)} %add_bitcast_fusion, s32[1024]{0:T(1024)S(1)} %eq.77), kind=kLoop, calls=%fused_computation.2 | loop fusion | flops 1966080 | bytes 139264 | tf_op jit(solution)/shard_map/reduce_or | solution.py:35
  37.5 3.2 convolution_convert_fusion.1
  40.7 87.0 %all-to-all-done = bf16[64,8,4352]{2,1,0:T(8,128)(2,1)} async-done(((bf16[64,8,4352]{2,1,0:T(8,128)(2,1)}), bf16[64,8,4352]{2,1,0:T(8,128)(2,1)}, u32[]{:S(2)}, u32[]{:S(2)}) %all-to-all-start) | async-done | bytes 4456480 | tf_op jit(solution)/shard_map/all_to_all | solution.py:74
  127.8 6.2 %all-to-all-start.1 = ((bf16[64,16,2048]{2,1,0:T(8,128)(2,1)}), bf16[64,16,2048]{2,1,0:T(8,128)(2,1)}, u32[]{:S(2)}, u32[]{:S(2)}) async-start(bf16[64,16,2048]{2,1,0:T(8,128)(2,1)} %bitcast.46), calls=%async_computation.1 | async-start | bytes 8388608 | tf_op jit(solution)/shard_map/all_to_all | solution.py:74
  134.0 2.7 collective-permute-start.2
  136.7 0.1 select_reduce_fusion.2
  136.8 0.9 bitcast_dynamic-update-slice_fusion.1
  137.8 0.0 collective-permute-done
  137.8 2.1 slice_dynamic-update-slice_fusion.5
  139.9 0.0 collective-permute-done.1
  139.9 2.1 slice_dynamic-update-slice_fusion.4
  142.0 45.1 %collective-permute-done.2 = bf16[576,2048]{1,0:T(8,128)(2,1)S(1)} collective-permute-done((bf16[576,2048]{1,0:T(8,128)(2,1)}, bf16[576,2048]{1,0:T(8,128)(2,1)S(1)}, u32[]{:S(2)}, u32[]{:S(2)}) %collective-permute-start.2) | collective-permute-done | bytes 2359328 | tf_op jit(solution)/shard_map/ppermute | solution.py:51
  187.1 1.0 slice_dynamic-update-slice_fusion.3
  188.1 1.0 bitcast_dynamic-update-slice_fusion
  189.0 2.7 fusion.35
  191.8 2.7 fusion.36
  194.5 1.3 fusion.37
  195.8 3.3 slice.105
  199.0 2.4 gather_fusion
  201.4 0.0 copy-start.4
  201.4 0.0 copy-start.6
  201.4 0.0 copy-start.8
  201.5 6.4 %fusion.7 = f32[512,1536]{1,0:T(8,128)S(1)} fusion(bf16[1536,2048]{1,0:T(8,128)(2,1)} %get-tuple-element.20, bf16[64,8,4352]{2,1,0:T(8,128)(2,1)} %all-to-all-done), kind=kOutput, calls=%fused_computation.22 | convolution fusion | flops 3221225472 | bytes 11534336 | tf_op jit(solution)/shard_map/dot_general | solution.py:64
  207.9 1.8 fusion.3
  209.8 0.3 broadcast_select_fusion
  210.1 2.4 pad_maximum_fusion.1
  212.4 17.4 %all-to-all-done.1 = bf16[64,16,2048]{2,1,0:T(8,128)(2,1)} async-done(((bf16[64,16,2048]{2,1,0:T(8,128)(2,1)}), bf16[64,16,2048]{2,1,0:T(8,128)(2,1)}, u32[]{:S(2)}, u32[]{:S(2)}) %all-to-all-start.1) | async-done | bytes 4194336 | tf_op jit(solution)/shard_map/all_to_all | solution.py:74
  229.9 5.9 %all-to-all-start.2 = ((bf16[64,8,4352]{2,1,0:T(8,128)(2,1)}), bf16[64,8,4352]{2,1,0:T(8,128)(2,1)}, u32[]{:S(2)}, u32[]{:S(2)}) async-start(bf16[64,8,4352]{2,1,0:T(8,128)(2,1)} %pad_maximum_fusion.1), calls=%async_computation.2 | async-start | bytes 8912896 | tf_op jit(solution)/shard_map/all_to_all | solution.py:74
  235.8 0.0 copy-start.5
  235.8 0.0 copy-start.7
  235.8 0.0 copy-start.9
  235.8 10.2 %fusion.38 = f32[1024,1536]{1,0:T(8,128)S(1)} fusion(bf16[1024,2048]{1,0:T(8,128)(2,1)} %bitcast.13, bf16[1536,2048]{1,0:T(8,128)(2,1)} %get-tuple-element.20), kind=kOutput, calls=%fused_computation.81 | convolution fusion | flops 6442450944 | bytes 16777216 | tf_op jit(solution)/shard_map/dot_general | solution.py:64
  246.1 5.1 %convolution_convert_fusion = bf16[1024,2048]{1,0:T(8,128)(2,1)} fusion(f32[1024,1536]{1,0:T(8,128)S(1)} %fusion.38, bf16[192,2048]{1,0:T(8,128)(2,1)S(1)} %copy-done.11, bf16[192,2048]{1,0:T(8,128)(2,1)S(1)} %copy-done.9, bf16[192,2048]{1,0:T(8,128)(2,1)S(1)} %copy-done.7, bf16[192,2048]{1,0:T(8,128)(2,1)S(1)} %bitcast.51), kind=kOutput, calls=%fused_computation.6 | convolution fusion | flops 3240624128 | bytes 13631488 | tf_op jit(solution)/shard_map/dot_general | solution.py:70
  251.2 86.1 %all-to-all-done.2 = bf16[64,8,4352]{2,1,0:T(8,128)(2,1)} async-done(((bf16[64,8,4352]{2,1,0:T(8,128)(2,1)}), bf16[64,8,4352]{2,1,0:T(8,128)(2,1)}, u32[]{:S(2)}, u32[]{:S(2)}) %all-to-all-start.2) | async-done | bytes 4456480 | tf_op jit(solution)/shard_map/all_to_all | solution.py:74
  337.3 6.2 %all-to-all-start.3 = ((bf16[64,16,2048]{2,1,0:T(8,128)(2,1)}), bf16[64,16,2048]{2,1,0:T(8,128)(2,1)}, u32[]{:S(2)}, u32[]{:S(2)}) async-start(bf16[64,16,2048]{2,1,0:T(8,128)(2,1)} %bitcast.48), calls=%async_computation.3 | async-start | bytes 8388608 | tf_op jit(solution)/shard_map/all_to_all | solution.py:74
  343.6 2.9 fusion.4
  346.5 5.8 %fusion = f32[1024,128]{1,0:T(8,128)S(1)} fusion(f32[8,128]{1,0:T(8,128)S(1)} %divide_bitcast_fusion, s32[8,128]{1,0:T(8,128)S(1)} %add_bitcast_fusion, s32[1024]{0:T(1024)S(1)} %eq.77), kind=kLoop, calls=%fused_computation.5 | loop fusion | flops 3014656 | bytes 536576 | tf_op jit(solution)/shard_map/reduce_sum | solution.py:98
  352.3 0.8 reduce-precision_convert_fusion
  353.1 1.5 slice.113
  354.6 1.2 slice.114
  355.8 2.2 reshape.95
  358.0 1.8 reshape.96
  359.8 2.3 fusion.5
  362.1 77.3 %all-to-all-done.3 = bf16[64,16,2048]{2,1,0:T(8,128)(2,1)} async-done(((bf16[64,16,2048]{2,1,0:T(8,128)(2,1)}), bf16[64,16,2048]{2,1,0:T(8,128)(2,1)}, u32[]{:S(2)}, u32[]{:S(2)}) %all-to-all-start.3) | async-done | bytes 4194336 | tf_op jit(solution)/shard_map/all_to_all | solution.py:74
  439.4 3.6 fusion.19
  443.0 1.1 fusion.15
  (29 shorter events, 0.2 us)
Async XLA Ops:
  0.6 9.2 %copy-start = (bf16[128,2048]{1,0:T(8,128)(2,1)S(1)}, bf16[128,2048]{1,0:T(8,128)(2,1)}, u32[]{:S(2)}) copy-start(bf16[128,2048]{1,0:T(8,128)(2,1)} %param.6) | copy-start | bytes 1572868
  12.8 13.5 %copy-start.2 = (bf16[1,2,192,2048]{3,2,1,0:T(8,128)(2,1)S(1)}, bf16[1,2,192,2048]{3,2,1,0:T(8,128)(2,1)}, u32[]{:S(2)}) copy-start(bf16[1,2,192,2048]{3,2,1,0:T(8,128)(2,1)} %param.10) | copy-start | bytes 4718596
  12.8 13.5 %copy-start.3 = (bf16[1,192,2048]{2,1,0:T(8,128)(2,1)S(1)}, bf16[1,192,2048]{2,1,0:T(8,128)(2,1)}, u32[]{:S(2)}) copy-start(bf16[1,192,2048]{2,1,0:T(8,128)(2,1)} %param.11) | copy-start | bytes 2359300
  12.8 115.0 %all-to-all-start = ((bf16[64,8,4352]{2,1,0:T(8,128)(2,1)}), bf16[64,8,4352]{2,1,0:T(8,128)(2,1)}, u32[]{:S(2)}, u32[]{:S(2)}) async-start(bf16[64,8,4352]{2,1,0:T(8,128)(2,1)} %pad_maximum_fusion), calls=%async_computation | async-start | bytes 8912896 | tf_op jit(solution)/shard_map/all_to_all | solution.py:74
  27.9 109.9 %collective-permute-start = (bf16[576,2048]{1,0:T(8,128)(2,1)}, bf16[576,2048]{1,0:T(8,128)(2,1)}, u32[]{:S(2)}, u32[]{:S(2)}) collective-permute-start(bf16[576,2048]{1,0:T(8,128)(2,1)} %pad_maximum_fusion.3), channel_id=1, source_target_pairs={{0,64},{64,128},{128,192},{192,0},{1,65},{65,129},{129,193},{193,1... | collective-permute-start | bytes 7077896 | tf_op jit(solution)/shard_map/ppermute | solution.py:51
  29.1 110.8 %collective-permute-start.1 = (bf16[576,2048]{1,0:T(8,128)(2,1)}, bf16[576,2048]{1,0:T(8,128)(2,1)}, u32[]{:S(2)}, u32[]{:S(2)}) collective-permute-start(bf16[576,2048]{1,0:T(8,128)(2,1)} %pad_maximum_fusion.3), channel_id=1, source_target_pairs={{0,128},{64,192},{128,0},{192,64},{1,129},{65,193},{129,1},{193,65... | collective-permute-start | bytes 7077896 | tf_op jit(solution)/shard_map/ppermute | solution.py:51
  127.8 9.0 %copy-start.13 = (s32[64]{0:T(128)S(1)}, s32[64]{0:T(128)}, u32[]{:S(2)}) copy-start(s32[64]{0:T(128)} %param.9) | copy-start | bytes 772
  127.8 102.1 %all-to-all-start.1 = ((bf16[64,16,2048]{2,1,0:T(8,128)(2,1)}), bf16[64,16,2048]{2,1,0:T(8,128)(2,1)}, u32[]{:S(2)}, u32[]{:S(2)}) async-start(bf16[64,16,2048]{2,1,0:T(8,128)(2,1)} %bitcast.46), calls=%async_computation.1 | async-start | bytes 8388608 | tf_op jit(solution)/shard_map/all_to_all | solution.py:74
  134.0 53.1 %collective-permute-start.2 = (bf16[576,2048]{1,0:T(8,128)(2,1)}, bf16[576,2048]{1,0:T(8,128)(2,1)S(1)}, u32[]{:S(2)}, u32[]{:S(2)}) collective-permute-start(bf16[576,2048]{1,0:T(8,128)(2,1)} %pad_maximum_fusion.3), channel_id=1, source_target_pairs={{0,192},{64,0},{128,64},{192,128},{1,193},{65,1},{129,65},{193,129... | collective-permute-start | bytes 7077896 | tf_op jit(solution)/shard_map/ppermute | solution.py:51
  201.4 6.5 %copy-start.4 = (bf16[1,192,2048]{2,1,0:T(8,128)(2,1)S(1)}, bf16[1,192,2048]{2,1,0:T(8,128)(2,1)}, u32[]{:S(2)}) copy-start(bf16[1,192,2048]{2,1,0:T(8,128)(2,1)} %param.11) | copy-start | bytes 2359300
  201.4 6.4 %copy-start.6 = (bf16[192,2048]{1,0:T(8,128)(2,1)S(1)}, bf16[192,2048]{1,0:T(8,128)(2,1)}, u32[]{:S(2)}) copy-start(bf16[192,2048]{1,0:T(8,128)(2,1)} %get-tuple-element.15) | copy-start | bytes 2359300
  201.4 6.4 %copy-start.8 = (bf16[192,2048]{1,0:T(8,128)(2,1)S(1)}, bf16[192,2048]{1,0:T(8,128)(2,1)}, u32[]{:S(2)}) copy-start(bf16[192,2048]{1,0:T(8,128)(2,1)} %get-tuple-element.17) | copy-start | bytes 2359300
  201.5 6.4 %copy-start.10 = (bf16[192,2048]{1,0:T(8,128)(2,1)S(1)}, bf16[192,2048]{1,0:T(8,128)(2,1)}, u32[]{:S(2)}) copy-start(bf16[192,2048]{1,0:T(8,128)(2,1)} %get-tuple-element.19) | copy-start | bytes 2359300
  229.9 107.4 %all-to-all-start.2 = ((bf16[64,8,4352]{2,1,0:T(8,128)(2,1)}), bf16[64,8,4352]{2,1,0:T(8,128)(2,1)}, u32[]{:S(2)}, u32[]{:S(2)}) async-start(bf16[64,8,4352]{2,1,0:T(8,128)(2,1)} %pad_maximum_fusion.1), calls=%async_computation.2 | async-start | bytes 8912896 | tf_op jit(solution)/shard_map/all_to_all | solution.py:74
  235.8 10.3 %copy-start.5 = (bf16[1,192,2048]{2,1,0:T(8,128)(2,1)S(1)}, bf16[1,192,2048]{2,1,0:T(8,128)(2,1)}, u32[]{:S(2)}) copy-start(bf16[1,192,2048]{2,1,0:T(8,128)(2,1)} %param.11) | copy-start | bytes 2359300
  235.8 10.3 %copy-start.7 = (bf16[192,2048]{1,0:T(8,128)(2,1)S(1)}, bf16[192,2048]{1,0:T(8,128)(2,1)}, u32[]{:S(2)}) copy-start(bf16[192,2048]{1,0:T(8,128)(2,1)} %get-tuple-element.15) | copy-start | bytes 2359300
  235.8 10.3 %copy-start.9 = (bf16[192,2048]{1,0:T(8,128)(2,1)S(1)}, bf16[192,2048]{1,0:T(8,128)(2,1)}, u32[]{:S(2)}) copy-start(bf16[192,2048]{1,0:T(8,128)(2,1)} %get-tuple-element.17) | copy-start | bytes 2359300
  235.8 10.3 %copy-start.11 = (bf16[192,2048]{1,0:T(8,128)(2,1)S(1)}, bf16[192,2048]{1,0:T(8,128)(2,1)}, u32[]{:S(2)}) copy-start(bf16[192,2048]{1,0:T(8,128)(2,1)} %get-tuple-element.19) | copy-start | bytes 2359300
  337.3 6.2 %copy-start.12 = (f32[128,8]{0,1:T(8,128)S(1)}, f32[128,8]{0,1:T(8,128)}, u32[]{:S(2)}) copy-start(f32[128,8]{0,1:T(8,128)} %param.8) | copy-start | bytes 12292
  337.3 102.1 %all-to-all-start.3 = ((bf16[64,16,2048]{2,1,0:T(8,128)(2,1)}), bf16[64,16,2048]{2,1,0:T(8,128)(2,1)}, u32[]{:S(2)}, u32[]{:S(2)}) async-start(bf16[64,16,2048]{2,1,0:T(8,128)(2,1)} %bitcast.48), calls=%async_computation.3 | async-start | bytes 8388608 | tf_op jit(solution)/shard_map/all_to_all | solution.py:74
  439.4 4.7 %copy-start.1 = (bf16[128,2048]{1,0:T(8,128)(2,1)S(1)}, bf16[128,2048]{1,0:T(8,128)(2,1)}, u32[]{:S(2)}) copy-start(bf16[128,2048]{1,0:T(8,128)(2,1)} %param.6) | copy-start | bytes 1572868

commit v7 on v3

v7 whole, which is shorter than its diff:
```python
import jax
import jax.numpy as jnp
from jax import lax
from jax.sharding import PartitionSpec as P


def per_device(tokens, expert_ids, gate_probs, placement, w_gate_up, w_down):
    tok_dev = tokens.shape[0]
    model_width = tokens.shape[1]
    top_count = expert_ids.shape[1]
    experts = placement.shape[0]
    capacity = min(tok_dev, 3 * tok_dev * top_count // (2 * experts))
    slots = experts * capacity
    numbers = jnp.arange(experts, dtype=jnp.int32)

    owner = (placement[None, None, :] == expert_ids[:, :, None]).astype(jnp.int32)
    old_ids = jnp.sum(owner * numbers[None, None, :], axis=2)
    choice = (old_ids[:, :, None] == numbers[None, None, :]).astype(jnp.float32)
    token_hot = jnp.sum(choice, axis=1)
    earlier = (
        jnp.arange(tok_dev, dtype=jnp.int32)[None, :] < jnp.arange(tok_dev, dtype=jnp.int32)[:, None]
    ).astype(jnp.float32)
    before = jnp.dot(earlier, token_hot, preferred_element_type=jnp.float32)
    slot_of = jnp.sum(before[:, None, :] * choice, axis=2).astype(jnp.int32)
    flat_index = old_ids * capacity + slot_of
    slot_numbers = jnp.arange(slots, dtype=jnp.int32)
    hits = flat_index.T[None, :, :] == slot_numbers[:, None, None]
    pick = jnp.any(hits, axis=1).astype(jnp.bfloat16)

    def exchange(block):
        return lax.all_to_all(block, "expert", split_axis=0, concat_axis=0, tiled=True)

    gate_rows = w_gate_up.reshape(-1, model_width)
    down_rows = w_down.reshape(-1, model_width)
    shard = jnp.concatenate([gate_rows, down_rows], axis=0)
    spread = exchange(shard.reshape(experts, capacity, -1))

    ring = lax.psum(1, "dp")
    parts = [shard] + [
        lax.ppermute(shard, "dp", [(j, (j + shift) % ring) for j in range(ring)])
        for shift in range(1, ring)
    ]
    local_count = w_down.shape[1]
    hidden_count = local_count * ring
    gate_up_full = jnp.concatenate(
        [part[:local_count] for part in parts] + [part[local_count:2 * local_count] for part in parts],
        axis=0,
    )
    down_full = jnp.concatenate([part[2 * local_count:] for part in parts], axis=0)

    buffer = jnp.dot(pick, tokens, preferred_element_type=jnp.float32).astype(jnp.bfloat16)
    buffer = buffer.reshape(experts, capacity, model_width)
    spread, buffer = lax.optimization_barrier((spread, buffer))
    received = exchange(buffer)

    inverse = jnp.sum(jnp.where(placement[:, None] == numbers[None, :], numbers[:, None], 0), axis=0)
    reordered = jnp.take(spread, inverse, axis=0, mode="clip")
    received, reordered = lax.optimization_barrier((received, reordered))
    placed_rows = exchange(reordered)

    row_block = received.reshape(-1, model_width)
    projected = lax.dot_general(
        row_block, gate_up_full, (((1,), (1,)), ((), ())), preferred_element_type=jnp.float32
    )
    gate_part = projected[:, :hidden_count]
    up_part = projected[:, hidden_count:]
    hidden = (jax.nn.silu(gate_part) * up_part).astype(jnp.bfloat16)
    result = jnp.dot(hidden, down_full, preferred_element_type=jnp.float32).astype(jnp.bfloat16)
    result = result.reshape(experts, capacity, model_width)
    placed_rows, result = lax.optimization_barrier((placed_rows, result))
    returned = exchange(result)

    placed_rows = placed_rows.reshape(-1, model_width)
    gate_count = gate_rows.shape[0]
    placed_gate_up = placed_rows[:gate_count].reshape(w_gate_up.shape)
    placed_down = placed_rows[gate_count:].reshape(w_down.shape)

    gates = gate_probs / jnp.sum(gate_probs, axis=1, keepdims=True)
    part = jnp.sum(jnp.where(hits, gates.T[None, :, :], 0.0), axis=1).T
    rounded = lax.reduce_precision(part, exponent_bits=8, mantissa_bits=7)
    part_hi = rounded.astype(jnp.bfloat16)
    part_lo = (part - rounded).astype(jnp.bfloat16)
    both = jnp.dot(
        jnp.concatenate([part_hi, part_lo], axis=0),
        returned.reshape(slots, model_width),
        preferred_element_type=jnp.float32,
    )
    mixed_rows = both[:tok_dev] + both[tok_dev:]
    return (mixed_rows.astype(jnp.bfloat16), placed_gate_up, placed_down)


def solution(mesh):
    in_specs = (
        P(("dp", "expert"), None),
        P(("dp", "expert"), None),
        P(("dp", "expert"), None),
        P(),
        P("expert", None, "dp", None),
        P("expert", "dp", None),
    )
    out_specs = (P(("dp", "expert"), None), P("expert", None, "dp", None), P("expert", "dp", None))
    return jax.shard_map(
        per_device, mesh=mesh, in_specs=in_specs, out_specs=out_specs, check_vma=False
    )
```

time: 494 us -> 439 us (0.89)
  waiting for transfers between devices: 373 us -> 320 us
  starting transfers between devices: 20 us -> 36.3 us
  between operations: 14.2 us -> 0.82 us
  other arithmetic: 27.5 us -> 17.6 us
  matrix products: 29.3 us -> 36 us
    all_to_all x2 -> x4, waiting for transfers between devices: 372 us -> 222 us  [exchange(): lax.all_to_all(block, 'expert', split_axis=0, concat_axis=0, tiled=True)]
    ppermute x0 -> x3, waiting for transfers between devices: none -> 97.3 us  [per_device(): lax.ppermute(shard, 'dp', [(j, (j + shift) % ring) for j in range(ring)])]
    slice x4 -> x0, local copies, waits for them, and re-layouts: 16.6 us -> none  [the longest x1 6.6 us: per_device(): row_block = arrived[:, :, :model_width].reshape(-1, model_width)]
    unnamed x14 -> x31, local copies, waits for them, and re-layouts: 0.04 us -> 12.6 us
    all_to_all x2 -> x4, starting transfers between devices: 19.7 us -> 31.4 us  [exchange(): lax.all_to_all(block, 'expert', split_axis=0, concat_axis=0, tiled=True)]
    concatenate x2 -> x0, other arithmetic: 7.47 us -> none  [the longest x1 3.74 us: per_device(): outgoing = jnp.concatenate([buffer, chunks], axis=2)]
  transfers between devices with their start and end apart: 4 -> 7, of which waited for: 2 -> 6; matrix products, arithmetic and copies ran while one was open for 8% -> 16% of each run, Pallas kernels for 0% -> 0%
where the time goes in v7:
time: 439 us; the launch traced here: 438 us
  waiting for transfers between devices  320 us (73%)
  starting transfers between devices  36.3 us (8%)
  matrix products  36 us (8%)
  local copies, waits for them, and re-layouts  28.1 us (6%)
  other arithmetic  17.6 us (4%)
    all_to_all x4, waiting for transfers between devices, exchange(): lax.all_to_all(block, 'expert', split_axis=0, concat_axis=0, tiled=True)  222 us
    ppermute x3, waiting for transfers between devices, per_device(): lax.ppermute(shard, 'dp', [(j, (j + shift) % ring) for j in range(ring)])  97.3 us
    all_to_all x4, starting transfers between devices, exchange(): lax.all_to_all(block, 'expert', split_axis=0, concat_axis=0, tiled=True)  31.4 us
    dot_general x1, matrix products, per_device(): lax.dot_general(row_block, gate_up_full, (((1,), (1,)), ((), ())), prefer...  15.7 us
    unnamed x31, local copies, waits for them, and re-layouts  12.6 us
    dot_general x1, matrix products, per_device(): jnp.dot(hidden, down_full, preferred_element_type=jnp.float32)  11 us
  transfers between devices with their start and end apart: 7, of which 6 were waited for; matrix products, arithmetic and copies ran while one was open for 16% of the time, Pallas kernels for 0%

profile of v7, /device:TPU:1, one launch (start us, length us, event | category | flops | bytes accessed | tf_op | source)
XLA Modules:
  0.0 438.5 jit_solution(8487251926334873050)
XLA Ops:
  0.6 0.0 copy-start
  0.6 0.0 copy-start.10
  0.7 0.0 copy-start.11
  0.7 1.9 pad_maximum_fusion
  2.5 0.0 copy-start.2
  2.5 3.9 reshape.48
  6.4 0.0 copy-done.2
  6.4 13.2 %all-to-all-start = ((bf16[64,24,768]{2,1,0:T(8,128)(2,1)}), bf16[64,24,768]{2,1,0:T(8,128)(2,1)S(1)}, u32[]{:S(2)}, u32[]{:S(2)}) async-start(bf16[64,24,768]{2,1,0:T(8,128)(2,1)} %reshape.48), calls=%async_computation | async-start | bytes 4718592 | tf_op jit(solution)/shard_map/all_to_all | solution.py:31
  19.6 0.0 copy-done.10
  19.6 0.0 copy-done.11
  19.6 0.1 select_reduce_fusion.2
  19.7 0.1 fusion.17
  19.9 0.1 select_reduce_fusion.1
  19.9 5.6 %fusion = pred[1536,128]{1,0:T(8,128)(4,1)S(1)} fusion(s32[8,128]{1,0:T(8,128)S(1)} %add_bitcast_fusion), kind=kLoop, calls=%fused_computation.5 | loop fusion | flops 2949120 | bytes 200704 | tf_op jit(solution)/shard_map/reduce_or | solution.py:28
  25.5 0.0 copy-done
  25.5 4.4 %convolution_convert_fusion.1 = bf16[1536,2048]{1,0:T(8,128)(2,1)} fusion(pred[1536,128]{1,0:T(8,128)(4,1)S(1)} %fusion, bf16[128,2048]{1,0:T(8,128)(2,1)S(1)} %copy-done), kind=kOutput, calls=%fused_computation.2 | convolution fusion | flops 808452096 | bytes 7012352 | tf_op jit(solution)/shard_map/dot_general | solution.py:51
  30.0 46.2 %all-to-all-done = bf16[64,24,768]{2,1,0:T(8,128)(2,1)S(1)} async-done(((bf16[64,24,768]{2,1,0:T(8,128)(2,1)}), bf16[64,24,768]{2,1,0:T(8,128)(2,1)S(1)}, u32[]{:S(2)}, u32[]{:S(2)}) %all-to-all-start) | async-done | bytes 2359328 | tf_op jit(solution)/shard_map/all_to_all | solution.py:31
  76.2 6.2 %all-to-all-start.1 = ((bf16[64,24,2048]{2,1,0:T(8,128)(2,1)}), bf16[64,24,2048]{2,1,0:T(8,128)(2,1)}, u32[]{:S(2)}, u32[]{:S(2)}) async-start(bf16[64,24,2048]{2,1,0:T(8,128)(2,1)} %bitcast.26), calls=%async_computation.1 | async-start | bytes 12582912 | tf_op jit(solution)/shard_map/all_to_all | solution.py:31
  82.4 0.0 copy-start.3
  82.4 1.3 collective-permute-start
  83.7 2.5 collective-permute-start.1
  86.1 1.2 collective-permute-start.2
  87.3 0.1 select_reduce_fusion.3
  87.4 2.1 bitcast_dynamic-update-slice_fusion.1
  89.5 46.8 %collective-permute-done = bf16[576,2048]{1,0:T(8,128)(2,1)S(1)} collective-permute-done((bf16[576,2048]{1,0:T(8,128)(2,1)}, bf16[576,2048]{1,0:T(8,128)(2,1)S(1)}, u32[]{:S(2)}, u32[]{:S(2)}) %collective-permute-start) | collective-permute-done | bytes 2359328 | tf_op jit(solution)/shard_map/ppermute | solution.py:40
  136.3 0.0 copy-start.7
  136.3 1.1 slice_dynamic-update-slice_fusion.5
  137.3 50.5 %collective-permute-done.1 = bf16[576,2048]{1,0:T(8,128)(2,1)S(1)} collective-permute-done((bf16[576,2048]{1,0:T(8,128)(2,1)}, bf16[576,2048]{1,0:T(8,128)(2,1)S(1)}, u32[]{:S(2)}, u32[]{:S(2)}) %collective-permute-start.1) | collective-permute-done | bytes 2359328 | tf_op jit(solution)/shard_map/ppermute | solution.py:40
  187.8 0.0 copy-start.6
  187.8 1.0 slice_dynamic-update-slice_fusion.4
  188.9 0.0 collective-permute-done.2
  188.9 0.0 copy-start.4
  188.9 1.4 copy-done.4
  190.2 1.0 slice_dynamic-update-slice_fusion.3
  191.2 0.0 copy-done.7
  191.2 0.0 copy-done.6
  191.2 0.0 copy-done.3
  191.2 1.0 bitcast_dynamic-update-slice_fusion
  192.2 2.1 gather_fusion
  194.4 28.8 %all-to-all-done.1 = bf16[64,24,2048]{2,1,0:T(8,128)(2,1)} async-done(((bf16[64,24,2048]{2,1,0:T(8,128)(2,1)}), bf16[64,24,2048]{2,1,0:T(8,128)(2,1)}, u32[]{:S(2)}, u32[]{:S(2)}) %all-to-all-start.1) | async-done | bytes 6291488 | tf_op jit(solution)/shard_map/all_to_all | solution.py:31
  223.2 5.8 %all-to-all-start.2 = ((bf16[64,24,768]{2,1,0:T(8,128)(2,1)}), bf16[64,24,768]{2,1,0:T(8,128)(2,1)S(1)}, u32[]{:S(2)}, u32[]{:S(2)}) async-start(bf16[64,24,768]{2,1,0:T(8,128)(2,1)} %gather_fusion), calls=%async_computation.2 | async-start | bytes 4718592 | tf_op jit(solution)/shard_map/all_to_all | solution.py:31
  229.0 0.0 copy-start.5
  229.0 2.6 slice_dynamic-update-slice_fusion.2
  231.6 2.4 slice_dynamic-update-slice_fusion.1
  234.0 0.0 copy-done.5
  234.0 1.0 slice_dynamic-update-slice_fusion
  235.0 0.0 copy-start.8
  235.0 15.7 %fusion.21 = f32[1536,1536]{1,0:T(8,128)} fusion(bf16[1536,2048]{1,0:T(8,128)(2,1)} %bitcast.6, bf16[1536,2048]{1,0:T(8,128)(2,1)} %get-tuple-element.15), kind=kOutput, calls=%fused_computation.49 | convolution fusion | flops 9663676416 | bytes 22020096 | tf_op jit(solution)/shard_map/dot_general | solution.py:62
  250.7 0.0 copy-done.8
  250.7 11.0 %convolution_convert_fusion = bf16[1536,2048]{1,0:T(8,128)(2,1)} fusion(bf16[192,2048]{1,0:T(8,128)(2,1)S(1)} %get-tuple-element.16, bf16[192,2048]{1,0:T(8,128)(2,1)S(1)} %get-tuple-element.18, bf16[192,2048]{1,0:T(8,128)(2,1)S(1)} %get-tuple-element.20, bf16[192,2048]{1,0:T(8,128)(2,1)S(1)} %bitcast.31, f32[1536,1536]{1,0:T(8,128)} %fusion.21), kind=kOutput, calls=%fused_computation.1 | convolution fusion | flops 4854644736 | bytes 18874368 | tf_op jit(solution)/shard_map/dot_general | solution.py:68
  261.7 24.0 %all-to-all-done.2 = bf16[64,24,768]{2,1,0:T(8,128)(2,1)S(1)} async-done(((bf16[64,24,768]{2,1,0:T(8,128)(2,1)}), bf16[64,24,768]{2,1,0:T(8,128)(2,1)S(1)}, u32[]{:S(2)}, u32[]{:S(2)}) %all-to-all-start.2) | async-done | bytes 2359328 | tf_op jit(solution)/shard_map/all_to_all | solution.py:31
  285.7 0.0 copy-start.9
  285.7 6.3 %all-to-all-start.3 = ((bf16[64,24,2048]{2,1,0:T(8,128)(2,1)}), bf16[64,24,2048]{2,1,0:T(8,128)(2,1)}, u32[]{:S(2)}, u32[]{:S(2)}) async-start(bf16[64,24,2048]{2,1,0:T(8,128)(2,1)} %bitcast.27), calls=%async_computation.3 | async-start | bytes 12582912 | tf_op jit(solution)/shard_map/all_to_all | solution.py:31
  292.0 0.0 copy-done.9
  292.0 8.1 %select_reduce_fusion = f32[1536,128]{1,0:T(8,128)S(1)} fusion(f32[8,128]{1,0:T(8,128)S(1)} %divide_bitcast_fusion, s32[8,128]{1,0:T(8,128)S(1)} %add_bitcast_fusion), kind=kLoop, calls=%fused_computation.3 | loop fusion | flops 4521984 | bytes 794624 | tf_op jit(solution)/shard_map/reduce_sum | solution.py:79
  300.1 0.9 reduce-precision_convert_fusion
  301.0 3.7 reshape.53
  304.7 2.7 slice.91
  307.4 2.1 slice_bitcast_fusion
  309.5 123.3 %all-to-all-done.3 = bf16[64,24,2048]{2,1,0:T(8,128)(2,1)} async-done(((bf16[64,24,2048]{2,1,0:T(8,128)(2,1)}), bf16[64,24,2048]{2,1,0:T(8,128)(2,1)}, u32[]{:S(2)}, u32[]{:S(2)}) %all-to-all-start.3) | async-done | bytes 6291488 | tf_op jit(solution)/shard_map/all_to_all | solution.py:31
  432.8 0.0 copy-start.1
  432.8 4.8 %fusion.13 = f32[256,2048]{1,0:T(8,128)S(1)} fusion(bf16[1536,2048]{1,0:T(8,128)(2,1)} %bitcast.10, bf16[128,1536]{0,1:T(8,128)(2,1)} %get-tuple-element.22, bf16[128,1536]{0,1:T(8,128)(2,1)S(1)} %get-tuple-element.21), kind=kOutput, calls=%fused_computation.29 | convolution fusion | flops 1612185600 | bytes 9175040 | tf_op jit(solution)/shard_map/dot_general | solution.py:83
  437.6 0.9 fusion.11
  438.5 0.0 copy-done.1
  (5 shorter events, 0.1 us)
Async XLA Ops:
  0.6 24.9 %copy-start = (bf16[128,2048]{1,0:T(8,128)(2,1)S(1)}, bf16[128,2048]{1,0:T(8,128)(2,1)}, u32[]{:S(2)}) copy-start(bf16[128,2048]{1,0:T(8,128)(2,1)} %param.6) | copy-start | bytes 1572868
  0.6 18.9 %copy-start.10 = (s32[128,8]{0,1:T(8,128)S(1)}, s32[128,8]{0,1:T(8,128)}, u32[]{:S(2)}) copy-start(s32[128,8]{0,1:T(8,128)} %param.7) | copy-start | bytes 12292
  0.7 18.9 %copy-start.11 = (s32[64]{0:T(128)S(1)}, s32[64]{0:T(128)}, u32[]{:S(2)}) copy-start(s32[64]{0:T(128)} %param.9) | copy-start | bytes 772
  2.5 3.9 copy-start.2
  6.4 69.8 %all-to-all-start = ((bf16[64,24,768]{2,1,0:T(8,128)(2,1)}), bf16[64,24,768]{2,1,0:T(8,128)(2,1)S(1)}, u32[]{:S(2)}, u32[]{:S(2)}) async-start(bf16[64,24,768]{2,1,0:T(8,128)(2,1)} %reshape.48), calls=%async_computation | async-start | bytes 4718592 | tf_op jit(solution)/shard_map/all_to_all | solution.py:31
  76.2 147.0 %all-to-all-start.1 = ((bf16[64,24,2048]{2,1,0:T(8,128)(2,1)}), bf16[64,24,2048]{2,1,0:T(8,128)(2,1)}, u32[]{:S(2)}, u32[]{:S(2)}) async-start(bf16[64,24,2048]{2,1,0:T(8,128)(2,1)} %bitcast.26), calls=%async_computation.1 | async-start | bytes 12582912 | tf_op jit(solution)/shard_map/all_to_all | solution.py:31
  82.4 108.9 %copy-start.3 = (bf16[1,2,192,2048]{3,2,1,0:T(8,128)(2,1)S(1)}, bf16[1,2,192,2048]{3,2,1,0:T(8,128)(2,1)}, u32[]{:S(2)}) copy-start(bf16[1,2,192,2048]{3,2,1,0:T(8,128)(2,1)} %param.10) | copy-start | bytes 4718596
  82.4 53.9 %collective-permute-start = (bf16[576,2048]{1,0:T(8,128)(2,1)}, bf16[576,2048]{1,0:T(8,128)(2,1)S(1)}, u32[]{:S(2)}, u32[]{:S(2)}) collective-permute-start(bf16[576,2048]{1,0:T(8,128)(2,1)} %copy-done.2), channel_id=1, source_target_pairs={{0,64},{64,128},{128,192},{192,0},{1,65},{65,129},{129,193},{193,1... | collective-permute-start | bytes 7077896 | tf_op jit(solution)/shard_map/ppermute | solution.py:40
  83.7 104.2 %collective-permute-start.1 = (bf16[576,2048]{1,0:T(8,128)(2,1)}, bf16[576,2048]{1,0:T(8,128)(2,1)S(1)}, u32[]{:S(2)}, u32[]{:S(2)}) collective-permute-start(bf16[576,2048]{1,0:T(8,128)(2,1)} %copy-done.2), channel_id=1, source_target_pairs={{0,128},{64,192},{128,0},{192,64},{1,129},{65,193},{129,1},{193,65... | collective-permute-start | bytes 7077896 | tf_op jit(solution)/shard_map/ppermute | solution.py:40
  86.1 102.8 %collective-permute-start.2 = (bf16[576,2048]{1,0:T(8,128)(2,1)}, bf16[576,2048]{1,0:T(8,128)(2,1)S(1)}, u32[]{:S(2)}, u32[]{:S(2)}) collective-permute-start(bf16[576,2048]{1,0:T(8,128)(2,1)} %copy-done.2), channel_id=1, source_target_pairs={{0,192},{64,0},{128,64},{192,128},{1,193},{65,1},{129,65},{193,129... | collective-permute-start | bytes 7077896 | tf_op jit(solution)/shard_map/ppermute | solution.py:40
  136.3 55.0 %copy-start.7 = (bf16[576,2048]{1,0:T(8,128)(2,1)}, bf16[576,2048]{1,0:T(8,128)(2,1)S(1)}, u32[]{:S(2)}) copy-start(bf16[576,2048]{1,0:T(8,128)(2,1)S(1)} %collective-permute-done) | copy-start | bytes 7077892
  187.8 3.4 copy-start.6
  188.9 1.4 copy-start.4
  223.2 62.4 %all-to-all-start.2 = ((bf16[64,24,768]{2,1,0:T(8,128)(2,1)}), bf16[64,24,768]{2,1,0:T(8,128)(2,1)S(1)}, u32[]{:S(2)}, u32[]{:S(2)}) async-start(bf16[64,24,768]{2,1,0:T(8,128)(2,1)} %gather_fusion), calls=%async_computation.2 | async-start | bytes 4718592 | tf_op jit(solution)/shard_map/all_to_all | solution.py:31
  229.0 5.0 %copy-start.5 = (bf16[576,2048]{1,0:T(8,128)(2,1)S(1)}, bf16[576,2048]{1,0:T(8,128)(2,1)}, u32[]{:S(2)}) copy-start(bf16[576,2048]{1,0:T(8,128)(2,1)} %copy-done.4) | copy-start | bytes 7077892
  235.0 15.7 %copy-start.8 = (bf16[1,192,2048]{2,1,0:T(8,128)(2,1)S(1)}, bf16[1,192,2048]{2,1,0:T(8,128)(2,1)}, u32[]{:S(2)}) copy-start(bf16[1,192,2048]{2,1,0:T(8,128)(2,1)} %param.11) | copy-start | bytes 2359300
  285.7 6.3 %copy-start.9 = (f32[128,8]{0,1:T(8,128)S(1)}, f32[128,8]{0,1:T(8,128)}, u32[]{:S(2)}) copy-start(f32[128,8]{0,1:T(8,128)} %param.8) | copy-start | bytes 12292
  285.7 147.1 %all-to-all-start.3 = ((bf16[64,24,2048]{2,1,0:T(8,128)(2,1)}), bf16[64,24,2048]{2,1,0:T(8,128)(2,1)}, u32[]{:S(2)}, u32[]{:S(2)}) async-start(bf16[64,24,2048]{2,1,0:T(8,128)(2,1)} %bitcast.27), calls=%async_computation.3 | async-start | bytes 12582912 | tf_op jit(solution)/shard_map/all_to_all | solution.py:31
  432.8 5.7 %copy-start.1 = (bf16[128,2048]{1,0:T(8,128)(2,1)S(1)}, bf16[128,2048]{1,0:T(8,128)(2,1)}, u32[]{:S(2)}) copy-start(bf16[128,2048]{1,0:T(8,128)(2,1)} %param.6) | copy-start | bytes 1572868

commit v8 on v7

--- a/solution.py
+++ b/solution.py
@@ -80,12 +80,13 @@
     rounded = lax.reduce_precision(part, exponent_bits=8, mantissa_bits=7)
     part_hi = rounded.astype(jnp.bfloat16)
     part_lo = (part - rounded).astype(jnp.bfloat16)
-    both = jnp.dot(
+    both = lax.dot_general(
+        returned.reshape(slots, model_width),
         jnp.concatenate([part_hi, part_lo], axis=0),
-        returned.reshape(slots, model_width),
+        (((0,), (1,)), ((), ())),
         preferred_element_type=jnp.float32,
     )
-    mixed_rows = both[:tok_dev] + both[tok_dev:]
+    mixed_rows = (both[:, :tok_dev] + both[:, tok_dev:]).T
     return (mixed_rows.astype(jnp.bfloat16), placed_gate_up, placed_down)
 
 

time: 439 us -> 439 us (level)
    unnamed x31 -> x32, local copies, waits for them, and re-layouts: 12.6 us -> 13.6 us
where the time goes in v8:
time: 439 us
  waiting for transfers between devices  320 us (73%)
  starting transfers between devices  36.3 us (8%)
  matrix products  36.1 us (8%)
  local copies, waits for them, and re-layouts  29.1 us (7%)
  other arithmetic  16.8 us (4%)
    all_to_all x4, waiting for transfers between devices, exchange(): lax.all_to_all(block, 'expert', split_axis=0, concat_axis=0, tiled=True)  222 us
    ppermute x3, waiting for transfers between devices, per_device(): lax.ppermute(shard, 'dp', [(j, (j + shift) % ring) for j in range(ring)])  97.3 us
    all_to_all x4, starting transfers between devices, exchange(): lax.all_to_all(block, 'expert', split_axis=0, concat_axis=0, tiled=True)  31.4 us
    dot_general x1, matrix products, per_device(): lax.dot_general(row_block, gate_up_full, (((1,), (1,)), ((), ())), prefer...  15.7 us
    unnamed x32, local copies, waits for them, and re-layouts  13.6 us
    dot_general x1, matrix products, per_device(): jnp.dot(hidden, down_full, preferred_element_type=jnp.float32)  11 us
  transfers between devices with their start and end apart: 7, of which 6 were waited for; matrix products, arithmetic and copies ran while one was open for 16% of the time, Pallas kernels for 0%

profile of v8, /device:TPU:1, one launch (start us, length us, event | category | flops | bytes accessed | tf_op | source)
XLA Modules:
  0.0 438.8 jit_solution(5156217774079201023)
XLA Ops:
  0.6 0.0 copy-start
  0.6 0.0 copy-start.10
  0.7 0.0 copy-start.11
  0.7 1.9 pad_maximum_fusion
  2.5 0.0 copy-start.2
  2.5 3.9 reshape.48
  6.4 0.0 copy-done.2
  6.4 13.2 %all-to-all-start = ((bf16[64,24,768]{2,1,0:T(8,128)(2,1)}), bf16[64,24,768]{2,1,0:T(8,128)(2,1)S(1)}, u32[]{:S(2)}, u32[]{:S(2)}) async-start(bf16[64,24,768]{2,1,0:T(8,128)(2,1)} %reshape.48), calls=%async_computation | async-start | bytes 4718592 | tf_op jit(solution)/shard_map/all_to_all | solution.py:31
  19.6 0.0 copy-done.10
  19.6 0.0 copy-done.11
  19.6 0.1 select_reduce_fusion.2
  19.7 0.1 fusion.18
  19.9 0.1 select_reduce_fusion.1
  19.9 5.6 %fusion = pred[1536,128]{1,0:T(8,128)(4,1)S(1)} fusion(s32[8,128]{1,0:T(8,128)S(1)} %add_bitcast_fusion), kind=kLoop, calls=%fused_computation.5 | loop fusion | flops 2949120 | bytes 200704 | tf_op jit(solution)/shard_map/reduce_or | solution.py:28
  25.5 0.0 copy-done
  25.5 4.4 %convolution_convert_fusion.1 = bf16[1536,2048]{1,0:T(8,128)(2,1)} fusion(pred[1536,128]{1,0:T(8,128)(4,1)S(1)} %fusion, bf16[128,2048]{1,0:T(8,128)(2,1)S(1)} %copy-done), kind=kOutput, calls=%fused_computation.2 | convolution fusion | flops 808452096 | bytes 7012352 | tf_op jit(solution)/shard_map/dot_general | solution.py:51
  30.0 46.2 %all-to-all-done = bf16[64,24,768]{2,1,0:T(8,128)(2,1)S(1)} async-done(((bf16[64,24,768]{2,1,0:T(8,128)(2,1)}), bf16[64,24,768]{2,1,0:T(8,128)(2,1)S(1)}, u32[]{:S(2)}, u32[]{:S(2)}) %all-to-all-start) | async-done | bytes 2359328 | tf_op jit(solution)/shard_map/all_to_all | solution.py:31
  76.2 6.2 %all-to-all-start.1 = ((bf16[64,24,2048]{2,1,0:T(8,128)(2,1)}), bf16[64,24,2048]{2,1,0:T(8,128)(2,1)}, u32[]{:S(2)}, u32[]{:S(2)}) async-start(bf16[64,24,2048]{2,1,0:T(8,128)(2,1)} %bitcast.28), calls=%async_computation.1 | async-start | bytes 12582912 | tf_op jit(solution)/shard_map/all_to_all | solution.py:31
  82.4 0.0 copy-start.3
  82.4 1.3 collective-permute-start
  83.7 2.5 collective-permute-start.1
  86.1 1.2 collective-permute-start.2
  87.3 0.1 select_reduce_fusion.3
  87.4 2.1 bitcast_dynamic-update-slice_fusion.1
  89.5 46.8 %collective-permute-done = bf16[576,2048]{1,0:T(8,128)(2,1)S(1)} collective-permute-done((bf16[576,2048]{1,0:T(8,128)(2,1)}, bf16[576,2048]{1,0:T(8,128)(2,1)S(1)}, u32[]{:S(2)}, u32[]{:S(2)}) %collective-permute-start) | collective-permute-done | bytes 2359328 | tf_op jit(solution)/shard_map/ppermute | solution.py:40
  136.3 0.0 copy-start.7
  136.3 1.1 slice_dynamic-update-slice_fusion.5
  137.3 50.5 %collective-permute-done.1 = bf16[576,2048]{1,0:T(8,128)(2,1)S(1)} collective-permute-done((bf16[576,2048]{1,0:T(8,128)(2,1)}, bf16[576,2048]{1,0:T(8,128)(2,1)S(1)}, u32[]{:S(2)}, u32[]{:S(2)}) %collective-permute-start.1) | collective-permute-done | bytes 2359328 | tf_op jit(solution)/shard_map/ppermute | solution.py:40
  187.8 0.0 copy-start.6
  187.8 1.0 slice_dynamic-update-slice_fusion.4
  188.9 0.0 collective-permute-done.2
  188.9 1.4 copy-done.4
  190.2 1.0 slice_dynamic-update-slice_fusion.3
  191.2 0.0 copy-done.7
  191.2 0.0 copy-done.6
  191.2 0.0 copy-done.3
  191.2 1.0 bitcast_dynamic-update-slice_fusion
  192.2 2.2 gather_fusion
  194.4 28.8 %all-to-all-done.1 = bf16[64,24,2048]{2,1,0:T(8,128)(2,1)} async-done(((bf16[64,24,2048]{2,1,0:T(8,128)(2,1)}), bf16[64,24,2048]{2,1,0:T(8,128)(2,1)}, u32[]{:S(2)}, u32[]{:S(2)}) %all-to-all-start.1) | async-done | bytes 6291488 | tf_op jit(solution)/shard_map/all_to_all | solution.py:31
  223.2 5.8 %all-to-all-start.2 = ((bf16[64,24,768]{2,1,0:T(8,128)(2,1)}), bf16[64,24,768]{2,1,0:T(8,128)(2,1)S(1)}, u32[]{:S(2)}, u32[]{:S(2)}) async-start(bf16[64,24,768]{2,1,0:T(8,128)(2,1)} %gather_fusion), calls=%async_computation.2 | async-start | bytes 4718592 | tf_op jit(solution)/shard_map/all_to_all | solution.py:31
  229.0 0.0 copy-start.5
  229.0 2.6 slice_dynamic-update-slice_fusion.2
  231.6 2.4 slice_dynamic-update-slice_fusion.1
  234.0 0.0 copy-done.5
  234.0 1.0 slice_dynamic-update-slice_fusion
  235.0 0.0 copy-start.8
  235.0 15.7 %fusion.22 = f32[1536,1536]{1,0:T(8,128)} fusion(bf16[1536,2048]{1,0:T(8,128)(2,1)} %bitcast.4, bf16[1536,2048]{1,0:T(8,128)(2,1)} %get-tuple-element.21), kind=kOutput, calls=%fused_computation.50 | convolution fusion | flops 9663676416 | bytes 22020096 | tf_op jit(solution)/shard_map/dot_general | solution.py:62
  250.7 0.0 copy-done.8
  250.7 11.0 %convolution_convert_fusion = bf16[1536,2048]{1,0:T(8,128)(2,1)} fusion(bf16[192,2048]{1,0:T(8,128)(2,1)S(1)} %get-tuple-element.22, bf16[192,2048]{1,0:T(8,128)(2,1)S(1)} %get-tuple-element.24, bf16[192,2048]{1,0:T(8,128)(2,1)S(1)} %get-tuple-element.26, bf16[192,2048]{1,0:T(8,128)(2,1)S(1)} %bitcast.33, f32[1536,1536]{1,0:T(8,128)} %fusion.22), kind=kOutput, calls=%fused_computation.1 | convolution fusion | flops 4854644736 | bytes 18874368 | tf_op jit(solution)/shard_map/dot_general | solution.py:68
  261.7 24.0 %all-to-all-done.2 = bf16[64,24,768]{2,1,0:T(8,128)(2,1)S(1)} async-done(((bf16[64,24,768]{2,1,0:T(8,128)(2,1)}), bf16[64,24,768]{2,1,0:T(8,128)(2,1)S(1)}, u32[]{:S(2)}, u32[]{:S(2)}) %all-to-all-start.2) | async-done | bytes 2359328 | tf_op jit(solution)/shard_map/all_to_all | solution.py:31
  285.7 0.0 copy-start.9
  285.7 6.3 %all-to-all-start.3 = ((bf16[64,24,2048]{2,1,0:T(8,128)(2,1)}), bf16[64,24,2048]{2,1,0:T(8,128)(2,1)}, u32[]{:S(2)}, u32[]{:S(2)}) async-start(bf16[64,24,2048]{2,1,0:T(8,128)(2,1)} %bitcast.29), calls=%async_computation.3 | async-start | bytes 12582912 | tf_op jit(solution)/shard_map/all_to_all | solution.py:31
  292.0 0.0 copy-done.9
  292.0 8.1 %select_reduce_fusion = f32[1536,128]{1,0:T(8,128)S(1)} fusion(f32[8,128]{1,0:T(8,128)S(1)} %divide_bitcast_fusion, s32[8,128]{1,0:T(8,128)S(1)} %add_bitcast_fusion), kind=kLoop, calls=%fused_computation.3 | loop fusion | flops 4521984 | bytes 794624 | tf_op jit(solution)/shard_map/reduce_sum | solution.py:79
  300.1 0.9 reduce-precision_convert_fusion
  301.0 3.7 reshape.53
  304.7 2.7 slice.91
  307.4 2.1 slice_bitcast_fusion
  309.5 123.3 %all-to-all-done.3 = bf16[64,24,2048]{2,1,0:T(8,128)(2,1)} async-done(((bf16[64,24,2048]{2,1,0:T(8,128)(2,1)}), bf16[64,24,2048]{2,1,0:T(8,128)(2,1)}, u32[]{:S(2)}, u32[]{:S(2)}) %all-to-all-start.3) | async-done | bytes 6291488 | tf_op jit(solution)/shard_map/all_to_all | solution.py:31
  432.8 0.0 copy-start.1
  432.8 4.8 %fusion.13 = f32[2048,256]{1,0:T(8,128)S(1)} fusion(bf16[1536,2048]{1,0:T(8,128)(2,1)} %bitcast.8, bf16[128,1536]{0,1:T(8,128)(2,1)} %get-tuple-element.28, bf16[128,1536]{0,1:T(8,128)(2,1)S(1)} %get-tuple-element.27), kind=kOutput, calls=%fused_computation.29 | convolution fusion | flops 1612185600 | bytes 9175040 | tf_op jit(solution)/shard_map/dot_general | solution.py:83
  437.6 0.1 fusion.17
  437.8 1.0 copy.13
  438.8 0.0 copy-done.1
  (6 shorter events, 0.1 us)
Async XLA Ops:
  0.6 24.9 %copy-start = (bf16[128,2048]{1,0:T(8,128)(2,1)S(1)}, bf16[128,2048]{1,0:T(8,128)(2,1)}, u32[]{:S(2)}) copy-start(bf16[128,2048]{1,0:T(8,128)(2,1)} %param.6) | copy-start | bytes 1572868
  0.6 18.9 %copy-start.10 = (s32[128,8]{0,1:T(8,128)S(1)}, s32[128,8]{0,1:T(8,128)}, u32[]{:S(2)}) copy-start(s32[128,8]{0,1:T(8,128)} %param.7) | copy-start | bytes 12292
  0.7 18.9 %copy-start.11 = (s32[64]{0:T(128)S(1)}, s32[64]{0:T(128)}, u32[]{:S(2)}) copy-start(s32[64]{0:T(128)} %param.9) | copy-start | bytes 772
  2.5 3.9 copy-start.2
  6.4 69.8 %all-to-all-start = ((bf16[64,24,768]{2,1,0:T(8,128)(2,1)}), bf16[64,24,768]{2,1,0:T(8,128)(2,1)S(1)}, u32[]{:S(2)}, u32[]{:S(2)}) async-start(bf16[64,24,768]{2,1,0:T(8,128)(2,1)} %reshape.48), calls=%async_computation | async-start | bytes 4718592 | tf_op jit(solution)/shard_map/all_to_all | solution.py:31
  76.2 147.0 %all-to-all-start.1 = ((bf16[64,24,2048]{2,1,0:T(8,128)(2,1)}), bf16[64,24,2048]{2,1,0:T(8,128)(2,1)}, u32[]{:S(2)}, u32[]{:S(2)}) async-start(bf16[64,24,2048]{2,1,0:T(8,128)(2,1)} %bitcast.28), calls=%async_computation.1 | async-start | bytes 12582912 | tf_op jit(solution)/shard_map/all_to_all | solution.py:31
  82.4 108.9 %copy-start.3 = (bf16[1,2,192,2048]{3,2,1,0:T(8,128)(2,1)S(1)}, bf16[1,2,192,2048]{3,2,1,0:T(8,128)(2,1)}, u32[]{:S(2)}) copy-start(bf16[1,2,192,2048]{3,2,1,0:T(8,128)(2,1)} %param.10) | copy-start | bytes 4718596
  82.4 53.9 %collective-permute-start = (bf16[576,2048]{1,0:T(8,128)(2,1)}, bf16[576,2048]{1,0:T(8,128)(2,1)S(1)}, u32[]{:S(2)}, u32[]{:S(2)}) collective-permute-start(bf16[576,2048]{1,0:T(8,128)(2,1)} %copy-done.2), channel_id=1, source_target_pairs={{0,64},{64,128},{128,192},{192,0},{1,65},{65,129},{129,193},{193,1... | collective-permute-start | bytes 7077896 | tf_op jit(solution)/shard_map/ppermute | solution.py:40
  83.7 104.2 %collective-permute-start.1 = (bf16[576,2048]{1,0:T(8,128)(2,1)}, bf16[576,2048]{1,0:T(8,128)(2,1)S(1)}, u32[]{:S(2)}, u32[]{:S(2)}) collective-permute-start(bf16[576,2048]{1,0:T(8,128)(2,1)} %copy-done.2), channel_id=1, source_target_pairs={{0,128},{64,192},{128,0},{192,64},{1,129},{65,193},{129,1},{193,65... | collective-permute-start | bytes 7077896 | tf_op jit(solution)/shard_map/ppermute | solution.py:40
  86.1 102.8 %collective-permute-start.2 = (bf16[576,2048]{1,0:T(8,128)(2,1)}, bf16[576,2048]{1,0:T(8,128)(2,1)S(1)}, u32[]{:S(2)}, u32[]{:S(2)}) collective-permute-start(bf16[576,2048]{1,0:T(8,128)(2,1)} %copy-done.2), channel_id=1, source_target_pairs={{0,192},{64,0},{128,64},{192,128},{1,193},{65,1},{129,65},{193,129... | collective-permute-start | bytes 7077896 | tf_op jit(solution)/shard_map/ppermute | solution.py:40
  136.3 55.0 %copy-start.7 = (bf16[576,2048]{1,0:T(8,128)(2,1)}, bf16[576,2048]{1,0:T(8,128)(2,1)S(1)}, u32[]{:S(2)}) copy-start(bf16[576,2048]{1,0:T(8,128)(2,1)S(1)} %collective-permute-done) | copy-start | bytes 7077892
  187.8 3.4 copy-start.6
  188.9 1.4 copy-start.4
  223.2 62.4 %all-to-all-start.2 = ((bf16[64,24,768]{2,1,0:T(8,128)(2,1)}), bf16[64,24,768]{2,1,0:T(8,128)(2,1)S(1)}, u32[]{:S(2)}, u32[]{:S(2)}) async-start(bf16[64,24,768]{2,1,0:T(8,128)(2,1)} %gather_fusion), calls=%async_computation.2 | async-start | bytes 4718592 | tf_op jit(solution)/shard_map/all_to_all | solution.py:31
  229.0 5.0 %copy-start.5 = (bf16[576,2048]{1,0:T(8,128)(2,1)S(1)}, bf16[576,2048]{1,0:T(8,128)(2,1)}, u32[]{:S(2)}) copy-start(bf16[576,2048]{1,0:T(8,128)(2,1)} %copy-done.4) | copy-start | bytes 7077892
  235.0 15.7 %copy-start.8 = (bf16[1,192,2048]{2,1,0:T(8,128)(2,1)S(1)}, bf16[1,192,2048]{2,1,0:T(8,128)(2,1)}, u32[]{:S(2)}) copy-start(bf16[1,192,2048]{2,1,0:T(8,128)(2,1)} %param.11) | copy-start | bytes 2359300
  285.7 6.3 %copy-start.9 = (f32[128,8]{0,1:T(8,128)S(1)}, f32[128,8]{0,1:T(8,128)}, u32[]{:S(2)}) copy-start(f32[128,8]{0,1:T(8,128)} %param.8) | copy-start | bytes 12292
  285.7 147.1 %all-to-all-start.3 = ((bf16[64,24,2048]{2,1,0:T(8,128)(2,1)}), bf16[64,24,2048]{2,1,0:T(8,128)(2,1)}, u32[]{:S(2)}, u32[]{:S(2)}) async-start(bf16[64,24,2048]{2,1,0:T(8,128)(2,1)} %bitcast.29), calls=%async_computation.3 | async-start | bytes 12582912 | tf_op jit(solution)/shard_map/all_to_all | solution.py:31
  432.8 6.0 %copy-start.1 = (bf16[128,2048]{1,0:T(8,128)(2,1)S(1)}, bf16[128,2048]{1,0:T(8,128)(2,1)}, u32[]{:S(2)}) copy-start(bf16[128,2048]{1,0:T(8,128)(2,1)} %param.6) | copy-start | bytes 1572868

commit v9 on v7

--- a/solution.py
+++ b/solution.py
@@ -77,15 +77,9 @@
 
     gates = gate_probs / jnp.sum(gate_probs, axis=1, keepdims=True)
     part = jnp.sum(jnp.where(hits, gates.T[None, :, :], 0.0), axis=1).T
-    rounded = lax.reduce_precision(part, exponent_bits=8, mantissa_bits=7)
-    part_hi = rounded.astype(jnp.bfloat16)
-    part_lo = (part - rounded).astype(jnp.bfloat16)
-    both = jnp.dot(
-        jnp.concatenate([part_hi, part_lo], axis=0),
-        returned.reshape(slots, model_width),
-        preferred_element_type=jnp.float32,
+    mixed_rows = jnp.dot(
+        part.astype(jnp.bfloat16), returned.reshape(slots, model_width), preferred_element_type=jnp.float32
     )
-    mixed_rows = both[:tok_dev] + both[tok_dev:]
     return (mixed_rows.astype(jnp.bfloat16), placed_gate_up, placed_down)
 
 

time: 439 us -> 438 us (level)
  no operation moved by 1% of the time
where the time goes in v9:
time: 438 us; the launch traced here: 437 us
  waiting for transfers between devices  320 us (73%)
  starting transfers between devices  36.3 us (8%)
  matrix products  35.9 us (8%)
  local copies, waits for them, and re-layouts  28.1 us (6%)
  other arithmetic  15.9 us (4%)
    all_to_all x4, waiting for transfers between devices, exchange(): lax.all_to_all(block, 'expert', split_axis=0, concat_axis=0, tiled=True)  223 us
    ppermute x3, waiting for transfers between devices, per_device(): lax.ppermute(shard, 'dp', [(j, (j + shift) % ring) for j in range(ring)])  97.3 us
    all_to_all x4, starting transfers between devices, exchange(): lax.all_to_all(block, 'expert', split_axis=0, concat_axis=0, tiled=True)  31.4 us
    dot_general x1, matrix products, per_device(): lax.dot_general(row_block, gate_up_full, (((1,), (1,)), ((), ())), prefer...  15.8 us
    unnamed x31, local copies, waits for them, and re-layouts  12.5 us
    dot_general x1, matrix products, per_device(): jnp.dot(hidden, down_full, preferred_element_type=jnp.float32)  10.9 us
  transfers between devices with their start and end apart: 7, of which 6 were waited for; matrix products, arithmetic and copies ran while one was open for 16% of the time, Pallas kernels for 0%

profile of v9, /device:TPU:1, one launch (start us, length us, event | category | flops | bytes accessed | tf_op | source)
XLA Modules:
  0.0 437.4 jit_solution(10428651246061342004)
XLA Ops:
  0.6 0.0 copy-start
  0.6 0.0 copy-start.10
  0.7 0.0 copy-start.11
  0.7 1.9 pad_maximum_fusion
  2.5 0.0 copy-start.2
  2.5 3.9 reshape.48
  6.4 0.0 copy-done.2
  6.4 13.2 %all-to-all-start = ((bf16[64,24,768]{2,1,0:T(8,128)(2,1)}), bf16[64,24,768]{2,1,0:T(8,128)(2,1)S(1)}, u32[]{:S(2)}, u32[]{:S(2)}) async-start(bf16[64,24,768]{2,1,0:T(8,128)(2,1)} %reshape.48), calls=%async_computation | async-start | bytes 4718592 | tf_op jit(solution)/shard_map/all_to_all | solution.py:31
  19.6 0.0 copy-done.10
  19.6 0.0 copy-done.11
  19.6 0.1 select_reduce_fusion.2
  19.7 0.1 fusion.12
  19.9 0.1 select_reduce_fusion.1
  19.9 5.6 %fusion = pred[1536,128]{1,0:T(8,128)(4,1)S(1)} fusion(s32[8,128]{1,0:T(8,128)S(1)} %add_bitcast_fusion), kind=kLoop, calls=%fused_computation.5 | loop fusion | flops 2949120 | bytes 200704 | tf_op jit(solution)/shard_map/reduce_or | solution.py:28
  25.5 0.0 copy-done
  25.5 4.4 %convolution_convert_fusion.1 = bf16[1536,2048]{1,0:T(8,128)(2,1)} fusion(pred[1536,128]{1,0:T(8,128)(4,1)S(1)} %fusion, bf16[128,2048]{1,0:T(8,128)(2,1)S(1)} %copy-done), kind=kOutput, calls=%fused_computation.2 | convolution fusion | flops 808452096 | bytes 7012352 | tf_op jit(solution)/shard_map/dot_general | solution.py:51
  30.0 46.3 %all-to-all-done = bf16[64,24,768]{2,1,0:T(8,128)(2,1)S(1)} async-done(((bf16[64,24,768]{2,1,0:T(8,128)(2,1)}), bf16[64,24,768]{2,1,0:T(8,128)(2,1)S(1)}, u32[]{:S(2)}, u32[]{:S(2)}) %all-to-all-start) | async-done | bytes 2359328 | tf_op jit(solution)/shard_map/all_to_all | solution.py:31
  76.2 6.2 %all-to-all-start.1 = ((bf16[64,24,2048]{2,1,0:T(8,128)(2,1)}), bf16[64,24,2048]{2,1,0:T(8,128)(2,1)}, u32[]{:S(2)}, u32[]{:S(2)}) async-start(bf16[64,24,2048]{2,1,0:T(8,128)(2,1)} %bitcast.24), calls=%async_computation.1 | async-start | bytes 12582912 | tf_op jit(solution)/shard_map/all_to_all | solution.py:31
  82.4 0.0 copy-start.3
  82.4 1.3 collective-permute-start
  83.7 2.5 collective-permute-start.1
  86.1 1.2 collective-permute-start.2
  87.3 0.1 select_reduce_fusion.3
  87.4 2.1 bitcast_dynamic-update-slice_fusion.1
  89.5 46.8 %collective-permute-done = bf16[576,2048]{1,0:T(8,128)(2,1)S(1)} collective-permute-done((bf16[576,2048]{1,0:T(8,128)(2,1)}, bf16[576,2048]{1,0:T(8,128)(2,1)S(1)}, u32[]{:S(2)}, u32[]{:S(2)}) %collective-permute-start) | collective-permute-done | bytes 2359328 | tf_op jit(solution)/shard_map/ppermute | solution.py:40
  136.3 0.0 copy-start.7
  136.3 1.0 slice_dynamic-update-slice_fusion.5
  137.3 50.5 %collective-permute-done.1 = bf16[576,2048]{1,0:T(8,128)(2,1)S(1)} collective-permute-done((bf16[576,2048]{1,0:T(8,128)(2,1)}, bf16[576,2048]{1,0:T(8,128)(2,1)S(1)}, u32[]{:S(2)}, u32[]{:S(2)}) %collective-permute-start.1) | collective-permute-done | bytes 2359328 | tf_op jit(solution)/shard_map/ppermute | solution.py:40
  187.8 0.0 copy-start.6
  187.8 1.0 slice_dynamic-update-slice_fusion.4
  188.9 0.0 collective-permute-done.2
  188.9 0.0 copy-start.4
  188.9 1.4 copy-done.4
  190.2 1.0 slice_dynamic-update-slice_fusion.3
  191.2 0.0 copy-done.7
  191.2 0.0 copy-done.6
  191.2 0.0 copy-done.3
  191.2 1.0 bitcast_dynamic-update-slice_fusion
  192.2 2.2 gather_fusion
  194.4 28.8 %all-to-all-done.1 = bf16[64,24,2048]{2,1,0:T(8,128)(2,1)} async-done(((bf16[64,24,2048]{2,1,0:T(8,128)(2,1)}), bf16[64,24,2048]{2,1,0:T(8,128)(2,1)}, u32[]{:S(2)}, u32[]{:S(2)}) %all-to-all-start.1) | async-done | bytes 6291488 | tf_op jit(solution)/shard_map/all_to_all | solution.py:31
  223.2 5.8 %all-to-all-start.2 = ((bf16[64,24,768]{2,1,0:T(8,128)(2,1)}), bf16[64,24,768]{2,1,0:T(8,128)(2,1)S(1)}, u32[]{:S(2)}, u32[]{:S(2)}) async-start(bf16[64,24,768]{2,1,0:T(8,128)(2,1)} %gather_fusion), calls=%async_computation.2 | async-start | bytes 4718592 | tf_op jit(solution)/shard_map/all_to_all | solution.py:31
  229.0 0.0 copy-start.5
  229.0 2.5 slice_dynamic-update-slice_fusion.2
  231.6 2.4 slice_dynamic-update-slice_fusion.1
  234.0 0.0 copy-done.5
  234.0 1.0 slice_dynamic-update-slice_fusion
  235.0 0.0 copy-start.8
  235.0 15.8 %fusion.15 = f32[1536,1536]{1,0:T(8,128)} fusion(bf16[1536,2048]{1,0:T(8,128)(2,1)} %bitcast.5, bf16[1536,2048]{1,0:T(8,128)(2,1)} %get-tuple-element.15), kind=kOutput, calls=%fused_computation.41 | convolution fusion | flops 9663676416 | bytes 22020096 | tf_op jit(solution)/shard_map/dot_general | solution.py:62
  250.8 0.0 copy-done.8
  250.8 10.9 %convolution_convert_fusion = bf16[1536,2048]{1,0:T(8,128)(2,1)} fusion(bf16[192,2048]{1,0:T(8,128)(2,1)S(1)} %get-tuple-element.16, bf16[192,2048]{1,0:T(8,128)(2,1)S(1)} %get-tuple-element.18, bf16[192,2048]{1,0:T(8,128)(2,1)S(1)} %get-tuple-element.20, bf16[192,2048]{1,0:T(8,128)(2,1)S(1)} %bitcast.29, f32[1536,1536]{1,0:T(8,128)} %fusion.15), kind=kOutput, calls=%fused_computation.1 | convolution fusion | flops 4854644736 | bytes 18874368 | tf_op jit(solution)/shard_map/dot_general | solution.py:68
  261.7 24.0 %all-to-all-done.2 = bf16[64,24,768]{2,1,0:T(8,128)(2,1)S(1)} async-done(((bf16[64,24,768]{2,1,0:T(8,128)(2,1)}), bf16[64,24,768]{2,1,0:T(8,128)(2,1)S(1)}, u32[]{:S(2)}, u32[]{:S(2)}) %all-to-all-start.2) | async-done | bytes 2359328 | tf_op jit(solution)/shard_map/all_to_all | solution.py:31
  285.7 0.0 copy-start.9
  285.7 6.3 %all-to-all-start.3 = ((bf16[64,24,2048]{2,1,0:T(8,128)(2,1)}), bf16[64,24,2048]{2,1,0:T(8,128)(2,1)}, u32[]{:S(2)}, u32[]{:S(2)}) async-start(bf16[64,24,2048]{2,1,0:T(8,128)(2,1)} %bitcast.25), calls=%async_computation.3 | async-start | bytes 12582912 | tf_op jit(solution)/shard_map/all_to_all | solution.py:31
  292.0 0.0 copy-done.9
  292.0 8.1 %select_reduce_fusion = bf16[1536,128]{1,0:T(8,128)(2,1)S(1)} fusion(f32[8,128]{1,0:T(8,128)S(1)} %divide_bitcast_fusion, s32[8,128]{1,0:T(8,128)S(1)} %add_bitcast_fusion), kind=kLoop, calls=%fused_computation.3 | loop fusion | flops 4521984 | bytes 401408 | tf_op jit(solution)/shard_map/reduce_sum | solution.py:79
  300.2 0.0 copy-start.1
  300.2 3.7 reshape.53
  303.9 2.7 slice.81
  306.6 2.1 slice_bitcast_fusion
  308.7 124.1 %all-to-all-done.3 = bf16[64,24,2048]{2,1,0:T(8,128)(2,1)} async-done(((bf16[64,24,2048]{2,1,0:T(8,128)(2,1)}), bf16[64,24,2048]{2,1,0:T(8,128)(2,1)}, u32[]{:S(2)}, u32[]{:S(2)}) %all-to-all-start.3) | async-done | bytes 6291488 | tf_op jit(solution)/shard_map/all_to_all | solution.py:31
  432.8 4.6 %convolution_convert_fusion.2 = bf16[128,2048]{1,0:T(8,128)(2,1)} fusion(bf16[1536,2048]{1,0:T(8,128)(2,1)} %bitcast.9, bf16[1536,128]{1,0:T(8,128)(2,1)S(1)} %select_reduce_fusion), kind=kOutput, calls=%fused_computation.15 | convolution fusion | flops 805568512 | bytes 7208960 | tf_op jit(solution)/shard_map/dot_general | solution.py:80
  437.4 0.0 copy-done.1
  (5 shorter events, 0.1 us)
Async XLA Ops:
  0.6 24.9 %copy-start = (bf16[128,2048]{1,0:T(8,128)(2,1)S(1)}, bf16[128,2048]{1,0:T(8,128)(2,1)}, u32[]{:S(2)}) copy-start(bf16[128,2048]{1,0:T(8,128)(2,1)} %param.6) | copy-start | bytes 1572868
  0.6 18.9 %copy-start.10 = (s32[128,8]{0,1:T(8,128)S(1)}, s32[128,8]{0,1:T(8,128)}, u32[]{:S(2)}) copy-start(s32[128,8]{0,1:T(8,128)} %param.7) | copy-start | bytes 12292
  0.7 18.9 %copy-start.11 = (s32[64]{0:T(128)S(1)}, s32[64]{0:T(128)}, u32[]{:S(2)}) copy-start(s32[64]{0:T(128)} %param.9) | copy-start | bytes 772
  2.5 3.9 copy-start.2
  6.4 69.8 %all-to-all-start = ((bf16[64,24,768]{2,1,0:T(8,128)(2,1)}), bf16[64,24,768]{2,1,0:T(8,128)(2,1)S(1)}, u32[]{:S(2)}, u32[]{:S(2)}) async-start(bf16[64,24,768]{2,1,0:T(8,128)(2,1)} %reshape.48), calls=%async_computation | async-start | bytes 4718592 | tf_op jit(solution)/shard_map/all_to_all | solution.py:31
  76.2 147.0 %all-to-all-start.1 = ((bf16[64,24,2048]{2,1,0:T(8,128)(2,1)}), bf16[64,24,2048]{2,1,0:T(8,128)(2,1)}, u32[]{:S(2)}, u32[]{:S(2)}) async-start(bf16[64,24,2048]{2,1,0:T(8,128)(2,1)} %bitcast.24), calls=%async_computation.1 | async-start | bytes 12582912 | tf_op jit(solution)/shard_map/all_to_all | solution.py:31
  82.4 108.9 %copy-start.3 = (bf16[1,2,192,2048]{3,2,1,0:T(8,128)(2,1)S(1)}, bf16[1,2,192,2048]{3,2,1,0:T(8,128)(2,1)}, u32[]{:S(2)}) copy-start(bf16[1,2,192,2048]{3,2,1,0:T(8,128)(2,1)} %param.10) | copy-start | bytes 4718596
  82.4 53.9 %collective-permute-start = (bf16[576,2048]{1,0:T(8,128)(2,1)}, bf16[576,2048]{1,0:T(8,128)(2,1)S(1)}, u32[]{:S(2)}, u32[]{:S(2)}) collective-permute-start(bf16[576,2048]{1,0:T(8,128)(2,1)} %copy-done.2), channel_id=1, source_target_pairs={{0,64},{64,128},{128,192},{192,0},{1,65},{65,129},{129,193},{193,1... | collective-permute-start | bytes 7077896 | tf_op jit(solution)/shard_map/ppermute | solution.py:40
  83.7 104.2 %collective-permute-start.1 = (bf16[576,2048]{1,0:T(8,128)(2,1)}, bf16[576,2048]{1,0:T(8,128)(2,1)S(1)}, u32[]{:S(2)}, u32[]{:S(2)}) collective-permute-start(bf16[576,2048]{1,0:T(8,128)(2,1)} %copy-done.2), channel_id=1, source_target_pairs={{0,128},{64,192},{128,0},{192,64},{1,129},{65,193},{129,1},{193,65... | collective-permute-start | bytes 7077896 | tf_op jit(solution)/shard_map/ppermute | solution.py:40
  86.1 102.7 %collective-permute-start.2 = (bf16[576,2048]{1,0:T(8,128)(2,1)}, bf16[576,2048]{1,0:T(8,128)(2,1)S(1)}, u32[]{:S(2)}, u32[]{:S(2)}) collective-permute-start(bf16[576,2048]{1,0:T(8,128)(2,1)} %copy-done.2), channel_id=1, source_target_pairs={{0,192},{64,0},{128,64},{192,128},{1,193},{65,1},{129,65},{193,129... | collective-permute-start | bytes 7077896 | tf_op jit(solution)/shard_map/ppermute | solution.py:40
  136.3 55.0 %copy-start.7 = (bf16[576,2048]{1,0:T(8,128)(2,1)}, bf16[576,2048]{1,0:T(8,128)(2,1)S(1)}, u32[]{:S(2)}) copy-start(bf16[576,2048]{1,0:T(8,128)(2,1)S(1)} %collective-permute-done) | copy-start | bytes 7077892
  187.8 3.4 copy-start.6
  188.9 1.4 copy-start.4
  223.2 62.4 %all-to-all-start.2 = ((bf16[64,24,768]{2,1,0:T(8,128)(2,1)}), bf16[64,24,768]{2,1,0:T(8,128)(2,1)S(1)}, u32[]{:S(2)}, u32[]{:S(2)}) async-start(bf16[64,24,768]{2,1,0:T(8,128)(2,1)} %gather_fusion), calls=%async_computation.2 | async-start | bytes 4718592 | tf_op jit(solution)/shard_map/all_to_all | solution.py:31
  229.0 4.9 %copy-start.5 = (bf16[576,2048]{1,0:T(8,128)(2,1)S(1)}, bf16[576,2048]{1,0:T(8,128)(2,1)}, u32[]{:S(2)}) copy-start(bf16[576,2048]{1,0:T(8,128)(2,1)} %copy-done.4) | copy-start | bytes 7077892
  235.0 15.8 %copy-start.8 = (bf16[1,192,2048]{2,1,0:T(8,128)(2,1)S(1)}, bf16[1,192,2048]{2,1,0:T(8,128)(2,1)}, u32[]{:S(2)}) copy-start(bf16[1,192,2048]{2,1,0:T(8,128)(2,1)} %param.11) | copy-start | bytes 2359300
  285.7 6.3 %copy-start.9 = (f32[128,8]{0,1:T(8,128)S(1)}, f32[128,8]{0,1:T(8,128)}, u32[]{:S(2)}) copy-start(f32[128,8]{0,1:T(8,128)} %param.8) | copy-start | bytes 12292
  285.7 147.1 %all-to-all-start.3 = ((bf16[64,24,2048]{2,1,0:T(8,128)(2,1)}), bf16[64,24,2048]{2,1,0:T(8,128)(2,1)}, u32[]{:S(2)}, u32[]{:S(2)}) async-start(bf16[64,24,2048]{2,1,0:T(8,128)(2,1)} %bitcast.25), calls=%async_computation.3 | async-start | bytes 12582912 | tf_op jit(solution)/shard_map/all_to_all | solution.py:31
  300.2 137.2 %copy-start.1 = (bf16[128,2048]{1,0:T(8,128)(2,1)S(1)}, bf16[128,2048]{1,0:T(8,128)(2,1)}, u32[]{:S(2)}) copy-start(bf16[128,2048]{1,0:T(8,128)(2,1)} %param.6) | copy-start | bytes 1572868

commit v10 on v7

--- a/solution.py
+++ b/solution.py
@@ -33,7 +33,9 @@
     gate_rows = w_gate_up.reshape(-1, model_width)
     down_rows = w_down.reshape(-1, model_width)
     shard = jnp.concatenate([gate_rows, down_rows], axis=0)
-    spread = exchange(shard.reshape(experts, capacity, -1))
+    sub, lane = 8, 128
+    tiled = shard.reshape(shard.shape[0] // sub, sub, model_width // lane, lane).transpose(0, 2, 1, 3)
+    spread = exchange(tiled.reshape(experts, -1, sub, lane))
 
     ring = lax.psum(1, "dp")
     parts = [shard] + [
@@ -70,7 +72,7 @@
     placed_rows, result = lax.optimization_barrier((placed_rows, result))
     returned = exchange(result)
 
-    placed_rows = placed_rows.reshape(-1, model_width)
+    placed_rows = placed_rows.reshape(tiled.shape).transpose(0, 2, 1, 3).reshape(-1, model_width)
     gate_count = gate_rows.shape[0]
     placed_gate_up = placed_rows[:gate_count].reshape(w_gate_up.shape)
     placed_down = placed_rows[gate_count:].reshape(w_down.shape)

time: 439 us -> 437 us (level)
  local copies, waits for them, and re-layouts: 28.1 us -> 18 us
  waiting for transfers between devices: 320 us -> 326 us
    reshape x2 -> x0, local copies, waits for them, and re-layouts: 7.55 us -> none  [the longest x1 3.85 us: per_device(): spread = exchange(shard.reshape(experts, capacity, -1))]
    all_to_all x4, waiting for transfers between devices: 222 us -> 229 us  [exchange(): lax.all_to_all(block, 'expert', split_axis=0, concat_axis=0, tiled=True)]
    unnamed x31 -> x29, local copies, waits for them, and re-layouts: 12.6 us -> 12.5 us
  transfers between devices with their start and end apart: 7 -> 7, of which waited for: 6 -> 6; matrix products, arithmetic and copies ran while one was open for 16% -> 14% of each run, Pallas kernels for 0% -> 0%
where the time goes in v10:
time: 437 us; the launch traced here: 436 us
  waiting for transfers between devices  326 us (75%)
  starting transfers between devices  36.3 us (8%)
  matrix products  36 us (8%)
  other arithmetic  19.2 us (4%)
  local copies, waits for them, and re-layouts  18 us (4%)
    all_to_all x4, waiting for transfers between devices, exchange(): lax.all_to_all(block, 'expert', split_axis=0, concat_axis=0, tiled=True)  229 us
    ppermute x3, waiting for transfers between devices, per_device(): lax.ppermute(shard, 'dp', [(j, (j + shift) % ring) for j in range(ring)])  97.3 us
    all_to_all x4, starting transfers between devices, exchange(): lax.all_to_all(block, 'expert', split_axis=0, concat_axis=0, tiled=True)  31.4 us
    dot_general x1, matrix products, per_device(): lax.dot_general(row_block, gate_up_full, (((1,), (1,)), ((), ())), prefer...  15.8 us
    unnamed x29, local copies, waits for them, and re-layouts  12.5 us
    dot_general x1, matrix products, per_device(): jnp.dot(hidden, down_full, preferred_element_type=jnp.float32)  10.9 us
  transfers between devices with their start and end apart: 7, of which 6 were waited for; matrix products, arithmetic and copies ran while one was open for 14% of the time, Pallas kernels for 0%

profile of v10, /device:TPU:1, one launch (start us, length us, event | category | flops | bytes accessed | tf_op | source)
XLA Modules:
  0.0 436.2 jit_solution(417839701576812328)
XLA Ops:
  0.6 0.0 copy-start
  0.6 0.0 copy-start.9
  0.7 0.0 copy-start.10
  0.7 3.4 pad_maximum_fusion
  4.1 13.2 %all-to-all-start = ((bf16[64,18,8,128]{3,2,1,0:T(8,128)(2,1)}), bf16[64,18,8,128]{3,2,1,0:T(8,128)(2,1)S(1)}, u32[]{:S(2)}, u32[]{:S(2)}) async-start(bf16[64,18,8,128]{3,2,1,0:T(8,128)(2,1)} %bitcast.37), calls=%async_computation | async-start | bytes 4718592 | tf_op jit(solution)/shard_map/all_to_all | solution.py:31
  17.3 0.0 copy-done.9
  17.3 0.0 copy-done.10
  17.3 0.1 select_reduce_fusion.2
  17.4 0.1 fusion.17
  17.6 0.1 select_reduce_fusion.1
  17.7 5.6 %fusion = pred[1536,128]{1,0:T(8,128)(4,1)S(1)} fusion(s32[8,128]{1,0:T(8,128)S(1)} %add_bitcast_fusion), kind=kLoop, calls=%fused_computation.5 | loop fusion | flops 2949120 | bytes 200704 | tf_op jit(solution)/shard_map/reduce_or | solution.py:28
  23.2 0.0 copy-done
  23.2 4.4 %convolution_convert_fusion.1 = bf16[1536,2048]{1,0:T(8,128)(2,1)} fusion(pred[1536,128]{1,0:T(8,128)(4,1)S(1)} %fusion, bf16[128,2048]{1,0:T(8,128)(2,1)S(1)} %copy-done), kind=kOutput, calls=%fused_computation.2 | convolution fusion | flops 808452096 | bytes 7012352 | tf_op jit(solution)/shard_map/dot_general | solution.py:53
  27.7 46.2 %all-to-all-done = bf16[64,18,8,128]{3,2,1,0:T(8,128)(2,1)S(1)} async-done(((bf16[64,18,8,128]{3,2,1,0:T(8,128)(2,1)}), bf16[64,18,8,128]{3,2,1,0:T(8,128)(2,1)S(1)}, u32[]{:S(2)}, u32[]{:S(2)}) %all-to-all-start) | async-done | bytes 2359328 | tf_op jit(solution)/shard_map/all_to_all | solution.py:31
  73.9 6.2 %all-to-all-start.1 = ((bf16[64,24,2048]{2,1,0:T(8,128)(2,1)}), bf16[64,24,2048]{2,1,0:T(8,128)(2,1)}, u32[]{:S(2)}, u32[]{:S(2)}) async-start(bf16[64,24,2048]{2,1,0:T(8,128)(2,1)} %bitcast.34), calls=%async_computation.1 | async-start | bytes 12582912 | tf_op jit(solution)/shard_map/all_to_all | solution.py:31
  80.1 0.0 copy-start.2
  80.1 1.3 collective-permute-start
  81.4 2.5 collective-permute-start.1
  83.8 1.2 collective-permute-start.2
  85.0 0.1 select_reduce_fusion.3
  85.1 2.1 bitcast_dynamic-update-slice_fusion.1
  87.2 46.8 %collective-permute-done = bf16[576,2048]{1,0:T(8,128)(2,1)S(1)} collective-permute-done((bf16[576,2048]{1,0:T(8,128)(2,1)}, bf16[576,2048]{1,0:T(8,128)(2,1)S(1)}, u32[]{:S(2)}, u32[]{:S(2)}) %collective-permute-start) | collective-permute-done | bytes 2359328 | tf_op jit(solution)/shard_map/ppermute | solution.py:42
  134.0 0.0 copy-start.6
  134.0 1.0 slice_dynamic-update-slice_fusion.5
  135.0 50.5 %collective-permute-done.1 = bf16[576,2048]{1,0:T(8,128)(2,1)S(1)} collective-permute-done((bf16[576,2048]{1,0:T(8,128)(2,1)}, bf16[576,2048]{1,0:T(8,128)(2,1)S(1)}, u32[]{:S(2)}, u32[]{:S(2)}) %collective-permute-start.1) | collective-permute-done | bytes 2359328 | tf_op jit(solution)/shard_map/ppermute | solution.py:42
  185.5 0.0 copy-start.5
  185.5 1.0 slice_dynamic-update-slice_fusion.4
  186.6 0.0 collective-permute-done.2
  186.6 0.0 copy-start.3
  186.6 1.4 copy-done.3
  188.0 1.0 slice_dynamic-update-slice_fusion.3
  188.9 0.0 copy-done.6
  188.9 0.0 copy-done.5
  189.0 0.0 copy-done.2
  189.0 1.0 bitcast_dynamic-update-slice_fusion
  189.9 2.3 gather_fusion
  192.2 28.7 %all-to-all-done.1 = bf16[64,24,2048]{2,1,0:T(8,128)(2,1)} async-done(((bf16[64,24,2048]{2,1,0:T(8,128)(2,1)}), bf16[64,24,2048]{2,1,0:T(8,128)(2,1)}, u32[]{:S(2)}, u32[]{:S(2)}) %all-to-all-start.1) | async-done | bytes 6291488 | tf_op jit(solution)/shard_map/all_to_all | solution.py:31
  220.9 5.8 %all-to-all-start.2 = ((bf16[64,18,8,128]{3,2,1,0:T(8,128)(2,1)}), bf16[64,18,8,128]{3,2,1,0:T(8,128)(2,1)S(1)}, u32[]{:S(2)}, u32[]{:S(2)}) async-start(bf16[64,18,8,128]{3,2,1,0:T(8,128)(2,1)} %gather_fusion), calls=%async_computation.2 | async-start | bytes 4718592 | tf_op jit(solution)/shard_map/all_to_all | solution.py:31
  226.7 0.0 copy-start.4
  226.7 2.5 slice_dynamic-update-slice_fusion.2
  229.3 2.4 slice_dynamic-update-slice_fusion.1
  231.7 0.0 copy-done.4
  231.7 1.0 slice_dynamic-update-slice_fusion
  232.7 0.0 copy-start.7
  232.7 15.8 %fusion.21 = f32[1536,1536]{1,0:T(8,128)} fusion(bf16[1536,2048]{1,0:T(8,128)(2,1)} %bitcast.9, bf16[1536,2048]{1,0:T(8,128)(2,1)} %get-tuple-element.15), kind=kOutput, calls=%fused_computation.49 | convolution fusion | flops 9663676416 | bytes 22020096 | tf_op jit(solution)/shard_map/dot_general | solution.py:64
  248.5 0.0 copy-done.7
  248.5 10.9 %convolution_convert_fusion = bf16[1536,2048]{1,0:T(8,128)(2,1)} fusion(bf16[192,2048]{1,0:T(8,128)(2,1)S(1)} %get-tuple-element.16, bf16[192,2048]{1,0:T(8,128)(2,1)S(1)} %get-tuple-element.18, bf16[192,2048]{1,0:T(8,128)(2,1)S(1)} %get-tuple-element.20, bf16[192,2048]{1,0:T(8,128)(2,1)S(1)} %bitcast.42, f32[1536,1536]{1,0:T(8,128)} %fusion.21), kind=kOutput, calls=%fused_computation.1 | convolution fusion | flops 4854644736 | bytes 18874368 | tf_op jit(solution)/shard_map/dot_general | solution.py:70
  259.4 24.0 %all-to-all-done.2 = bf16[64,18,8,128]{3,2,1,0:T(8,128)(2,1)S(1)} async-done(((bf16[64,18,8,128]{3,2,1,0:T(8,128)(2,1)}), bf16[64,18,8,128]{3,2,1,0:T(8,128)(2,1)S(1)}, u32[]{:S(2)}, u32[]{:S(2)}) %all-to-all-start.2) | async-done | bytes 2359328 | tf_op jit(solution)/shard_map/all_to_all | solution.py:31
  283.4 0.0 copy-start.8
  283.4 6.3 %all-to-all-start.3 = ((bf16[64,24,2048]{2,1,0:T(8,128)(2,1)}), bf16[64,24,2048]{2,1,0:T(8,128)(2,1)}, u32[]{:S(2)}, u32[]{:S(2)}) async-start(bf16[64,24,2048]{2,1,0:T(8,128)(2,1)} %bitcast.38), calls=%async_computation.3 | async-start | bytes 12582912 | tf_op jit(solution)/shard_map/all_to_all | solution.py:31
  289.7 0.0 copy-done.8
  289.7 8.1 %select_reduce_fusion = f32[1536,128]{1,0:T(8,128)S(1)} fusion(f32[8,128]{1,0:T(8,128)S(1)} %divide_bitcast_fusion, s32[8,128]{1,0:T(8,128)S(1)} %add_bitcast_fusion), kind=kLoop, calls=%fused_computation.3 | loop fusion | flops 4521984 | bytes 794624 | tf_op jit(solution)/shard_map/reduce_sum | solution.py:81
  297.8 0.9 reduce-precision_convert_fusion
  298.7 1.2 slice.93
  300.0 0.9 slice_bitcast_fusion
  300.9 129.6 %all-to-all-done.3 = bf16[64,24,2048]{2,1,0:T(8,128)(2,1)} async-done(((bf16[64,24,2048]{2,1,0:T(8,128)(2,1)}), bf16[64,24,2048]{2,1,0:T(8,128)(2,1)}, u32[]{:S(2)}, u32[]{:S(2)}) %all-to-all-start.3) | async-done | bytes 6291488 | tf_op jit(solution)/shard_map/all_to_all | solution.py:31
  430.5 0.0 copy-start.1
  430.5 4.8 %fusion.13 = f32[256,2048]{1,0:T(8,128)S(1)} fusion(bf16[1536,2048]{1,0:T(8,128)(2,1)} %bitcast.13, bf16[128,1536]{0,1:T(8,128)(2,1)} %get-tuple-element.22, bf16[128,1536]{0,1:T(8,128)(2,1)S(1)} %get-tuple-element.21), kind=kOutput, calls=%fused_computation.29 | convolution fusion | flops 1612185600 | bytes 9175040 | tf_op jit(solution)/shard_map/dot_general | solution.py:85
  435.3 0.9 fusion.11
  436.2 0.0 copy-done.1
  (5 shorter events, 0.1 us)
Async XLA Ops:
  0.6 22.6 %copy-start = (bf16[128,2048]{1,0:T(8,128)(2,1)S(1)}, bf16[128,2048]{1,0:T(8,128)(2,1)}, u32[]{:S(2)}) copy-start(bf16[128,2048]{1,0:T(8,128)(2,1)} %param.6) | copy-start | bytes 1572868
  0.6 16.6 %copy-start.9 = (s32[128,8]{0,1:T(8,128)S(1)}, s32[128,8]{0,1:T(8,128)}, u32[]{:S(2)}) copy-start(s32[128,8]{0,1:T(8,128)} %param.7) | copy-start | bytes 12292
  0.7 16.6 %copy-start.10 = (s32[64]{0:T(128)S(1)}, s32[64]{0:T(128)}, u32[]{:S(2)}) copy-start(s32[64]{0:T(128)} %param.9) | copy-start | bytes 772
  4.1 69.8 %all-to-all-start = ((bf16[64,18,8,128]{3,2,1,0:T(8,128)(2,1)}), bf16[64,18,8,128]{3,2,1,0:T(8,128)(2,1)S(1)}, u32[]{:S(2)}, u32[]{:S(2)}) async-start(bf16[64,18,8,128]{3,2,1,0:T(8,128)(2,1)} %bitcast.37), calls=%async_computation | async-start | bytes 4718592 | tf_op jit(solution)/shard_map/all_to_all | solution.py:31
  73.9 147.0 %all-to-all-start.1 = ((bf16[64,24,2048]{2,1,0:T(8,128)(2,1)}), bf16[64,24,2048]{2,1,0:T(8,128)(2,1)}, u32[]{:S(2)}, u32[]{:S(2)}) async-start(bf16[64,24,2048]{2,1,0:T(8,128)(2,1)} %bitcast.34), calls=%async_computation.1 | async-start | bytes 12582912 | tf_op jit(solution)/shard_map/all_to_all | solution.py:31
  80.1 108.9 %copy-start.2 = (bf16[1,2,192,2048]{3,2,1,0:T(8,128)(2,1)S(1)}, bf16[1,2,192,2048]{3,2,1,0:T(8,128)(2,1)}, u32[]{:S(2)}) copy-start(bf16[1,2,192,2048]{3,2,1,0:T(8,128)(2,1)} %param.10) | copy-start | bytes 4718596
  80.1 53.9 %collective-permute-start = (bf16[576,2048]{1,0:T(8,128)(2,1)}, bf16[576,2048]{1,0:T(8,128)(2,1)S(1)}, u32[]{:S(2)}, u32[]{:S(2)}) collective-permute-start(bf16[576,2048]{1,0:T(8,128)(2,1)} %pad_maximum_fusion), channel_id=1, source_target_pairs={{0,64},{64,128},{128,192},{192,0},{1,65},{65,129},{129,193},{193,1... | collective-permute-start | bytes 7077896 | tf_op jit(solution)/shard_map/ppermute | solution.py:42
  81.4 104.2 %collective-permute-start.1 = (bf16[576,2048]{1,0:T(8,128)(2,1)}, bf16[576,2048]{1,0:T(8,128)(2,1)S(1)}, u32[]{:S(2)}, u32[]{:S(2)}) collective-permute-start(bf16[576,2048]{1,0:T(8,128)(2,1)} %pad_maximum_fusion), channel_id=1, source_target_pairs={{0,128},{64,192},{128,0},{192,64},{1,129},{65,193},{129,1},{193,65... | collective-permute-start | bytes 7077896 | tf_op jit(solution)/shard_map/ppermute | solution.py:42
  83.8 102.7 %collective-permute-start.2 = (bf16[576,2048]{1,0:T(8,128)(2,1)}, bf16[576,2048]{1,0:T(8,128)(2,1)S(1)}, u32[]{:S(2)}, u32[]{:S(2)}) collective-permute-start(bf16[576,2048]{1,0:T(8,128)(2,1)} %pad_maximum_fusion), channel_id=1, source_target_pairs={{0,192},{64,0},{128,64},{192,128},{1,193},{65,1},{129,65},{193,129... | collective-permute-start | bytes 7077896 | tf_op jit(solution)/shard_map/ppermute | solution.py:42
  134.0 55.0 %copy-start.6 = (bf16[576,2048]{1,0:T(8,128)(2,1)}, bf16[576,2048]{1,0:T(8,128)(2,1)S(1)}, u32[]{:S(2)}) copy-start(bf16[576,2048]{1,0:T(8,128)(2,1)S(1)} %collective-permute-done) | copy-start | bytes 7077892
  185.5 3.4 copy-start.5
  186.6 1.4 copy-start.3
  220.9 62.4 %all-to-all-start.2 = ((bf16[64,18,8,128]{3,2,1,0:T(8,128)(2,1)}), bf16[64,18,8,128]{3,2,1,0:T(8,128)(2,1)S(1)}, u32[]{:S(2)}, u32[]{:S(2)}) async-start(bf16[64,18,8,128]{3,2,1,0:T(8,128)(2,1)} %gather_fusion), calls=%async_computation.2 | async-start | bytes 4718592 | tf_op jit(solution)/shard_map/all_to_all | solution.py:31
  226.7 4.9 %copy-start.4 = (bf16[576,2048]{1,0:T(8,128)(2,1)S(1)}, bf16[576,2048]{1,0:T(8,128)(2,1)}, u32[]{:S(2)}) copy-start(bf16[576,2048]{1,0:T(8,128)(2,1)} %copy-done.3) | copy-start | bytes 7077892
  232.7 15.8 %copy-start.7 = (bf16[1,192,2048]{2,1,0:T(8,128)(2,1)S(1)}, bf16[1,192,2048]{2,1,0:T(8,128)(2,1)}, u32[]{:S(2)}) copy-start(bf16[1,192,2048]{2,1,0:T(8,128)(2,1)} %param.11) | copy-start | bytes 2359300
  283.4 6.3 %copy-start.8 = (f32[128,8]{0,1:T(8,128)S(1)}, f32[128,8]{0,1:T(8,128)}, u32[]{:S(2)}) copy-start(f32[128,8]{0,1:T(8,128)} %param.8) | copy-start | bytes 12292
  283.4 147.1 %all-to-all-start.3 = ((bf16[64,24,2048]{2,1,0:T(8,128)(2,1)}), bf16[64,24,2048]{2,1,0:T(8,128)(2,1)}, u32[]{:S(2)}, u32[]{:S(2)}) async-start(bf16[64,24,2048]{2,1,0:T(8,128)(2,1)} %bitcast.38), calls=%async_computation.3 | async-start | bytes 12582912 | tf_op jit(solution)/shard_map/all_to_all | solution.py:31
  430.5 5.7 %copy-start.1 = (bf16[128,2048]{1,0:T(8,128)(2,1)S(1)}, bf16[128,2048]{1,0:T(8,128)(2,1)}, u32[]{:S(2)}) copy-start(bf16[128,2048]{1,0:T(8,128)(2,1)} %param.6) | copy-start | bytes 1572868

commit v11 on v10

--- a/solution.py
+++ b/solution.py
@@ -2,6 +2,8 @@
 import jax.numpy as jnp
 from jax import lax
 from jax.sharding import PartitionSpec as P
+from jax.experimental import pallas as pl
+from jax.experimental.pallas import tpu as pltpu
 
 
 def per_device(tokens, expert_ids, gate_probs, placement, w_gate_up, w_down):
@@ -82,13 +84,37 @@
     rounded = lax.reduce_precision(part, exponent_bits=8, mantissa_bits=7)
     part_hi = rounded.astype(jnp.bfloat16)
     part_lo = (part - rounded).astype(jnp.bfloat16)
-    both = jnp.dot(
-        jnp.concatenate([part_hi, part_lo], axis=0),
-        returned.reshape(slots, model_width),
-        preferred_element_type=jnp.float32,
-    )
-    mixed_rows = both[:tok_dev] + both[tok_dev:]
-    return (mixed_rows.astype(jnp.bfloat16), placed_gate_up, placed_down)
+    mixed_rows = combine(part_hi, part_lo, returned.reshape(slots, model_width))
+    return (mixed_rows, placed_gate_up, placed_down)
+
+
+def combine_kernel(hi_ref, lo_ref, rows_ref, out_ref):
+    rows = rows_ref[...]
+    total = jnp.dot(hi_ref[...], rows, preferred_element_type=jnp.float32)
+    total = total + jnp.dot(lo_ref[...], rows, preferred_element_type=jnp.float32)
+    out_ref[...] = total.astype(out_ref.dtype)
+
+
+def combine(hi, lo, rows):
+    count, depth = hi.shape
+    width = rows.shape[1]
+    block = 512
+    return pl.pallas_call(
+        combine_kernel,
+        out_shape=jax.ShapeDtypeStruct((count, width), jnp.bfloat16),
+        grid=(width // block,),
+        in_specs=[
+            pl.BlockSpec((count, depth), lambda j: (0, 0)),
+            pl.BlockSpec((count, depth), lambda j: (0, 0)),
+            pl.BlockSpec((depth, block), lambda j: (0, j)),
+        ],
+        out_specs=pl.BlockSpec((count, block), lambda j: (0, j)),
+        cost_estimate=pl.CostEstimate(
+            flops=4 * count * depth * width,
+            bytes_accessed=2 * (2 * count * depth + depth * width + count * width),
+            transcendentals=0,
+        ),
+    )(hi, lo, rows)
 
 
 def solution(mesh):

time: 437 us -> 437 us (level)
  Pallas kernels: 0 us -> 5.61 us
  waiting for transfers between devices: 326 us -> 321 us
  matrix products: 36 us -> 31.3 us
    pallas_call x0 -> x1, Pallas kernels: none -> 5.61 us  [combine(): pl.pallas_call(combine_kernel, out_shape=jax.ShapeDtypeStruct((count, wid...]
    dot_general x1 -> x0, matrix products: 4.78 us -> none  [per_device(): jnp.dot(jnp.concatenate([part_hi, part_lo], axis=0), returned.reshape(slo...]
    all_to_all x4, waiting for transfers between devices: 229 us -> 224 us  [exchange(): lax.all_to_all(block, 'expert', split_axis=0, concat_axis=0, tiled=True)]
  transfers between devices with their start and end apart: 7 -> 7, of which waited for: 6 -> 6; matrix products, arithmetic and copies ran while one was open for 14% -> 15% of each run, Pallas kernels for 0% -> 0%
where the time goes in v11:
time: 437 us; the launch traced here: 436 us
  waiting for transfers between devices  321 us (73%)
  starting transfers between devices  36.3 us (8%)
  matrix products  31.3 us (7%)
  other arithmetic  20.5 us (5%)
  local copies, waits for them, and re-layouts  20.3 us (5%)
  Pallas kernels  5.61 us (1%)
    all_to_all x4, waiting for transfers between devices, exchange(): lax.all_to_all(block, 'expert', split_axis=0, concat_axis=0, tiled=True)  224 us
    ppermute x3, waiting for transfers between devices, per_device(): lax.ppermute(shard, 'dp', [(j, (j + shift) % ring) for j in range(ring)])  97.3 us
    all_to_all x4, starting transfers between devices, exchange(): lax.all_to_all(block, 'expert', split_axis=0, concat_axis=0, tiled=True)  31.4 us
    dot_general x1, matrix products, per_device(): lax.dot_general(row_block, gate_up_full, (((1,), (1,)), ((), ())), prefer...  15.8 us
    unnamed x29, local copies, waits for them, and re-layouts  12.5 us
    dot_general x1, matrix products, per_device(): jnp.dot(hidden, down_full, preferred_element_type=jnp.float32)  10.9 us
    reduce_sum x1, other arithmetic, per_device(): part = jnp.sum(jnp.where(hits, gates.T[None, :, :], 0.0), axis=1).T  8.99 us
  transfers between devices with their start and end apart: 7, of which 6 were waited for; matrix products, arithmetic and copies ran while one was open for 15% of the time, Pallas kernels for 0%

profile of v11, /device:TPU:1, one launch (start us, length us, event | category | flops | bytes accessed | tf_op | source)
XLA Modules:
  0.0 436.1 jit_solution(15576595545473852635)
XLA Ops:
  0.6 0.0 copy-start
  0.6 0.0 copy-start.9
  0.7 0.0 copy-start.10
  0.7 3.4 pad_maximum_fusion
  4.1 13.2 %all-to-all-start = ((bf16[64,18,8,128]{3,2,1,0:T(8,128)(2,1)}), bf16[64,18,8,128]{3,2,1,0:T(8,128)(2,1)S(1)}, u32[]{:S(2)}, u32[]{:S(2)}) async-start(bf16[64,18,8,128]{3,2,1,0:T(8,128)(2,1)} %bitcast.36), calls=%async_computation | async-start | bytes 4718592 | tf_op jit(solution)/shard_map/all_to_all | solution.py:33
  17.3 0.0 copy-done.9
  17.3 0.0 copy-done.10
  17.3 0.1 select_reduce_fusion.2
  17.4 0.1 fusion.12
  17.6 0.1 select_reduce_fusion.1
  17.7 5.6 %fusion = pred[1536,128]{1,0:T(8,128)(4,1)S(1)} fusion(s32[8,128]{1,0:T(8,128)S(1)} %add_bitcast_fusion), kind=kLoop, calls=%fused_computation.5 | loop fusion | flops 2949120 | bytes 200704 | tf_op jit(solution)/shard_map/reduce_or | solution.py:30
  23.2 0.0 copy-done
  23.2 4.4 %convolution_convert_fusion.1 = bf16[1536,2048]{1,0:T(8,128)(2,1)} fusion(pred[1536,128]{1,0:T(8,128)(4,1)S(1)} %fusion, bf16[128,2048]{1,0:T(8,128)(2,1)S(1)} %copy-done), kind=kOutput, calls=%fused_computation.2 | convolution fusion | flops 808452096 | bytes 7012352 | tf_op jit(solution)/shard_map/dot_general | solution.py:55
  27.7 46.2 %all-to-all-done = bf16[64,18,8,128]{3,2,1,0:T(8,128)(2,1)S(1)} async-done(((bf16[64,18,8,128]{3,2,1,0:T(8,128)(2,1)}), bf16[64,18,8,128]{3,2,1,0:T(8,128)(2,1)S(1)}, u32[]{:S(2)}, u32[]{:S(2)}) %all-to-all-start) | async-done | bytes 2359328 | tf_op jit(solution)/shard_map/all_to_all | solution.py:33
  73.9 6.2 %all-to-all-start.1 = ((bf16[64,24,2048]{2,1,0:T(8,128)(2,1)}), bf16[64,24,2048]{2,1,0:T(8,128)(2,1)}, u32[]{:S(2)}, u32[]{:S(2)}) async-start(bf16[64,24,2048]{2,1,0:T(8,128)(2,1)} %bitcast.33), calls=%async_computation.1 | async-start | bytes 12582912 | tf_op jit(solution)/shard_map/all_to_all | solution.py:33
  80.1 0.0 copy-start.2
  80.1 1.3 collective-permute-start
  81.4 2.5 collective-permute-start.1
  83.8 1.2 collective-permute-start.2
  85.0 0.1 select_reduce_fusion.3
  85.1 2.1 bitcast_dynamic-update-slice_fusion.1
  87.2 46.8 %collective-permute-done = bf16[576,2048]{1,0:T(8,128)(2,1)S(1)} collective-permute-done((bf16[576,2048]{1,0:T(8,128)(2,1)}, bf16[576,2048]{1,0:T(8,128)(2,1)S(1)}, u32[]{:S(2)}, u32[]{:S(2)}) %collective-permute-start) | collective-permute-done | bytes 2359328 | tf_op jit(solution)/shard_map/ppermute | solution.py:44
  134.0 0.0 copy-start.6
  134.0 1.0 slice_dynamic-update-slice_fusion.5
  135.0 50.5 %collective-permute-done.1 = bf16[576,2048]{1,0:T(8,128)(2,1)S(1)} collective-permute-done((bf16[576,2048]{1,0:T(8,128)(2,1)}, bf16[576,2048]{1,0:T(8,128)(2,1)S(1)}, u32[]{:S(2)}, u32[]{:S(2)}) %collective-permute-start.1) | collective-permute-done | bytes 2359328 | tf_op jit(solution)/shard_map/ppermute | solution.py:44
  185.5 0.0 copy-start.5
  185.5 1.0 slice_dynamic-update-slice_fusion.4
  186.6 0.0 collective-permute-done.2
  186.6 0.0 copy-start.3
  186.6 1.4 copy-done.3
  188.0 1.0 slice_dynamic-update-slice_fusion.3
  188.9 0.0 copy-done.6
  188.9 0.0 copy-done.5
  188.9 0.0 copy-done.2
  189.0 1.0 bitcast_dynamic-update-slice_fusion
  189.9 2.3 gather_fusion
  192.2 28.7 %all-to-all-done.1 = bf16[64,24,2048]{2,1,0:T(8,128)(2,1)} async-done(((bf16[64,24,2048]{2,1,0:T(8,128)(2,1)}), bf16[64,24,2048]{2,1,0:T(8,128)(2,1)}, u32[]{:S(2)}, u32[]{:S(2)}) %all-to-all-start.1) | async-done | bytes 6291488 | tf_op jit(solution)/shard_map/all_to_all | solution.py:33
  220.9 5.8 %all-to-all-start.2 = ((bf16[64,18,8,128]{3,2,1,0:T(8,128)(2,1)}), bf16[64,18,8,128]{3,2,1,0:T(8,128)(2,1)S(1)}, u32[]{:S(2)}, u32[]{:S(2)}) async-start(bf16[64,18,8,128]{3,2,1,0:T(8,128)(2,1)} %gather_fusion), calls=%async_computation.2 | async-start | bytes 4718592 | tf_op jit(solution)/shard_map/all_to_all | solution.py:33
  226.7 0.0 copy-start.4
  226.7 2.5 slice_dynamic-update-slice_fusion.2
  229.3 2.4 slice_dynamic-update-slice_fusion.1
  231.7 0.0 copy-done.4
  231.7 1.0 slice_dynamic-update-slice_fusion
  232.7 0.0 copy-start.7
  232.7 15.8 %fusion.15 = f32[1536,1536]{1,0:T(8,128)} fusion(bf16[1536,2048]{1,0:T(8,128)(2,1)} %bitcast.9, bf16[1536,2048]{1,0:T(8,128)(2,1)} %get-tuple-element.15), kind=kOutput, calls=%fused_computation.42 | convolution fusion | flops 9663676416 | bytes 22020096 | tf_op jit(solution)/shard_map/dot_general | solution.py:66
  248.5 0.0 copy-done.7
  248.5 10.9 %convolution_convert_fusion = bf16[1536,2048]{1,0:T(8,128)(2,1)} fusion(bf16[192,2048]{1,0:T(8,128)(2,1)S(1)} %get-tuple-element.16, bf16[192,2048]{1,0:T(8,128)(2,1)S(1)} %get-tuple-element.18, bf16[192,2048]{1,0:T(8,128)(2,1)S(1)} %get-tuple-element.20, bf16[192,2048]{1,0:T(8,128)(2,1)S(1)} %bitcast.41, f32[1536,1536]{1,0:T(8,128)} %fusion.15), kind=kOutput, calls=%fused_computation.1 | convolution fusion | flops 4854644736 | bytes 18874368 | tf_op jit(solution)/shard_map/dot_general | solution.py:72
  259.4 24.0 %all-to-all-done.2 = bf16[64,18,8,128]{3,2,1,0:T(8,128)(2,1)S(1)} async-done(((bf16[64,18,8,128]{3,2,1,0:T(8,128)(2,1)}), bf16[64,18,8,128]{3,2,1,0:T(8,128)(2,1)S(1)}, u32[]{:S(2)}, u32[]{:S(2)}) %all-to-all-start.2) | async-done | bytes 2359328 | tf_op jit(solution)/shard_map/all_to_all | solution.py:33
  283.4 0.0 copy-start.8
  283.4 6.3 %all-to-all-start.3 = ((bf16[64,24,2048]{2,1,0:T(8,128)(2,1)}), bf16[64,24,2048]{2,1,0:T(8,128)(2,1)}, u32[]{:S(2)}, u32[]{:S(2)}) async-start(bf16[64,24,2048]{2,1,0:T(8,128)(2,1)} %bitcast.37), calls=%async_computation.3 | async-start | bytes 12582912 | tf_op jit(solution)/shard_map/all_to_all | solution.py:33
  289.7 0.0 copy-done.8
  289.7 9.0 %select_reduce_fusion = f32[1536,128]{1,0:T(8,128)} fusion(f32[8,128]{1,0:T(8,128)S(1)} %divide_bitcast_fusion, s32[8,128]{1,0:T(8,128)S(1)} %add_bitcast_fusion), kind=kLoop, calls=%fused_computation.3 | loop fusion | flops 4521984 | bytes 794624 | tf_op jit(solution)/shard_map/reduce_sum | solution.py:83
  298.7 2.3 copy.12
  301.0 0.0 copy-start.1
  301.0 2.2 fusion.11
  303.1 1.2 slice.83
  304.4 0.9 slice_bitcast_fusion
  305.3 125.2 %all-to-all-done.3 = bf16[64,24,2048]{2,1,0:T(8,128)(2,1)} async-done(((bf16[64,24,2048]{2,1,0:T(8,128)(2,1)}), bf16[64,24,2048]{2,1,0:T(8,128)(2,1)}, u32[]{:S(2)}, u32[]{:S(2)}) %all-to-all-start.3) | async-done | bytes 6291488 | tf_op jit(solution)/shard_map/all_to_all | solution.py:33
  430.5 5.6 %shard_map.85 = bf16[128,2048]{1,0:T(8,128)(2,1)} custom-call(bf16[128,1536]{1,0:T(8,128)(2,1)} %get-tuple-element.22.hi_ref, bf16[128,1536]{1,0:T(8,128)(2,1)} %get-tuple-element.21.lo_ref, bf16[1536,2048]{1,0:T(8,128)(2,1)} %bitcast.13.rows_ref), custom_call_target="tpu_custom_call" | custom-call | flops 1610612736 | bytes 7602176 | tf_op jit(solution)/shard_map/pallas_call | solution.py:102
  436.1 0.0 copy-done.1
  (5 shorter events, 0.1 us)
Async XLA Ops:
  0.6 22.6 %copy-start = (bf16[128,2048]{1,0:T(8,128)(2,1)S(1)}, bf16[128,2048]{1,0:T(8,128)(2,1)}, u32[]{:S(2)}) copy-start(bf16[128,2048]{1,0:T(8,128)(2,1)} %param.6) | copy-start | bytes 1572868
  0.6 16.6 %copy-start.9 = (s32[128,8]{0,1:T(8,128)S(1)}, s32[128,8]{0,1:T(8,128)}, u32[]{:S(2)}) copy-start(s32[128,8]{0,1:T(8,128)} %param.7) | copy-start | bytes 12292
  0.7 16.6 %copy-start.10 = (s32[64]{0:T(128)S(1)}, s32[64]{0:T(128)}, u32[]{:S(2)}) copy-start(s32[64]{0:T(128)} %param.9) | copy-start | bytes 772
  4.1 69.8 %all-to-all-start = ((bf16[64,18,8,128]{3,2,1,0:T(8,128)(2,1)}), bf16[64,18,8,128]{3,2,1,0:T(8,128)(2,1)S(1)}, u32[]{:S(2)}, u32[]{:S(2)}) async-start(bf16[64,18,8,128]{3,2,1,0:T(8,128)(2,1)} %bitcast.36), calls=%async_computation | async-start | bytes 4718592 | tf_op jit(solution)/shard_map/all_to_all | solution.py:33
  73.9 147.0 %all-to-all-start.1 = ((bf16[64,24,2048]{2,1,0:T(8,128)(2,1)}), bf16[64,24,2048]{2,1,0:T(8,128)(2,1)}, u32[]{:S(2)}, u32[]{:S(2)}) async-start(bf16[64,24,2048]{2,1,0:T(8,128)(2,1)} %bitcast.33), calls=%async_computation.1 | async-start | bytes 12582912 | tf_op jit(solution)/shard_map/all_to_all | solution.py:33
  80.1 108.9 %copy-start.2 = (bf16[1,2,192,2048]{3,2,1,0:T(8,128)(2,1)S(1)}, bf16[1,2,192,2048]{3,2,1,0:T(8,128)(2,1)}, u32[]{:S(2)}) copy-start(bf16[1,2,192,2048]{3,2,1,0:T(8,128)(2,1)} %param.10) | copy-start | bytes 4718596
  80.1 53.9 %collective-permute-start = (bf16[576,2048]{1,0:T(8,128)(2,1)}, bf16[576,2048]{1,0:T(8,128)(2,1)S(1)}, u32[]{:S(2)}, u32[]{:S(2)}) collective-permute-start(bf16[576,2048]{1,0:T(8,128)(2,1)} %pad_maximum_fusion), channel_id=1, source_target_pairs={{0,64},{64,128},{128,192},{192,0},{1,65},{65,129},{129,193},{193,1... | collective-permute-start | bytes 7077896 | tf_op jit(solution)/shard_map/ppermute | solution.py:44
  81.4 104.2 %collective-permute-start.1 = (bf16[576,2048]{1,0:T(8,128)(2,1)}, bf16[576,2048]{1,0:T(8,128)(2,1)S(1)}, u32[]{:S(2)}, u32[]{:S(2)}) collective-permute-start(bf16[576,2048]{1,0:T(8,128)(2,1)} %pad_maximum_fusion), channel_id=1, source_target_pairs={{0,128},{64,192},{128,0},{192,64},{1,129},{65,193},{129,1},{193,65... | collective-permute-start | bytes 7077896 | tf_op jit(solution)/shard_map/ppermute | solution.py:44
  83.8 102.7 %collective-permute-start.2 = (bf16[576,2048]{1,0:T(8,128)(2,1)}, bf16[576,2048]{1,0:T(8,128)(2,1)S(1)}, u32[]{:S(2)}, u32[]{:S(2)}) collective-permute-start(bf16[576,2048]{1,0:T(8,128)(2,1)} %pad_maximum_fusion), channel_id=1, source_target_pairs={{0,192},{64,0},{128,64},{192,128},{1,193},{65,1},{129,65},{193,129... | collective-permute-start | bytes 7077896 | tf_op jit(solution)/shard_map/ppermute | solution.py:44
  134.0 55.0 %copy-start.6 = (bf16[576,2048]{1,0:T(8,128)(2,1)}, bf16[576,2048]{1,0:T(8,128)(2,1)S(1)}, u32[]{:S(2)}) copy-start(bf16[576,2048]{1,0:T(8,128)(2,1)S(1)} %collective-permute-done) | copy-start | bytes 7077892
  185.5 3.4 copy-start.5
  186.6 1.4 copy-start.3
  220.9 62.4 %all-to-all-start.2 = ((bf16[64,18,8,128]{3,2,1,0:T(8,128)(2,1)}), bf16[64,18,8,128]{3,2,1,0:T(8,128)(2,1)S(1)}, u32[]{:S(2)}, u32[]{:S(2)}) async-start(bf16[64,18,8,128]{3,2,1,0:T(8,128)(2,1)} %gather_fusion), calls=%async_computation.2 | async-start | bytes 4718592 | tf_op jit(solution)/shard_map/all_to_all | solution.py:33
  226.7 4.9 %copy-start.4 = (bf16[576,2048]{1,0:T(8,128)(2,1)S(1)}, bf16[576,2048]{1,0:T(8,128)(2,1)}, u32[]{:S(2)}) copy-start(bf16[576,2048]{1,0:T(8,128)(2,1)} %copy-done.3) | copy-start | bytes 7077892
  232.7 15.8 %copy-start.7 = (bf16[1,192,2048]{2,1,0:T(8,128)(2,1)S(1)}, bf16[1,192,2048]{2,1,0:T(8,128)(2,1)}, u32[]{:S(2)}) copy-start(bf16[1,192,2048]{2,1,0:T(8,128)(2,1)} %param.11) | copy-start | bytes 2359300
  283.4 6.3 %copy-start.8 = (f32[128,8]{0,1:T(8,128)S(1)}, f32[128,8]{0,1:T(8,128)}, u32[]{:S(2)}) copy-start(f32[128,8]{0,1:T(8,128)} %param.8) | copy-start | bytes 12292
  283.4 147.1 %all-to-all-start.3 = ((bf16[64,24,2048]{2,1,0:T(8,128)(2,1)}), bf16[64,24,2048]{2,1,0:T(8,128)(2,1)}, u32[]{:S(2)}, u32[]{:S(2)}) async-start(bf16[64,24,2048]{2,1,0:T(8,128)(2,1)} %bitcast.37), calls=%async_computation.3 | async-start | bytes 12582912 | tf_op jit(solution)/shard_map/all_to_all | solution.py:33
  301.0 135.2 %copy-start.1 = (bf16[128,2048]{1,0:T(8,128)(2,1)S(1)}, bf16[128,2048]{1,0:T(8,128)(2,1)}, u32[]{:S(2)}) copy-start(bf16[128,2048]{1,0:T(8,128)(2,1)} %param.6) | copy-start | bytes 1572868

commit v12 on v10

--- a/solution.py
+++ b/solution.py
@@ -42,6 +42,10 @@
         lax.ppermute(shard, "dp", [(j, (j + shift) % ring) for j in range(ring)])
         for shift in range(1, ring)
     ]
+    buffer = jnp.dot(pick, tokens, preferred_element_type=jnp.float32).astype(jnp.bfloat16)
+    buffer = buffer.reshape(experts, capacity, model_width)
+    spread, buffer, parts[1] = lax.optimization_barrier((spread, buffer, parts[1]))
+    received = exchange(buffer)
     local_count = w_down.shape[1]
     hidden_count = local_count * ring
     gate_up_full = jnp.concatenate(
@@ -50,10 +54,6 @@
     )
     down_full = jnp.concatenate([part[2 * local_count:] for part in parts], axis=0)
 
-    buffer = jnp.dot(pick, tokens, preferred_element_type=jnp.float32).astype(jnp.bfloat16)
-    buffer = buffer.reshape(experts, capacity, model_width)
-    spread, buffer = lax.optimization_barrier((spread, buffer))
-    received = exchange(buffer)
 
     inverse = jnp.sum(jnp.where(placement[:, None] == numbers[None, :], numbers[:, None], 0), axis=0)
     reordered = jnp.take(spread, inverse, axis=0, mode="clip")

time: 437 us -> 440 us (level)
    all_to_all x4, waiting for transfers between devices: 229 us -> 188 us  [exchange(): lax.all_to_all(block, 'expert', split_axis=0, concat_axis=0, tiled=True)]
    ppermute x3, waiting for transfers between devices: 97.3 us -> 135 us  [per_device(): lax.ppermute(shard, 'dp', [(j, (j + shift) % ring) for j in range(ring)])]
    unnamed x29 -> x19, local copies, waits for them, and re-layouts: 12.5 us -> 15.5 us
  transfers between devices with their start and end apart: 7 -> 7, of which waited for: 6 -> 7; matrix products, arithmetic and copies ran while one was open for 14% -> 16% of each run, Pallas kernels for 0% -> 0%
where the time goes in v12:
time: 440 us; the launch traced here: 439 us
  waiting for transfers between devices  323 us (73%)
  starting transfers between devices  37.8 us (9%)
  matrix products  36.1 us (8%)
  local copies, waits for them, and re-layouts  22.3 us (5%)
  other arithmetic  19.3 us (4%)
    all_to_all x4, waiting for transfers between devices, exchange(): lax.all_to_all(block, 'expert', split_axis=0, concat_axis=0, tiled=True)  188 us
    ppermute x3, waiting for transfers between devices, per_device(): lax.ppermute(shard, 'dp', [(j, (j + shift) % ring) for j in range(ring)])  135 us
    all_to_all x4, starting transfers between devices, exchange(): lax.all_to_all(block, 'expert', split_axis=0, concat_axis=0, tiled=True)  34 us
    dot_general x1, matrix products, per_device(): lax.dot_general(row_block, gate_up_full, (((1,), (1,)), ((), ())), prefer...  15.6 us
    unnamed x19, local copies, waits for them, and re-layouts  15.5 us
    dot_general x1, matrix products, per_device(): jnp.dot(hidden, down_full, preferred_element_type=jnp.float32)  11 us
  transfers between devices with their start and end apart: 7, of which 7 were waited for; matrix products, arithmetic and copies ran while one was open for 16% of the time, Pallas kernels for 0%

profile of v12, /device:TPU:1, one launch (start us, length us, event | category | flops | bytes accessed | tf_op | source)
XLA Modules:
  0.0 438.9 jit_solution(18279438757871441302)
XLA Ops:
  0.6 0.0 copy-start
  0.6 0.0 copy-start.4
  0.7 0.0 copy-start.5
  0.7 3.5 pad_maximum_fusion
  4.2 13.2 %all-to-all-start = ((bf16[64,18,8,128]{3,2,1,0:T(8,128)(2,1)}), bf16[64,18,8,128]{3,2,1,0:T(8,128)(2,1)S(1)}, u32[]{:S(2)}, u32[]{:S(2)}) async-start(bf16[64,18,8,128]{3,2,1,0:T(8,128)(2,1)} %bitcast.7), calls=%async_computation | async-start | bytes 4718592 | tf_op jit(solution)/shard_map/all_to_all | solution.py:31
  17.3 1.3 collective-permute-start
  18.6 0.0 copy-done.4
  18.6 0.0 copy-done.5
  18.6 0.1 select_reduce_fusion.2
  18.8 0.1 fusion.17
  18.9 0.1 select_reduce_fusion.1
  19.0 5.6 %fusion = pred[1536,128]{1,0:T(8,128)(4,1)S(1)} fusion(s32[8,128]{1,0:T(8,128)S(1)} %add_bitcast_fusion), kind=kLoop, calls=%fused_computation.5 | loop fusion | flops 2949120 | bytes 200704 | tf_op jit(solution)/shard_map/reduce_or | solution.py:28
  24.6 0.0 copy-done
  24.6 4.5 %convolution_convert_fusion.1 = bf16[1536,2048]{1,0:T(8,128)(2,1)} fusion(pred[1536,128]{1,0:T(8,128)(4,1)S(1)} %fusion, bf16[128,2048]{1,0:T(8,128)(2,1)S(1)} %copy-done), kind=kOutput, calls=%fused_computation.2 | convolution fusion | flops 808452096 | bytes 7012352 | tf_op jit(solution)/shard_map/dot_general | solution.py:45
  29.1 42.2 %collective-permute-done = bf16[576,2048]{1,0:T(8,128)(2,1)} collective-permute-done((bf16[576,2048]{1,0:T(8,128)(2,1)}, bf16[576,2048]{1,0:T(8,128)(2,1)}, u32[]{:S(2)}, u32[]{:S(2)}) %collective-permute-start) | collective-permute-done | bytes 2359328 | tf_op jit(solution)/shard_map/ppermute | solution.py:42
  71.3 2.7 all-to-all-done
  74.0 8.8 %all-to-all-start.1 = ((bf16[64,24,2048]{2,1,0:T(8,128)(2,1)}), bf16[64,24,2048]{2,1,0:T(8,128)(2,1)}, u32[]{:S(2)}, u32[]{:S(2)}) async-start(bf16[64,24,2048]{2,1,0:T(8,128)(2,1)} %bitcast.34), calls=%async_computation.1 | async-start | bytes 12582912 | tf_op jit(solution)/shard_map/all_to_all | solution.py:31
  82.8 1.6 collective-permute-start.1
  84.4 0.9 collective-permute-start.2
  85.2 0.1 select_reduce_fusion.3
  85.3 2.2 bitcast_dynamic-update-slice_fusion.1
  87.5 2.3 gather_fusion
  89.8 2.1 slice_dynamic-update-slice_fusion.5
  91.9 45.0 %collective-permute-done.1 = bf16[576,2048]{1,0:T(8,128)(2,1)} collective-permute-done((bf16[576,2048]{1,0:T(8,128)(2,1)}, bf16[576,2048]{1,0:T(8,128)(2,1)}, u32[]{:S(2)}, u32[]{:S(2)}) %collective-permute-start.1) | collective-permute-done | bytes 2359328 | tf_op jit(solution)/shard_map/ppermute | solution.py:42
  137.0 2.1 slice_dynamic-update-slice_fusion.3
  139.1 47.4 %collective-permute-done.2 = bf16[576,2048]{1,0:T(8,128)(2,1)} collective-permute-done((bf16[576,2048]{1,0:T(8,128)(2,1)}, bf16[576,2048]{1,0:T(8,128)(2,1)}, u32[]{:S(2)}, u32[]{:S(2)}) %collective-permute-start.2) | collective-permute-done | bytes 2359328 | tf_op jit(solution)/shard_map/ppermute | solution.py:42
  186.4 2.1 slice_dynamic-update-slice_fusion.2
  188.5 2.1 bitcast_dynamic-update-slice_fusion
  190.6 33.0 %all-to-all-done.1 = bf16[64,24,2048]{2,1,0:T(8,128)(2,1)} async-done(((bf16[64,24,2048]{2,1,0:T(8,128)(2,1)}), bf16[64,24,2048]{2,1,0:T(8,128)(2,1)}, u32[]{:S(2)}, u32[]{:S(2)}) %all-to-all-start.1) | async-done | bytes 6291488 | tf_op jit(solution)/shard_map/all_to_all | solution.py:31
  223.6 5.8 %all-to-all-start.2 = ((bf16[64,18,8,128]{3,2,1,0:T(8,128)(2,1)}), bf16[64,18,8,128]{3,2,1,0:T(8,128)(2,1)S(1)}, u32[]{:S(2)}, u32[]{:S(2)}) async-start(bf16[64,18,8,128]{3,2,1,0:T(8,128)(2,1)} %gather_fusion), calls=%async_computation.2 | async-start | bytes 4718592 | tf_op jit(solution)/shard_map/all_to_all | solution.py:31
  229.4 2.4 slice_dynamic-update-slice_fusion.4
  231.8 2.4 slice_dynamic-update-slice_fusion.1
  234.2 2.4 slice_dynamic-update-slice_fusion
  236.6 0.0 copy-start.2
  236.6 15.6 %fusion.21 = f32[1536,1536]{1,0:T(8,128)} fusion(bf16[1536,2048]{1,0:T(8,128)(2,1)} %bitcast.9, bf16[1536,2048]{1,0:T(8,128)(2,1)} %get-tuple-element.17), kind=kOutput, calls=%fused_computation.49 | convolution fusion | flops 9663676416 | bytes 22020096 | tf_op jit(solution)/shard_map/dot_general | solution.py:64
  252.3 0.0 copy-done.2
  252.3 11.0 %convolution_convert_fusion = bf16[1536,2048]{1,0:T(8,128)(2,1)} fusion(bf16[192,2048]{1,0:T(8,128)(2,1)S(1)} %get-tuple-element.18, bf16[192,2048]{1,0:T(8,128)(2,1)S(1)} %get-tuple-element.20, bf16[192,2048]{1,0:T(8,128)(2,1)S(1)} %get-tuple-element.22, bf16[192,2048]{1,0:T(8,128)(2,1)S(1)} %bitcast.41, f32[1536,1536]{1,0:T(8,128)} %fusion.21), kind=kOutput, calls=%fused_computation.1 | convolution fusion | flops 4854644736 | bytes 18874368 | tf_op jit(solution)/shard_map/dot_general | solution.py:70
  263.3 22.8 %all-to-all-done.2 = bf16[64,18,8,128]{3,2,1,0:T(8,128)(2,1)S(1)} async-done(((bf16[64,18,8,128]{3,2,1,0:T(8,128)(2,1)}), bf16[64,18,8,128]{3,2,1,0:T(8,128)(2,1)S(1)}, u32[]{:S(2)}, u32[]{:S(2)}) %all-to-all-start.2) | async-done | bytes 2359328 | tf_op jit(solution)/shard_map/all_to_all | solution.py:31
  286.0 0.0 copy-start.3
  286.0 6.3 %all-to-all-start.3 = ((bf16[64,24,2048]{2,1,0:T(8,128)(2,1)}), bf16[64,24,2048]{2,1,0:T(8,128)(2,1)}, u32[]{:S(2)}, u32[]{:S(2)}) async-start(bf16[64,24,2048]{2,1,0:T(8,128)(2,1)} %bitcast.37), calls=%async_computation.3 | async-start | bytes 12582912 | tf_op jit(solution)/shard_map/all_to_all | solution.py:31
  292.4 0.0 copy-done.3
  292.4 8.1 %select_reduce_fusion = f32[1536,128]{1,0:T(8,128)S(1)} fusion(f32[8,128]{1,0:T(8,128)S(1)} %divide_bitcast_fusion, s32[8,128]{1,0:T(8,128)S(1)} %add_bitcast_fusion), kind=kLoop, calls=%fused_computation.3 | loop fusion | flops 4521984 | bytes 794624 | tf_op jit(solution)/shard_map/reduce_sum | solution.py:81
  300.5 0.9 reduce-precision_convert_fusion
  301.4 1.2 slice.90
  302.6 0.9 slice_bitcast_fusion
  303.6 129.6 %all-to-all-done.3 = bf16[64,24,2048]{2,1,0:T(8,128)(2,1)} async-done(((bf16[64,24,2048]{2,1,0:T(8,128)(2,1)}), bf16[64,24,2048]{2,1,0:T(8,128)(2,1)}, u32[]{:S(2)}, u32[]{:S(2)}) %all-to-all-start.3) | async-done | bytes 6291488 | tf_op jit(solution)/shard_map/all_to_all | solution.py:31
  433.2 0.0 copy-start.1
  433.2 4.8 %fusion.13 = f32[256,2048]{1,0:T(8,128)S(1)} fusion(bf16[1536,2048]{1,0:T(8,128)(2,1)} %bitcast.13, bf16[128,1536]{0,1:T(8,128)(2,1)} %get-tuple-element.24, bf16[128,1536]{0,1:T(8,128)(2,1)S(1)} %get-tuple-element.23), kind=kOutput, calls=%fused_computation.27 | convolution fusion | flops 1612185600 | bytes 9175040 | tf_op jit(solution)/shard_map/dot_general | solution.py:85
  438.0 0.9 fusion.11
  438.9 0.0 copy-done.1
  (5 shorter events, 0.1 us)
Async XLA Ops:
  0.6 23.9 %copy-start = (bf16[128,2048]{1,0:T(8,128)(2,1)S(1)}, bf16[128,2048]{1,0:T(8,128)(2,1)}, u32[]{:S(2)}) copy-start(bf16[128,2048]{1,0:T(8,128)(2,1)} %param.6) | copy-start | bytes 1572868
  0.6 18.0 %copy-start.4 = (s32[128,8]{0,1:T(8,128)S(1)}, s32[128,8]{0,1:T(8,128)}, u32[]{:S(2)}) copy-start(s32[128,8]{0,1:T(8,128)} %param.7) | copy-start | bytes 12292
  0.7 18.0 %copy-start.5 = (s32[64]{0:T(128)S(1)}, s32[64]{0:T(128)}, u32[]{:S(2)}) copy-start(s32[64]{0:T(128)} %param.9) | copy-start | bytes 772
  4.2 69.8 %all-to-all-start = ((bf16[64,18,8,128]{3,2,1,0:T(8,128)(2,1)}), bf16[64,18,8,128]{3,2,1,0:T(8,128)(2,1)S(1)}, u32[]{:S(2)}, u32[]{:S(2)}) async-start(bf16[64,18,8,128]{3,2,1,0:T(8,128)(2,1)} %bitcast.7), calls=%async_computation | async-start | bytes 4718592 | tf_op jit(solution)/shard_map/all_to_all | solution.py:31
  17.3 54.0 %collective-permute-start = (bf16[576,2048]{1,0:T(8,128)(2,1)}, bf16[576,2048]{1,0:T(8,128)(2,1)}, u32[]{:S(2)}, u32[]{:S(2)}) collective-permute-start(bf16[576,2048]{1,0:T(8,128)(2,1)} %pad_maximum_fusion), channel_id=1, source_target_pairs={{0,64},{64,128},{128,192},{192,0},{1,65},{65,129},{129,193},{193,1... | collective-permute-start | bytes 7077896 | tf_op jit(solution)/shard_map/ppermute | solution.py:42
  74.0 149.6 %all-to-all-start.1 = ((bf16[64,24,2048]{2,1,0:T(8,128)(2,1)}), bf16[64,24,2048]{2,1,0:T(8,128)(2,1)}, u32[]{:S(2)}, u32[]{:S(2)}) async-start(bf16[64,24,2048]{2,1,0:T(8,128)(2,1)} %bitcast.34), calls=%async_computation.1 | async-start | bytes 12582912 | tf_op jit(solution)/shard_map/all_to_all | solution.py:31
  82.8 54.2 %collective-permute-start.1 = (bf16[576,2048]{1,0:T(8,128)(2,1)}, bf16[576,2048]{1,0:T(8,128)(2,1)}, u32[]{:S(2)}, u32[]{:S(2)}) collective-permute-start(bf16[576,2048]{1,0:T(8,128)(2,1)} %pad_maximum_fusion), channel_id=1, source_target_pairs={{0,128},{64,192},{128,0},{192,64},{1,129},{65,193},{129,1},{193,65... | collective-permute-start | bytes 7077896 | tf_op jit(solution)/shard_map/ppermute | solution.py:42
  84.4 102.1 %collective-permute-start.2 = (bf16[576,2048]{1,0:T(8,128)(2,1)}, bf16[576,2048]{1,0:T(8,128)(2,1)}, u32[]{:S(2)}, u32[]{:S(2)}) collective-permute-start(bf16[576,2048]{1,0:T(8,128)(2,1)} %pad_maximum_fusion), channel_id=1, source_target_pairs={{0,192},{64,0},{128,64},{192,128},{1,193},{65,1},{129,65},{193,129... | collective-permute-start | bytes 7077896 | tf_op jit(solution)/shard_map/ppermute | solution.py:42
  223.6 62.4 %all-to-all-start.2 = ((bf16[64,18,8,128]{3,2,1,0:T(8,128)(2,1)}), bf16[64,18,8,128]{3,2,1,0:T(8,128)(2,1)S(1)}, u32[]{:S(2)}, u32[]{:S(2)}) async-start(bf16[64,18,8,128]{3,2,1,0:T(8,128)(2,1)} %gather_fusion), calls=%async_computation.2 | async-start | bytes 4718592 | tf_op jit(solution)/shard_map/all_to_all | solution.py:31
  236.6 15.7 %copy-start.2 = (bf16[1,192,2048]{2,1,0:T(8,128)(2,1)S(1)}, bf16[1,192,2048]{2,1,0:T(8,128)(2,1)}, u32[]{:S(2)}) copy-start(bf16[1,192,2048]{2,1,0:T(8,128)(2,1)} %param.11) | copy-start | bytes 2359300
  286.0 6.3 %copy-start.3 = (f32[128,8]{0,1:T(8,128)S(1)}, f32[128,8]{0,1:T(8,128)}, u32[]{:S(2)}) copy-start(f32[128,8]{0,1:T(8,128)} %param.8) | copy-start | bytes 12292
  286.0 147.1 %all-to-all-start.3 = ((bf16[64,24,2048]{2,1,0:T(8,128)(2,1)}), bf16[64,24,2048]{2,1,0:T(8,128)(2,1)}, u32[]{:S(2)}, u32[]{:S(2)}) async-start(bf16[64,24,2048]{2,1,0:T(8,128)(2,1)} %bitcast.37), calls=%async_computation.3 | async-start | bytes 12582912 | tf_op jit(solution)/shard_map/all_to_all | solution.py:31
  433.2 5.7 %copy-start.1 = (bf16[128,2048]{1,0:T(8,128)(2,1)S(1)}, bf16[128,2048]{1,0:T(8,128)(2,1)}, u32[]{:S(2)}) copy-start(bf16[128,2048]{1,0:T(8,128)(2,1)} %param.6) | copy-start | bytes 1572868

commit v13 on v10

--- a/solution.py
+++ b/solution.py
@@ -34,8 +34,13 @@
     down_rows = w_down.reshape(-1, model_width)
     shard = jnp.concatenate([gate_rows, down_rows], axis=0)
     sub, lane = 8, 128
-    tiled = shard.reshape(shard.shape[0] // sub, sub, model_width // lane, lane).transpose(0, 2, 1, 3)
-    spread = exchange(tiled.reshape(experts, -1, sub, lane))
+
+    def tile_view(rows):
+        view = rows.reshape(rows.shape[0] // sub, sub, model_width // lane, lane).transpose(0, 2, 1, 3)
+        return view.reshape(experts, -1, sub, lane)
+
+    gate_tiles = tile_view(gate_rows)
+    spread = exchange(jnp.concatenate([gate_tiles, tile_view(down_rows)], axis=1))
 
     ring = lax.psum(1, "dp")
     parts = [shard] + [
@@ -72,10 +77,13 @@
     placed_rows, result = lax.optimization_barrier((placed_rows, result))
     returned = exchange(result)
 
-    placed_rows = placed_rows.reshape(tiled.shape).transpose(0, 2, 1, 3).reshape(-1, model_width)
-    gate_count = gate_rows.shape[0]
-    placed_gate_up = placed_rows[:gate_count].reshape(w_gate_up.shape)
-    placed_down = placed_rows[gate_count:].reshape(w_down.shape)
+    def untile(pieces, rows):
+        view = pieces.reshape(rows.shape[0] // sub, model_width // lane, sub, lane)
+        return view.transpose(0, 2, 1, 3).reshape(rows.shape)
+
+    gate_pieces = gate_tiles.shape[1]
+    placed_gate_up = untile(placed_rows[:, :gate_pieces], gate_rows).reshape(w_gate_up.shape)
+    placed_down = untile(placed_rows[:, gate_pieces:], down_rows).reshape(w_down.shape)
 
     gates = gate_probs / jnp.sum(gate_probs, axis=1, keepdims=True)
     part = jnp.sum(jnp.where(hits, gates.T[None, :, :], 0.0), axis=1).T

time: 437 us -> 438 us (level)
    unnamed x29 -> x33, local copies, waits for them, and re-layouts: 12.5 us -> 13 us
  transfers between devices with their start and end apart: 7 -> 7, of which waited for: 6 -> 6; matrix products, arithmetic and copies ran while one was open for 14% -> 15% of each run, Pallas kernels for 0% -> 0%
where the time goes in v13:
time: 438 us
  waiting for transfers between devices  325 us (74%)
  starting transfers between devices  36.4 us (8%)
  matrix products  36 us (8%)
  local copies, waits for them, and re-layouts  20.2 us (5%)
  other arithmetic  19.4 us (4%)
    all_to_all x4, waiting for transfers between devices, exchange(): lax.all_to_all(block, 'expert', split_axis=0, concat_axis=0, tiled=True)  227 us
    ppermute x3, waiting for transfers between devices, per_device(): lax.ppermute(shard, 'dp', [(j, (j + shift) % ring) for j in range(ring)])  98.2 us
    all_to_all x4, starting transfers between devices, exchange(): lax.all_to_all(block, 'expert', split_axis=0, concat_axis=0, tiled=True)  31.5 us
    dot_general x1, matrix products, per_device(): lax.dot_general(row_block, gate_up_full, (((1,), (1,)), ((), ())), prefer...  15.7 us
    unnamed x33, local copies, waits for them, and re-layouts  13 us
    dot_general x1, matrix products, per_device(): jnp.dot(hidden, down_full, preferred_element_type=jnp.float32)  11 us
  transfers between devices with their start and end apart: 7, of which 6 were waited for; matrix products, arithmetic and copies ran while one was open for 15% of the time, Pallas kernels for 0%

profile of v13, /device:TPU:1, one launch (start us, length us, event | category | flops | bytes accessed | tf_op | source)
XLA Modules:
  0.0 437.6 jit_solution(2269715106716789439)
XLA Ops:
  0.6 0.0 copy-start
  0.6 0.0 copy-start.11
  0.7 0.0 copy-start.12
  0.7 3.3 pad_maximum_fusion
  4.0 13.2 %all-to-all-start = ((bf16[64,18,8,128]{3,2,1,0:T(8,128)(2,1)}), bf16[64,18,8,128]{3,2,1,0:T(8,128)(2,1)S(1)}, u32[]{:S(2)}, u32[]{:S(2)}) async-start(bf16[64,18,8,128]{3,2,1,0:T(8,128)(2,1)} %pad_maximum_fusion), calls=%async_computation | async-start | bytes 4718592 | tf_op jit(solution)/shard_map/all_to_all | solution.py:31
  17.1 0.0 copy-done.11
  17.2 0.0 copy-done.12
  17.2 0.1 select_reduce_fusion.2
  17.3 0.1 fusion.17
  17.5 0.1 select_reduce_fusion.1
  17.5 5.6 %fusion = pred[1536,128]{1,0:T(8,128)(4,1)S(1)} fusion(s32[8,128]{1,0:T(8,128)S(1)} %add_bitcast_fusion), kind=kLoop, calls=%fused_computation.5 | loop fusion | flops 2949120 | bytes 200704 | tf_op jit(solution)/shard_map/reduce_or | solution.py:28
  23.1 0.0 copy-done
  23.1 4.4 %convolution_convert_fusion.1 = bf16[1536,2048]{1,0:T(8,128)(2,1)} fusion(pred[1536,128]{1,0:T(8,128)(4,1)S(1)} %fusion, bf16[128,2048]{1,0:T(8,128)(2,1)S(1)} %copy-done), kind=kOutput, calls=%fused_computation.2 | convolution fusion | flops 808452096 | bytes 7012352 | tf_op jit(solution)/shard_map/dot_general | solution.py:58
  27.5 46.3 %all-to-all-done = bf16[64,18,8,128]{3,2,1,0:T(8,128)(2,1)S(1)} async-done(((bf16[64,18,8,128]{3,2,1,0:T(8,128)(2,1)}), bf16[64,18,8,128]{3,2,1,0:T(8,128)(2,1)S(1)}, u32[]{:S(2)}, u32[]{:S(2)}) %all-to-all-start) | async-done | bytes 2359328 | tf_op jit(solution)/shard_map/all_to_all | solution.py:31
  73.8 0.0 copy-start.3
  73.8 1.4 copy-done.3
  75.2 0.0 copy-start.2
  75.2 0.0 copy-start.4
  75.2 6.3 %all-to-all-start.1 = ((bf16[64,24,2048]{2,1,0:T(8,128)(2,1)}), bf16[64,24,2048]{2,1,0:T(8,128)(2,1)}, u32[]{:S(2)}, u32[]{:S(2)}) async-start(bf16[64,24,2048]{2,1,0:T(8,128)(2,1)} %bitcast.43), calls=%async_computation.1 | async-start | bytes 12582912 | tf_op jit(solution)/shard_map/all_to_all | solution.py:31
  81.5 0.0 copy-done.2
  81.5 0.0 copy-done.4
  81.5 0.3 pad_maximum_fusion.1
  81.8 1.3 collective-permute-start
  83.1 2.5 collective-permute-start.1
  85.6 1.2 collective-permute-start.2
  86.7 0.1 select_reduce_fusion.3
  86.8 0.9 bitcast_dynamic-update-slice_fusion.1
  87.7 47.7 %collective-permute-done = bf16[576,2048]{1,0:T(8,128)(2,1)S(1)} collective-permute-done((bf16[576,2048]{1,0:T(8,128)(2,1)S(1)}, bf16[576,2048]{1,0:T(8,128)(2,1)S(1)}, u32[]{:S(2)}, u32[]{:S(2)}) %collective-permute-start) | collective-permute-done | bytes 2359328 | tf_op jit(solution)/shard_map/ppermute | solution.py:47
  135.5 0.0 copy-start.9
  135.5 1.1 slice_dynamic-update-slice_fusion.5
  136.6 50.5 %collective-permute-done.1 = bf16[576,2048]{1,0:T(8,128)(2,1)S(1)} collective-permute-done((bf16[576,2048]{1,0:T(8,128)(2,1)S(1)}, bf16[576,2048]{1,0:T(8,128)(2,1)S(1)}, u32[]{:S(2)}, u32[]{:S(2)}) %collective-permute-start.1) | collective-permute-done | bytes 2359328 | tf_op jit(solution)/shard_map/ppermute | solution.py:47
  187.0 0.0 copy-start.8
  187.0 1.1 slice_dynamic-update-slice_fusion.4
  188.2 0.0 collective-permute-done.2
  188.2 0.0 copy-start.6
  188.2 1.5 copy-done.6
  189.7 1.0 slice_dynamic-update-slice_fusion.3
  190.7 0.0 copy-done.9
  190.7 0.0 copy-done.8
  190.7 0.9 bitcast_dynamic-update-slice_fusion
  191.7 3.9 gather_fusion
  195.6 26.8 %all-to-all-done.1 = bf16[64,24,2048]{2,1,0:T(8,128)(2,1)} async-done(((bf16[64,24,2048]{2,1,0:T(8,128)(2,1)}), bf16[64,24,2048]{2,1,0:T(8,128)(2,1)}, u32[]{:S(2)}, u32[]{:S(2)}) %all-to-all-start.1) | async-done | bytes 6291488 | tf_op jit(solution)/shard_map/all_to_all | solution.py:31
  222.4 5.8 %all-to-all-start.2 = ((bf16[64,18,8,128]{3,2,1,0:T(8,128)(2,1)}), bf16[64,18,8,128]{3,2,1,0:T(8,128)(2,1)S(1)}, u32[]{:S(2)}, u32[]{:S(2)}) async-start(bf16[64,18,8,128]{3,2,1,0:T(8,128)(2,1)} %gather_fusion), calls=%async_computation.2 | async-start | bytes 4718592 | tf_op jit(solution)/shard_map/all_to_all | solution.py:31
  228.2 0.0 copy-start.7
  228.2 2.6 slice_dynamic-update-slice_fusion.2
  230.7 2.4 slice_dynamic-update-slice_fusion.1
  233.1 0.0 copy-done.7
  233.2 1.0 slice_dynamic-update-slice_fusion
  234.2 0.0 copy-start.5
  234.2 15.7 %fusion.21 = f32[1536,1536]{1,0:T(8,128)} fusion(bf16[1536,2048]{1,0:T(8,128)(2,1)} %bitcast.10, bf16[1536,2048]{1,0:T(8,128)(2,1)} %get-tuple-element.15), kind=kOutput, calls=%fused_computation.49 | convolution fusion | flops 9663676416 | bytes 22020096 | tf_op jit(solution)/shard_map/dot_general | solution.py:69
  249.9 0.0 copy-done.5
  249.9 11.0 %convolution_convert_fusion = bf16[1536,2048]{1,0:T(8,128)(2,1)} fusion(bf16[192,2048]{1,0:T(8,128)(2,1)S(1)} %get-tuple-element.16, bf16[192,2048]{1,0:T(8,128)(2,1)S(1)} %get-tuple-element.18, bf16[192,2048]{1,0:T(8,128)(2,1)S(1)} %get-tuple-element.20, bf16[192,2048]{1,0:T(8,128)(2,1)S(1)} %bitcast.49, f32[1536,1536]{1,0:T(8,128)} %fusion.21), kind=kOutput, calls=%fused_computation.1 | convolution fusion | flops 4854644736 | bytes 18874368 | tf_op jit(solution)/shard_map/dot_general | solution.py:75
  260.9 23.9 %all-to-all-done.2 = bf16[64,18,8,128]{3,2,1,0:T(8,128)(2,1)S(1)} async-done(((bf16[64,18,8,128]{3,2,1,0:T(8,128)(2,1)}), bf16[64,18,8,128]{3,2,1,0:T(8,128)(2,1)S(1)}, u32[]{:S(2)}, u32[]{:S(2)}) %all-to-all-start.2) | async-done | bytes 2359328 | tf_op jit(solution)/shard_map/all_to_all | solution.py:31
  284.8 0.0 copy-start.10
  284.8 6.3 %all-to-all-start.3 = ((bf16[64,24,2048]{2,1,0:T(8,128)(2,1)}), bf16[64,24,2048]{2,1,0:T(8,128)(2,1)}, u32[]{:S(2)}, u32[]{:S(2)}) async-start(bf16[64,24,2048]{2,1,0:T(8,128)(2,1)} %bitcast.46), calls=%async_computation.3 | async-start | bytes 12582912 | tf_op jit(solution)/shard_map/all_to_all | solution.py:31
  291.1 0.0 copy-done.10
  291.1 8.1 %select_reduce_fusion = f32[1536,128]{1,0:T(8,128)S(1)} fusion(f32[8,128]{1,0:T(8,128)S(1)} %divide_bitcast_fusion, s32[8,128]{1,0:T(8,128)S(1)} %add_bitcast_fusion), kind=kLoop, calls=%fused_computation.3 | loop fusion | flops 4521984 | bytes 794624 | tf_op jit(solution)/shard_map/reduce_sum | solution.py:89
  299.3 0.9 reduce-precision_convert_fusion
  300.1 1.3 slice.74
  301.4 0.9 slice.75
  302.3 129.6 %all-to-all-done.3 = bf16[64,24,2048]{2,1,0:T(8,128)(2,1)} async-done(((bf16[64,24,2048]{2,1,0:T(8,128)(2,1)}), bf16[64,24,2048]{2,1,0:T(8,128)(2,1)}, u32[]{:S(2)}, u32[]{:S(2)}) %all-to-all-start.3) | async-done | bytes 6291488 | tf_op jit(solution)/shard_map/all_to_all | solution.py:31
  431.9 4.8 %fusion.13 = f32[256,2048]{1,0:T(8,128)S(1)} fusion(bf16[1536,2048]{1,0:T(8,128)(2,1)} %bitcast.16, bf16[128,1536]{0,1:T(8,128)(2,1)} %get-tuple-element.22, bf16[128,1536]{0,1:T(8,128)(2,1)S(1)} %get-tuple-element.21), kind=kOutput, calls=%fused_computation.29 | convolution fusion | flops 1612185600 | bytes 9175040 | tf_op jit(solution)/shard_map/dot_general | solution.py:93
  436.7 0.9 fusion.11
  437.6 0.0 copy-done.1
  (6 shorter events, 0.1 us)
Async XLA Ops:
  0.6 22.5 %copy-start = (bf16[128,2048]{1,0:T(8,128)(2,1)S(1)}, bf16[128,2048]{1,0:T(8,128)(2,1)}, u32[]{:S(2)}) copy-start(bf16[128,2048]{1,0:T(8,128)(2,1)} %param.6) | copy-start | bytes 1572868
  0.6 16.5 %copy-start.11 = (s32[128,8]{0,1:T(8,128)S(1)}, s32[128,8]{0,1:T(8,128)}, u32[]{:S(2)}) copy-start(s32[128,8]{0,1:T(8,128)} %param.7) | copy-start | bytes 12292
  0.7 16.5 %copy-start.12 = (s32[64]{0:T(128)S(1)}, s32[64]{0:T(128)}, u32[]{:S(2)}) copy-start(s32[64]{0:T(128)} %param.9) | copy-start | bytes 772
  4.0 69.8 %all-to-all-start = ((bf16[64,18,8,128]{3,2,1,0:T(8,128)(2,1)}), bf16[64,18,8,128]{3,2,1,0:T(8,128)(2,1)S(1)}, u32[]{:S(2)}, u32[]{:S(2)}) async-start(bf16[64,18,8,128]{3,2,1,0:T(8,128)(2,1)} %pad_maximum_fusion), calls=%async_computation | async-start | bytes 4718592 | tf_op jit(solution)/shard_map/all_to_all | solution.py:31
  73.8 1.4 copy-start.3
  75.2 6.3 %copy-start.2 = (bf16[1,2,192,2048]{3,2,1,0:T(8,128)(2,1)S(1)}, bf16[1,2,192,2048]{3,2,1,0:T(8,128)(2,1)}, u32[]{:S(2)}) copy-start(bf16[1,2,192,2048]{3,2,1,0:T(8,128)(2,1)} %param.10) | copy-start | bytes 4718596
  75.2 6.3 %copy-start.4 = (bf16[1,192,2048]{2,1,0:T(8,128)(2,1)S(1)}, bf16[1,192,2048]{2,1,0:T(8,128)(2,1)}, u32[]{:S(2)}) copy-start(bf16[1,192,2048]{2,1,0:T(8,128)(2,1)} %param.11) | copy-start | bytes 2359300
  75.2 147.1 %all-to-all-start.1 = ((bf16[64,24,2048]{2,1,0:T(8,128)(2,1)}), bf16[64,24,2048]{2,1,0:T(8,128)(2,1)}, u32[]{:S(2)}, u32[]{:S(2)}) async-start(bf16[64,24,2048]{2,1,0:T(8,128)(2,1)} %bitcast.43), calls=%async_computation.1 | async-start | bytes 12582912 | tf_op jit(solution)/shard_map/all_to_all | solution.py:31
  81.8 53.7 %collective-permute-start = (bf16[576,2048]{1,0:T(8,128)(2,1)S(1)}, bf16[576,2048]{1,0:T(8,128)(2,1)S(1)}, u32[]{:S(2)}, u32[]{:S(2)}) collective-permute-start(bf16[576,2048]{1,0:T(8,128)(2,1)S(1)} %pad_maximum_fusion.1), channel_id=1, source_target_pairs={{0,64},{64,128},{128,192},{192,0},{1,65},{65,129},{129,193},{193,1... | collective-permute-start | bytes 7077896 | tf_op jit(solution)/shard_map/ppermute | solution.py:47
  83.1 103.9 %collective-permute-start.1 = (bf16[576,2048]{1,0:T(8,128)(2,1)S(1)}, bf16[576,2048]{1,0:T(8,128)(2,1)S(1)}, u32[]{:S(2)}, u32[]{:S(2)}) collective-permute-start(bf16[576,2048]{1,0:T(8,128)(2,1)S(1)} %pad_maximum_fusion.1), channel_id=1, source_target_pairs={{0,128},{64,192},{128,0},{192,64},{1,129},{65,193},{129,1},{193,65... | collective-permute-start | bytes 7077896 | tf_op jit(solution)/shard_map/ppermute | solution.py:47
  85.6 102.6 %collective-permute-start.2 = (bf16[576,2048]{1,0:T(8,128)(2,1)S(1)}, bf16[576,2048]{1,0:T(8,128)(2,1)S(1)}, u32[]{:S(2)}, u32[]{:S(2)}) collective-permute-start(bf16[576,2048]{1,0:T(8,128)(2,1)S(1)} %pad_maximum_fusion.1), channel_id=1, source_target_pairs={{0,192},{64,0},{128,64},{192,128},{1,193},{65,1},{129,65},{193,129... | collective-permute-start | bytes 7077896 | tf_op jit(solution)/shard_map/ppermute | solution.py:47
  135.5 55.2 %copy-start.9 = (bf16[576,2048]{1,0:T(8,128)(2,1)}, bf16[576,2048]{1,0:T(8,128)(2,1)S(1)}, u32[]{:S(2)}) copy-start(bf16[576,2048]{1,0:T(8,128)(2,1)S(1)} %collective-permute-done) | copy-start | bytes 7077892
  187.0 3.7 copy-start.8
  188.2 1.5 copy-start.6
  222.4 62.4 %all-to-all-start.2 = ((bf16[64,18,8,128]{3,2,1,0:T(8,128)(2,1)}), bf16[64,18,8,128]{3,2,1,0:T(8,128)(2,1)S(1)}, u32[]{:S(2)}, u32[]{:S(2)}) async-start(bf16[64,18,8,128]{3,2,1,0:T(8,128)(2,1)} %gather_fusion), calls=%async_computation.2 | async-start | bytes 4718592 | tf_op jit(solution)/shard_map/all_to_all | solution.py:31
  228.2 5.0 %copy-start.7 = (bf16[576,2048]{1,0:T(8,128)(2,1)S(1)}, bf16[576,2048]{1,0:T(8,128)(2,1)}, u32[]{:S(2)}) copy-start(bf16[576,2048]{1,0:T(8,128)(2,1)} %copy-done.6) | copy-start | bytes 7077892
  234.2 15.7 %copy-start.5 = (bf16[1,192,2048]{2,1,0:T(8,128)(2,1)S(1)}, bf16[1,192,2048]{2,1,0:T(8,128)(2,1)}, u32[]{:S(2)}) copy-start(bf16[1,192,2048]{2,1,0:T(8,128)(2,1)} %param.11) | copy-start | bytes 2359300
  284.8 6.3 %copy-start.10 = (f32[128,8]{0,1:T(8,128)S(1)}, f32[128,8]{0,1:T(8,128)}, u32[]{:S(2)}) copy-start(f32[128,8]{0,1:T(8,128)} %param.8) | copy-start | bytes 12292
  284.8 147.1 %all-to-all-start.3 = ((bf16[64,24,2048]{2,1,0:T(8,128)(2,1)}), bf16[64,24,2048]{2,1,0:T(8,128)(2,1)}, u32[]{:S(2)}, u32[]{:S(2)}) async-start(bf16[64,24,2048]{2,1,0:T(8,128)(2,1)} %bitcast.46), calls=%async_computation.3 | async-start | bytes 12582912 | tf_op jit(solution)/shard_map/all_to_all | solution.py:31
  431.9 5.7 %copy-start.1 = (bf16[128,2048]{1,0:T(8,128)(2,1)S(1)}, bf16[128,2048]{1,0:T(8,128)(2,1)}, u32[]{:S(2)}) copy-start(bf16[128,2048]{1,0:T(8,128)(2,1)} %param.6) | copy-start | bytes 1572868
